TPU v7x, 32 devices: a whole 2x2x4 slice. The times are simulated.
32 devices in a mesh: rows: 16 (over z, y, x), vecs: 2 (over core).
Axes of the slice: x: 2, y: 2, z: 4, core: 2. Of those that a mesh axis runs over, the one named last changes fastest.
Arguments:
- vectors: bfloat16 [8192, 256], P('rows', 'vecs'), may hold values from -6 to 6
- blocks: bfloat16 [64, 32, 128, 128], P('rows'), may hold values from -0.09375 to 0.09375
- scales: float32 [64, 32], P('rows'), may hold values from 0.5 to 1.5
- columns: int32 [64, 32], P('rows'), may hold values from 0 to 63, as said below
- owners: int32 [64], P('rows'), may hold values from 0 to 63, as said below
- center: float32 [1], replicated, may hold values from -0.3 to 0.3
- half_width: float32 [1], replicated, may hold values from 1.5 to 2.5
Outputs:
- filtered: bfloat16 [8192, 256], P('rows', 'vecs')
Inputs may be any that keep to these rules, and one draw needn't show every extreme that they name: `columns`: the block rows of one aligned group of 4 block rows read at most one atom of each aligned group of 4 atoms. owners is a permutation of the atoms; the 4 entries of one aligned group of 4 entries lie in distinct aligned groups of 4 atoms.
All inputs are finite; a program needn't handle non-finite values.
Results may differ from a plain program's by a relative error of at most 0.0054.
Values may be sent and summed in bfloat16 or wider, within the bound.
No kernel may reach another device: no remote copies, remote signals or barrier semaphores. Data moves between devices by JAX's collectives and lax.ppermute only.
A program may use at most 64 MiB of HBM per device.

v0:
```python
import jax
import jax.numpy as jnp
from jax import lax
from jax.sharding import PartitionSpec as P

STEPS = 4


def on_device(vectors, blocks, scales, columns, owners, center, half_width):
    nrows = lax.axis_size("rows")
    local_rows = blocks.shape[0]
    per_row = blocks.shape[1]
    orbitals = blocks.shape[2]
    group_width = vectors.shape[1]
    myself = lax.axis_index("rows")
    all_columns, all_owners = (
        lax.all_gather(columns, "rows", axis=0, tiled=True),
        lax.all_gather(owners, "rows", axis=0, tiled=True),
    )
    table = all_columns.reshape(nrows, local_rows * per_row)
    wanted = jnp.max(jnp.where(table // local_rows == myself, table % local_rows, 0), axis=1)
    owner_table = all_owners.reshape(nrows, local_rows)
    relay_want = jnp.max(
        jnp.where(owner_table // local_rows == myself, owner_table % local_rows, 0), axis=1
    )
    source_slot = (columns // local_rows).reshape(local_rows * per_row)

    def product(received):
        operand = jnp.take(received, source_slot, axis=0).reshape(
            local_rows, per_row, orbitals, received.shape[2]
        )
        partial_value = jnp.einsum(
            "rkij,rkjv->rkiv", blocks, operand, preferred_element_type=jnp.float32
        )
        return jnp.sum(partial_value * scales[:, :, None, None], axis=1)

    def apply_blocks(panels):
        outgoing = jnp.take(panels, wanted, axis=0)
        received = lax.all_to_all(outgoing, "rows", split_axis=0, concat_axis=0, tiled=True)
        return product(received)

    shift = center[0]
    width = half_width[0]
    previous = vectors.reshape(local_rows, orbitals, group_width)
    current = ((apply_blocks(previous) - shift * previous.astype(jnp.float32)) / width).astype(
        jnp.bfloat16
    )
    for step in range(STEPS - 1):
        image = apply_blocks(current)
        upcoming = (
            2.0 * (image - shift * current.astype(jnp.float32)) / width
            - previous.astype(jnp.float32)
        ).astype(jnp.bfloat16)
        previous, current = (current, upcoming)
    sending = jnp.take(current, relay_want, axis=0)
    arrived = lax.all_to_all(sending, "rows", split_axis=0, concat_axis=0, tiled=True)
    placed = jnp.take(arrived, owners // local_rows, axis=0)
    return placed.reshape(local_rows * orbitals, group_width)


def solution(mesh):
    in_specs = (
        P("rows", "vecs"),
        P("rows", None, None, None),
        P("rows", None),
        P("rows", None),
        P("rows"),
        P(),
        P(),
    )
    out_specs = P("rows", "vecs")
    return jax.shard_map(
        on_device, mesh=mesh, in_specs=in_specs, out_specs=out_specs, check_vma=False
    )
```

profile of v0, /device:TPU:0, one launch (start us, length us, event | category | flops | bytes accessed | tf_op | source)
XLA Modules:
  0.0 168.9 jit_solution(865698939790303324)
XLA Ops:
  0.0 42.8 %all-gather = s32[16,4,32]{2,1,0:T(4,128)S(1)} all-gather(s32[1,4,32]{2,1,0:T(4,128)} %bitcast.51), channel_id=1, replica_groups=mesh['rows'=16,'vecs'=2] {'rows'}, dimensions={0}, use_global_device_ids=true | all-gather | bytes 8704 | tf_op jit(solution)/shard_map/all_gather | solution.py:17
  43.2 1.6 gather_fusion.1
  44.7 0.9 broadcast_select_fusion.8
  45.6 3.6 %all-to-all-start = ((bf16[16,128,128]{2,1,0:T(8,128)(2,1)}), bf16[16,128,128]{2,1,0:T(8,128)(2,1)S(1)}, u32[]{:S(2)}, u32[]{:S(2)}) async-start(bf16[16,128,128]{2,1,0:T(8,128)(2,1)} %broadcast_select_fusion.8), calls=%async_computation | async-start | bytes 1048576 | tf_op jit(solution)/shard_map/all_to_all | solution.py:39
  49.2 1.0 copy.17
  50.2 0.7 add_select_fusion.4
  52.4 7.6 %all-to-all-done = bf16[16,128,128]{2,1,0:T(8,128)(2,1)S(1)} async-done(((bf16[16,128,128]{2,1,0:T(8,128)(2,1)}), bf16[16,128,128]{2,1,0:T(8,128)(2,1)S(1)}, u32[]{:S(2)}, u32[]{:S(2)}) %all-to-all-start) | async-done | bytes 524320 | tf_op jit(solution)/shard_map/all_to_all | solution.py:39
  59.9 3.0 %gather_fusion.2 = bf16[128,128,128]{2,1,0:T(8,128)(2,1)} fusion(bf16[16,128,128]{2,1,0:T(8,128)(2,1)S(1)} %all-to-all-done, s32[1024]{0:T(1024)S(1)} %pad_clamp_fusion.2), kind=kCustom, calls=%fused_computation.1.clone | custom fusion | bytes 8389120 | tf_op jit(solution)/shard_map/jit(_take)/gather | solution.py:29
  63.0 2.8 %broadcast_select_fusion.3 = bf16[128,128,128]{2,1,0:T(8,128)(2,1)S(1)} fusion(bf16[128,128,128]{2,1,0:T(8,128)(2,1)} %gather_fusion.2, pred[128]{0:T(512)(128)(4,1)S(1)} %compare_and_fusion.1), kind=kLoop, calls=%fused_computation.17 | loop fusion | flops 2097152 | bytes 8388736 | tf_op jit(solution)/shard_map/jit(_take)/select_n | solution.py:29
  66.4 3.1 %multiply_reduce_fusion.3 = f32[4,128,128]{2,1,0:T(8,128)S(1)} fusion(f32[4,32]{1,0:T(4,128)S(1)} %copy-done.4, bf16[4,32,128,128]{3,2,1,0:T(8,128)(2,1)S(1)} %bitcast.45, bf16[4,32,128,128]{3,2,1,0:T(8,128)(2,1)S(1)} %copy-done), kind=kOutput, calls=%fused_computation.13 | convolution fusion | flops 540999680 | bytes 8651264 | tf_op jit(solution)/shard_map/rkij,rkjv->rkiv/dot_general | solution.py:32
  70.4 14.6 %all_to_all.25 = bf16[16,128,128]{1,2,0:T(8,128)(2,1)S(1)} all-to-all(bf16[16,128,128]{1,2,0:T(8,128)(2,1)S(1)} %broadcast_select_fusion.5), channel_id=1, replica_groups=mesh['rows'=16,'vecs'=2] {'rows'}, dimensions={0} | all-to-all | bytes 1048576 | tf_op jit(solution)/shard_map/all_to_all | solution.py:39
  85.0 3.0 %gather_fusion.4 = bf16[128,128,128]{1,2,0:T(8,128)(2,1)} fusion(bf16[16,128,128]{1,2,0:T(8,128)(2,1)S(1)} %all_to_all.25, s32[1024]{0:T(1024)S(1)} %pad_clamp_fusion.2), kind=kCustom, calls=%fused_computation.6.clone | custom fusion | bytes 8389120 | tf_op jit(solution)/shard_map/jit(_take)/gather | solution.py:29
  88.0 2.8 %broadcast_select_fusion = bf16[128,128,128]{1,2,0:T(8,128)(2,1)S(1)} fusion(bf16[128,128,128]{1,2,0:T(8,128)(2,1)} %gather_fusion.4, pred[128]{0:T(512)(128)(4,1)S(1)} %compare_and_fusion.1), kind=kLoop, calls=%fused_computation.14 | loop fusion | flops 2097152 | bytes 8388736 | tf_op jit(solution)/shard_map/jit(_take)/select_n | solution.py:29
  90.8 0.7 copy-done.1
  91.4 3.0 %multiply_reduce_fusion.2 = f32[4,128,128]{2,1,0:T(8,128)S(1)} fusion(f32[4,32]{1,0:T(4,128)S(1)} %copy-done.4, bf16[4,32,128,128]{2,3,1,0:T(8,128)(2,1)S(1)} %bitcast.46, bf16[4,32,128,128]{3,2,1,0:T(8,128)(2,1)S(1)} %copy-done.1), kind=kOutput, calls=%fused_computation.12 | convolution fusion | flops 540999680 | bytes 8651264 | tf_op jit(solution)/shard_map/rkij,rkjv->rkiv/dot_general | solution.py:32
  95.3 14.6 %all_to_all.26 = bf16[16,128,128]{1,2,0:T(8,128)(2,1)S(1)} all-to-all(bf16[16,128,128]{1,2,0:T(8,128)(2,1)S(1)} %broadcast_select_fusion.6), channel_id=1, replica_groups=mesh['rows'=16,'vecs'=2] {'rows'}, dimensions={0} | all-to-all | bytes 1048576 | tf_op jit(solution)/shard_map/all_to_all | solution.py:39
  109.9 3.0 %gather_fusion.6 = bf16[128,128,128]{1,2,0:T(8,128)(2,1)} fusion(bf16[16,128,128]{1,2,0:T(8,128)(2,1)S(1)} %all_to_all.26, s32[1024]{0:T(1024)S(1)} %pad_clamp_fusion.2), kind=kCustom, calls=%fused_computation.7.clone | custom fusion | bytes 8389120 | tf_op jit(solution)/shard_map/jit(_take)/gather | solution.py:29
  112.9 2.8 %broadcast_select_fusion.1 = bf16[128,128,128]{1,2,0:T(8,128)(2,1)S(1)} fusion(bf16[128,128,128]{1,2,0:T(8,128)(2,1)} %gather_fusion.6, pred[128]{0:T(512)(128)(4,1)S(1)} %compare_and_fusion.1), kind=kLoop, calls=%fused_computation.15 | loop fusion | flops 2097152 | bytes 8388736 | tf_op jit(solution)/shard_map/jit(_take)/select_n | solution.py:29
  115.7 0.7 copy-done.2
  116.4 3.0 %multiply_reduce_fusion.1 = f32[4,128,128]{2,1,0:T(8,128)S(1)} fusion(f32[4,32]{1,0:T(4,128)S(1)} %copy-done.4, bf16[4,32,128,128]{2,3,1,0:T(8,128)(2,1)S(1)} %bitcast.47, bf16[4,32,128,128]{3,2,1,0:T(8,128)(2,1)S(1)} %copy-done.2), kind=kOutput, calls=%fused_computation.11 | convolution fusion | flops 540999680 | bytes 8651264 | tf_op jit(solution)/shard_map/rkij,rkjv->rkiv/dot_general | solution.py:32
  120.1 0.9 broadcast_select_fusion.7
  121.0 4.0 %all-to-all-start.3 = ((bf16[16,128,128]{1,2,0:T(8,128)(2,1)}), bf16[16,128,128]{1,2,0:T(8,128)(2,1)S(1)}, u32[]{:S(2)}, u32[]{:S(2)}) async-start(bf16[16,128,128]{1,2,0:T(8,128)(2,1)} %broadcast_select_fusion.7), calls=%async_computation.3 | async-start | bytes 1048576 | tf_op jit(solution)/shard_map/all_to_all | solution.py:39
  125.1 0.7 dynamic-slice
  126.7 15.0 %all-reduce = s32[64]{0:T(128)S(1)} all-reduce(s32[64]{0:T(128)S(1)} %dynamic-update-slice), channel_id=1, replica_groups=mesh['rows'=16,'vecs'=2] {'rows'}, use_global_device_ids=true, to_apply=%add | all-reduce | flops 64 | bytes 512
  142.0 3.0 %gather_fusion.8 = bf16[128,128,128]{1,2,0:T(8,128)(2,1)} fusion(bf16[16,128,128]{1,2,0:T(8,128)(2,1)S(1)} %all-to-all-done.3, s32[1024]{0:T(1024)S(1)} %pad_clamp_fusion.2), kind=kCustom, calls=%fused_computation.8.clone | custom fusion | bytes 8389120 | tf_op jit(solution)/shard_map/jit(_take)/gather | solution.py:29
  145.0 2.8 %broadcast_select_fusion.2 = bf16[128,128,128]{1,2,0:T(8,128)(2,1)S(1)} fusion(bf16[128,128,128]{1,2,0:T(8,128)(2,1)} %gather_fusion.8, pred[128]{0:T(512)(128)(4,1)S(1)} %compare_and_fusion.1), kind=kLoop, calls=%fused_computation.16 | loop fusion | flops 2097152 | bytes 8388736 | tf_op jit(solution)/shard_map/jit(_take)/select_n | solution.py:29
  147.8 0.7 copy-done.3
  148.4 3.0 %multiply_reduce_fusion = f32[4,128,128]{2,1,0:T(8,128)S(1)} fusion(f32[4,32]{1,0:T(4,128)S(1)} %copy-done.4, bf16[4,32,128,128]{2,3,1,0:T(8,128)(2,1)S(1)} %bitcast.44, bf16[4,32,128,128]{3,2,1,0:T(8,128)(2,1)S(1)} %copy-done.3), kind=kOutput, calls=%fused_computation.10 | convolution fusion | flops 540999680 | bytes 8651264 | tf_op jit(solution)/shard_map/rkij,rkjv->rkiv/dot_general | solution.py:32
  152.2 0.9 broadcast_select_fusion.4
  153.1 3.6 %all-to-all-start.4 = ((bf16[16,128,128]{1,2,0:T(8,128)(2,1)}), bf16[16,128,128]{1,2,0:T(8,128)(2,1)S(1)}, u32[]{:S(2)}, u32[]{:S(2)}) async-start(bf16[16,128,128]{1,2,0:T(8,128)(2,1)} %broadcast_select_fusion.4), calls=%async_computation.4 | async-start | bytes 1048576 | tf_op jit(solution)/shard_map/all_to_all | solution.py:56
  156.8 10.6 %all-to-all-done.4 = bf16[16,128,128]{1,2,0:T(8,128)(2,1)S(1)} async-done(((bf16[16,128,128]{1,2,0:T(8,128)(2,1)}), bf16[16,128,128]{1,2,0:T(8,128)(2,1)S(1)}, u32[]{:S(2)}, u32[]{:S(2)}) %all-to-all-start.4) | async-done | bytes 524320 | tf_op jit(solution)/shard_map/all_to_all | solution.py:56
  168.1 0.8 bitcast_select_fusion
  (44 shorter events, 5.5 us)
Async XLA Ops:
  45.6 14.3 %all-to-all-start = ((bf16[16,128,128]{2,1,0:T(8,128)(2,1)}), bf16[16,128,128]{2,1,0:T(8,128)(2,1)S(1)}, u32[]{:S(2)}, u32[]{:S(2)}) async-start(bf16[16,128,128]{2,1,0:T(8,128)(2,1)} %broadcast_select_fusion.8), calls=%async_computation | async-start | bytes 1048576 | tf_op jit(solution)/shard_map/all_to_all | solution.py:39
  62.9 3.4 %copy-start = (bf16[4,32,128,128]{3,2,1,0:T(8,128)(2,1)S(1)}, bf16[4,32,128,128]{3,2,1,0:T(8,128)(2,1)}, u32[]{:S(2)}) copy-start(bf16[4,32,128,128]{3,2,1,0:T(8,128)(2,1)} %param.12) | copy-start | bytes 12582916
  63.0 3.4 %copy-start.4 = (f32[4,32]{1,0:T(4,128)S(1)}, f32[4,32]{1,0:T(4,128)}, u32[]{:S(2)}) copy-start(f32[4,32]{1,0:T(4,128)} %param.13) | copy-start | bytes 1540
  88.0 3.4 %copy-start.1 = (bf16[4,32,128,128]{3,2,1,0:T(8,128)(2,1)S(1)}, bf16[4,32,128,128]{3,2,1,0:T(8,128)(2,1)}, u32[]{:S(2)}) copy-start(bf16[4,32,128,128]{3,2,1,0:T(8,128)(2,1)} %param.12) | copy-start | bytes 12582916
  112.9 3.4 %copy-start.2 = (bf16[4,32,128,128]{3,2,1,0:T(8,128)(2,1)S(1)}, bf16[4,32,128,128]{3,2,1,0:T(8,128)(2,1)}, u32[]{:S(2)}) copy-start(bf16[4,32,128,128]{3,2,1,0:T(8,128)(2,1)} %param.12) | copy-start | bytes 12582916
  116.4 8.7 %copy-start.6 = (u32[32]{0:T(128)S(1)}, u32[32]{0:T(128)}, u32[]{:S(2)}) copy-start(u32[32]{0:T(128)} %constant.117) | copy-start | bytes 388
  116.4 10.1 %copy-start.5 = (s32[4]{0:T(128)S(1)}, s32[4]{0:T(128)}, u32[]{:S(2)}) copy-start(s32[4]{0:T(128)} %param.15) | copy-start | bytes 52
  121.0 20.9 %all-to-all-start.3 = ((bf16[16,128,128]{1,2,0:T(8,128)(2,1)}), bf16[16,128,128]{1,2,0:T(8,128)(2,1)S(1)}, u32[]{:S(2)}, u32[]{:S(2)}) async-start(bf16[16,128,128]{1,2,0:T(8,128)(2,1)} %broadcast_select_fusion.7), calls=%async_computation.3 | async-start | bytes 1048576 | tf_op jit(solution)/shard_map/all_to_all | solution.py:39
  145.0 3.4 %copy-start.3 = (bf16[4,32,128,128]{3,2,1,0:T(8,128)(2,1)S(1)}, bf16[4,32,128,128]{3,2,1,0:T(8,128)(2,1)}, u32[]{:S(2)}) copy-start(bf16[4,32,128,128]{3,2,1,0:T(8,128)(2,1)} %param.12) | copy-start | bytes 12582916
  153.1 14.3 %all-to-all-start.4 = ((bf16[16,128,128]{1,2,0:T(8,128)(2,1)}), bf16[16,128,128]{1,2,0:T(8,128)(2,1)S(1)}, u32[]{:S(2)}, u32[]{:S(2)}) async-start(bf16[16,128,128]{1,2,0:T(8,128)(2,1)} %broadcast_select_fusion.4), calls=%async_computation.4 | async-start | bytes 1048576 | tf_op jit(solution)/shard_map/all_to_all | solution.py:56
where the time goes:
time: 170 us; the launch traced here: 169 us
  blocking collectives  86.9 us (51%)
  local copies, waits for them, and re-layouts  21.8 us (13%)
  waiting for transfers between devices  18.2 us (11%)
  other arithmetic  16.3 us (10%)
  matrix products  12.2 us (7%)
  starting transfers between devices  11.2 us (7%)
  between operations  2.32 us (1%)
    all_gather x1, blocking collectives, on_device(): lax.all_gather(columns, 'rows', axis=0, tiled=True)  42.8 us
    all_to_all x2, blocking collectives, apply_blocks(): lax.all_to_all(outgoing, 'rows', split_axis=0, concat_axis=0, tiled=True)  29.2 us
    unnamed x1, blocking collectives  15 us
    dot_general x4, matrix products, product(): jnp.einsum('rkij,rkjv->rkiv', blocks, operand, preferred_element_type=jnp...  12.2 us
    gather x4, local copies, waits for them, and re-layouts, product(): jnp.take(received, source_slot, axis=0)  12 us
    select_n x5, other arithmetic, product(): jnp.take(received, source_slot, axis=0)  11.1 us
    all_to_all x1, waiting for transfers between devices, on_device(): lax.all_to_all(sending, 'rows', split_axis=0, concat_axis=0, tiled=True)  10.6 us
    all_to_all x2, starting transfers between devices, apply_blocks(): lax.all_to_all(outgoing, 'rows', split_axis=0, concat_axis=0, tiled=True)  7.62 us
  transfers between devices with their start and end apart: 3, of which 2 were waited for; matrix products, arithmetic and copies ran while one was open for 2% of the time, Pallas kernels for 0%

commit v1 on v0

--- a/solution.py
+++ b/solution.py
@@ -6,23 +6,24 @@
 STEPS = 4
 
 
+def requests(index, nrows, local_rows):
+    flat = index.reshape(-1)
+    hit = (flat // local_rows)[None, :] == jnp.arange(nrows, dtype=flat.dtype)[:, None]
+    return jnp.max(jnp.where(hit, (flat % local_rows)[None, :], 0), axis=1)
+
+
 def on_device(vectors, blocks, scales, columns, owners, center, half_width):
     nrows = lax.axis_size("rows")
     local_rows = blocks.shape[0]
     per_row = blocks.shape[1]
     orbitals = blocks.shape[2]
     group_width = vectors.shape[1]
-    myself = lax.axis_index("rows")
-    all_columns, all_owners = (
-        lax.all_gather(columns, "rows", axis=0, tiled=True),
-        lax.all_gather(owners, "rows", axis=0, tiled=True),
+    asked = jnp.stack(
+        [requests(columns, nrows, local_rows), requests(owners, nrows, local_rows)], axis=1
     )
-    table = all_columns.reshape(nrows, local_rows * per_row)
-    wanted = jnp.max(jnp.where(table // local_rows == myself, table % local_rows, 0), axis=1)
-    owner_table = all_owners.reshape(nrows, local_rows)
-    relay_want = jnp.max(
-        jnp.where(owner_table // local_rows == myself, owner_table % local_rows, 0), axis=1
-    )
+    granted = lax.all_to_all(asked, "rows", split_axis=0, concat_axis=0, tiled=True)
+    wanted = granted[:, 0]
+    relay_want = granted[:, 1]
     source_slot = (columns // local_rows).reshape(local_rows * per_row)
 
     def product(received):

time: 170 us -> 153 us (0.900)
  blocking collectives: 86.9 us -> 50.4 us
  waiting for transfers between devices: 18.2 us -> 38.1 us
    all_gather x1 -> x0, blocking collectives: 42.8 us -> none  [on_device(): lax.all_gather(columns, 'rows', axis=0, tiled=True)]
    all_to_all x2, waiting for transfers between devices: 7.59 us -> 24.6 us  [apply_blocks(): lax.all_to_all(outgoing, 'rows', split_axis=0, concat_axis=0, tiled=True)]
    all_to_all x0 -> x1, blocking collectives: none -> 15.4 us  [on_device(): lax.all_to_all(asked, 'rows', split_axis=0, concat_axis=0, tiled=True)]
    unnamed x1 -> x0, blocking collectives: 15 us -> none
    all_to_all x2, blocking collectives: 29.2 us -> 35 us  [apply_blocks(): lax.all_to_all(outgoing, 'rows', split_axis=0, concat_axis=0, tiled=True)]
    all_to_all x1, waiting for transfers between devices: 10.6 us -> 13.6 us  [on_device(): lax.all_to_all(sending, 'rows', split_axis=0, concat_axis=0, tiled=True)]
    unnamed x17 -> x10, local copies, waits for them, and re-layouts: 3.56 us -> 2.65 us
  transfers between devices with their start and end apart: 3 -> 3, of which waited for: 2 -> 3; matrix products, arithmetic and copies ran while one was open for 2% -> 1% of each run, Pallas kernels for 0% -> 0%
where the time goes in v1:
time: 153 us
  blocking collectives  50.4 us (33%)
  waiting for transfers between devices  38.1 us (25%)
  local copies, waits for them, and re-layouts  21.6 us (14%)
  other arithmetic  17.4 us (11%)
  matrix products  12.2 us (8%)
  starting transfers between devices  11.3 us (7%)
  between operations  1.55 us (1%)
    all_to_all x2, blocking collectives, apply_blocks(): lax.all_to_all(outgoing, 'rows', split_axis=0, concat_axis=0, tiled=True)  35 us
    all_to_all x2, waiting for transfers between devices, apply_blocks(): lax.all_to_all(outgoing, 'rows', split_axis=0, concat_axis=0, tiled=True)  24.6 us
    all_to_all x1, blocking collectives, on_device(): lax.all_to_all(asked, 'rows', split_axis=0, concat_axis=0, tiled=True)  15.4 us
    all_to_all x1, waiting for transfers between devices, on_device(): lax.all_to_all(sending, 'rows', split_axis=0, concat_axis=0, tiled=True)  13.6 us
    dot_general x4, matrix products, product(): jnp.einsum('rkij,rkjv->rkiv', blocks, operand, preferred_element_type=jnp...  12.2 us
    gather x4, local copies, waits for them, and re-layouts, product(): jnp.take(received, source_slot, axis=0)  12 us
    select_n x5, other arithmetic, product(): jnp.take(received, source_slot, axis=0)  11.1 us
    all_to_all x2, starting transfers between devices, apply_blocks(): lax.all_to_all(outgoing, 'rows', split_axis=0, concat_axis=0, tiled=True)  7.42 us
  transfers between devices with their start and end apart: 3, of which 3 were waited for; matrix products, arithmetic and copies ran while one was open for 1% of the time, Pallas kernels for 0%

profile of v1, /device:TPU:0, one launch (start us, length us, event | category | flops | bytes accessed | tf_op | source)
XLA Modules:
  0.0 152.7 jit_solution(18542328784386445)
XLA Ops:
  0.0 0.7 compare_and_fusion.3
  0.7 0.7 and_select_fusion
  1.3 0.8 reshape.94
  2.4 15.4 %all_to_all.37 = s32[16,1,2]{2,1,0:T(1,128)S(1)} all-to-all(s32[16,1,2]{2,1,0:T(1,128)S(1)} %copy.19), channel_id=1, replica_groups=mesh['rows'=16,'vecs'=2] {'rows'}, dimensions={0} | all-to-all | bytes 256 | tf_op jit(solution)/shard_map/all_to_all | solution.py:24
  17.9 1.6 %gather_fusion.1 = bf16[16,128,128]{2,1,0:T(8,128)(2,1)S(1)} fusion(bf16[4,128,128]{2,1,0:T(8,128)(2,1)} %bitcast.56, s32[1024]{0:T(1024)S(1)} %pad_clamp_fusion.3), kind=kCustom, calls=%fused_computation.clone | custom fusion | bytes 1048640 | tf_op jit(solution)/shard_map/jit(_take)/gather | solution.py:39
  19.5 0.9 broadcast_select_fusion.8
  20.4 3.6 %all-to-all-start.1 = ((bf16[16,128,128]{2,1,0:T(8,128)(2,1)}), bf16[16,128,128]{2,1,0:T(8,128)(2,1)S(1)}, u32[]{:S(2)}, u32[]{:S(2)}) async-start(bf16[16,128,128]{2,1,0:T(8,128)(2,1)} %broadcast_select_fusion.8), calls=%async_computation.1 | async-start | bytes 1048576 | tf_op jit(solution)/shard_map/all_to_all | solution.py:40
  23.9 1.0 copy.22
  25.0 0.7 add_select_fusion
  27.1 10.8 %all-to-all-done.1 = bf16[16,128,128]{2,1,0:T(8,128)(2,1)S(1)} async-done(((bf16[16,128,128]{2,1,0:T(8,128)(2,1)}), bf16[16,128,128]{2,1,0:T(8,128)(2,1)S(1)}, u32[]{:S(2)}, u32[]{:S(2)}) %all-to-all-start.1) | async-done | bytes 524320 | tf_op jit(solution)/shard_map/all_to_all | solution.py:40
  37.9 3.0 %gather_fusion.2 = bf16[128,128,128]{2,1,0:T(8,128)(2,1)} fusion(bf16[16,128,128]{2,1,0:T(8,128)(2,1)S(1)} %all-to-all-done.1, s32[1024]{0:T(1024)S(1)} %pad_clamp_fusion.2), kind=kCustom, calls=%fused_computation.1.clone | custom fusion | bytes 8389120 | tf_op jit(solution)/shard_map/jit(_take)/gather | solution.py:30
  40.9 2.8 %broadcast_select_fusion.3 = bf16[128,128,128]{2,1,0:T(8,128)(2,1)S(1)} fusion(bf16[128,128,128]{2,1,0:T(8,128)(2,1)} %gather_fusion.2, pred[128]{0:T(512)(128)(4,1)S(1)} %compare_and_fusion.1), kind=kLoop, calls=%fused_computation.17 | loop fusion | flops 2097152 | bytes 8388736 | tf_op jit(solution)/shard_map/jit(_take)/select_n | solution.py:30
  44.4 3.1 %multiply_reduce_fusion.3 = f32[4,128,128]{2,1,0:T(8,128)S(1)} fusion(f32[4,32]{1,0:T(4,128)S(1)} %copy-done.4, bf16[4,32,128,128]{3,2,1,0:T(8,128)(2,1)S(1)} %bitcast.53, bf16[4,32,128,128]{3,2,1,0:T(8,128)(2,1)S(1)} %copy-done), kind=kOutput, calls=%fused_computation.13 | convolution fusion | flops 540999680 | bytes 8651264 | tf_op jit(solution)/shard_map/rkij,rkjv->rkiv/dot_general | solution.py:33
  48.4 17.6 %all_to_all.38 = bf16[16,128,128]{1,2,0:T(8,128)(2,1)S(1)} all-to-all(bf16[16,128,128]{1,2,0:T(8,128)(2,1)S(1)} %broadcast_select_fusion.5), channel_id=1, replica_groups=mesh['rows'=16,'vecs'=2] {'rows'}, dimensions={0} | all-to-all | bytes 1048576 | tf_op jit(solution)/shard_map/all_to_all | solution.py:40
  65.9 3.0 %gather_fusion.4 = bf16[128,128,128]{1,2,0:T(8,128)(2,1)} fusion(bf16[16,128,128]{1,2,0:T(8,128)(2,1)S(1)} %all_to_all.38, s32[1024]{0:T(1024)S(1)} %pad_clamp_fusion.2), kind=kCustom, calls=%fused_computation.6.clone | custom fusion | bytes 8389120 | tf_op jit(solution)/shard_map/jit(_take)/gather | solution.py:30
  68.9 2.8 %broadcast_select_fusion = bf16[128,128,128]{1,2,0:T(8,128)(2,1)S(1)} fusion(bf16[128,128,128]{1,2,0:T(8,128)(2,1)} %gather_fusion.4, pred[128]{0:T(512)(128)(4,1)S(1)} %compare_and_fusion.1), kind=kLoop, calls=%fused_computation.14 | loop fusion | flops 2097152 | bytes 8388736 | tf_op jit(solution)/shard_map/jit(_take)/select_n | solution.py:30
  71.7 0.7 copy-done.1
  72.4 3.0 %multiply_reduce_fusion.2 = f32[4,128,128]{2,1,0:T(8,128)S(1)} fusion(f32[4,32]{1,0:T(4,128)S(1)} %copy-done.4, bf16[4,32,128,128]{2,3,1,0:T(8,128)(2,1)S(1)} %bitcast.54, bf16[4,32,128,128]{3,2,1,0:T(8,128)(2,1)S(1)} %copy-done.1), kind=kOutput, calls=%fused_computation.12 | convolution fusion | flops 540999680 | bytes 8651264 | tf_op jit(solution)/shard_map/rkij,rkjv->rkiv/dot_general | solution.py:33
  76.3 17.5 %all_to_all.39 = bf16[16,128,128]{1,2,0:T(8,128)(2,1)S(1)} all-to-all(bf16[16,128,128]{1,2,0:T(8,128)(2,1)S(1)} %broadcast_select_fusion.6), channel_id=1, replica_groups=mesh['rows'=16,'vecs'=2] {'rows'}, dimensions={0} | all-to-all | bytes 1048576 | tf_op jit(solution)/shard_map/all_to_all | solution.py:40
  93.8 3.0 %gather_fusion.6 = bf16[128,128,128]{1,2,0:T(8,128)(2,1)} fusion(bf16[16,128,128]{1,2,0:T(8,128)(2,1)S(1)} %all_to_all.39, s32[1024]{0:T(1024)S(1)} %pad_clamp_fusion.2), kind=kCustom, calls=%fused_computation.7.clone | custom fusion | bytes 8389120 | tf_op jit(solution)/shard_map/jit(_take)/gather | solution.py:30
  96.8 2.8 %broadcast_select_fusion.1 = bf16[128,128,128]{1,2,0:T(8,128)(2,1)S(1)} fusion(bf16[128,128,128]{1,2,0:T(8,128)(2,1)} %gather_fusion.6, pred[128]{0:T(512)(128)(4,1)S(1)} %compare_and_fusion.1), kind=kLoop, calls=%fused_computation.15 | loop fusion | flops 2097152 | bytes 8388736 | tf_op jit(solution)/shard_map/jit(_take)/select_n | solution.py:30
  100.2 3.0 %multiply_reduce_fusion.1 = f32[4,128,128]{2,1,0:T(8,128)S(1)} fusion(f32[4,32]{1,0:T(4,128)S(1)} %copy-done.4, bf16[4,32,128,128]{2,3,1,0:T(8,128)(2,1)S(1)} %bitcast.55, bf16[4,32,128,128]{3,2,1,0:T(8,128)(2,1)S(1)} %copy-done.2), kind=kOutput, calls=%fused_computation.11 | convolution fusion | flops 540999680 | bytes 8651264 | tf_op jit(solution)/shard_map/rkij,rkjv->rkiv/dot_general | solution.py:33
  104.0 0.9 broadcast_select_fusion.7
  104.9 3.9 %all-to-all-start.4 = ((bf16[16,128,128]{1,2,0:T(8,128)(2,1)}), bf16[16,128,128]{1,2,0:T(8,128)(2,1)S(1)}, u32[]{:S(2)}, u32[]{:S(2)}) async-start(bf16[16,128,128]{1,2,0:T(8,128)(2,1)} %broadcast_select_fusion.7), calls=%async_computation.4 | async-start | bytes 1048576 | tf_op jit(solution)/shard_map/all_to_all | solution.py:40
  108.8 13.7 %all-to-all-done.4 = bf16[16,128,128]{1,2,0:T(8,128)(2,1)S(1)} async-done(((bf16[16,128,128]{1,2,0:T(8,128)(2,1)}), bf16[16,128,128]{1,2,0:T(8,128)(2,1)S(1)}, u32[]{:S(2)}, u32[]{:S(2)}) %all-to-all-start.4) | async-done | bytes 524320 | tf_op jit(solution)/shard_map/all_to_all | solution.py:40
  122.5 3.0 %gather_fusion.8 = bf16[128,128,128]{1,2,0:T(8,128)(2,1)} fusion(bf16[16,128,128]{1,2,0:T(8,128)(2,1)S(1)} %all-to-all-done.4, s32[1024]{0:T(1024)S(1)} %pad_clamp_fusion.2), kind=kCustom, calls=%fused_computation.8.clone | custom fusion | bytes 8389120 | tf_op jit(solution)/shard_map/jit(_take)/gather | solution.py:30
  125.5 2.8 %broadcast_select_fusion.2 = bf16[128,128,128]{1,2,0:T(8,128)(2,1)S(1)} fusion(bf16[128,128,128]{1,2,0:T(8,128)(2,1)} %gather_fusion.8, pred[128]{0:T(512)(128)(4,1)S(1)} %compare_and_fusion.1), kind=kLoop, calls=%fused_computation.16 | loop fusion | flops 2097152 | bytes 8388736 | tf_op jit(solution)/shard_map/jit(_take)/select_n | solution.py:30
  128.9 3.0 %multiply_reduce_fusion = f32[4,128,128]{2,1,0:T(8,128)S(1)} fusion(f32[4,32]{1,0:T(4,128)S(1)} %copy-done.4, bf16[4,32,128,128]{2,3,1,0:T(8,128)(2,1)S(1)} %bitcast.52, bf16[4,32,128,128]{3,2,1,0:T(8,128)(2,1)S(1)} %copy-done.3), kind=kOutput, calls=%fused_computation.10 | convolution fusion | flops 540999680 | bytes 8651264 | tf_op jit(solution)/shard_map/rkij,rkjv->rkiv/dot_general | solution.py:33
  132.7 0.9 broadcast_select_fusion.4
  133.6 3.8 %all-to-all-start.5 = ((bf16[16,128,128]{1,2,0:T(8,128)(2,1)}), bf16[16,128,128]{1,2,0:T(8,128)(2,1)S(1)}, u32[]{:S(2)}, u32[]{:S(2)}) async-start(bf16[16,128,128]{1,2,0:T(8,128)(2,1)} %broadcast_select_fusion.4), calls=%async_computation.5 | async-start | bytes 1048576 | tf_op jit(solution)/shard_map/all_to_all | solution.py:57
  137.6 13.6 %all-to-all-done.5 = bf16[16,128,128]{1,2,0:T(8,128)(2,1)S(1)} async-done(((bf16[16,128,128]{1,2,0:T(8,128)(2,1)}), bf16[16,128,128]{1,2,0:T(8,128)(2,1)S(1)}, u32[]{:S(2)}, u32[]{:S(2)}) %all-to-all-start.5) | async-done | bytes 524320 | tf_op jit(solution)/shard_map/all_to_all | solution.py:57
  151.9 0.8 bitcast_select_fusion
  (37 shorter events, 6.4 us)
Async XLA Ops:
  20.4 17.6 %all-to-all-start.1 = ((bf16[16,128,128]{2,1,0:T(8,128)(2,1)}), bf16[16,128,128]{2,1,0:T(8,128)(2,1)S(1)}, u32[]{:S(2)}, u32[]{:S(2)}) async-start(bf16[16,128,128]{2,1,0:T(8,128)(2,1)} %broadcast_select_fusion.8), calls=%async_computation.1 | async-start | bytes 1048576 | tf_op jit(solution)/shard_map/all_to_all | solution.py:40
  40.9 3.4 %copy-start = (bf16[4,32,128,128]{3,2,1,0:T(8,128)(2,1)S(1)}, bf16[4,32,128,128]{3,2,1,0:T(8,128)(2,1)}, u32[]{:S(2)}) copy-start(bf16[4,32,128,128]{3,2,1,0:T(8,128)(2,1)} %param.12) | copy-start | bytes 12582916
  40.9 3.4 %copy-start.4 = (f32[4,32]{1,0:T(4,128)S(1)}, f32[4,32]{1,0:T(4,128)}, u32[]{:S(2)}) copy-start(f32[4,32]{1,0:T(4,128)} %param.13) | copy-start | bytes 1540
  68.9 3.4 %copy-start.1 = (bf16[4,32,128,128]{3,2,1,0:T(8,128)(2,1)S(1)}, bf16[4,32,128,128]{3,2,1,0:T(8,128)(2,1)}, u32[]{:S(2)}) copy-start(bf16[4,32,128,128]{3,2,1,0:T(8,128)(2,1)} %param.12) | copy-start | bytes 12582916
  96.8 3.4 %copy-start.2 = (bf16[4,32,128,128]{3,2,1,0:T(8,128)(2,1)S(1)}, bf16[4,32,128,128]{3,2,1,0:T(8,128)(2,1)}, u32[]{:S(2)}) copy-start(bf16[4,32,128,128]{3,2,1,0:T(8,128)(2,1)} %param.12) | copy-start | bytes 12582916
  104.9 17.6 %all-to-all-start.4 = ((bf16[16,128,128]{1,2,0:T(8,128)(2,1)}), bf16[16,128,128]{1,2,0:T(8,128)(2,1)S(1)}, u32[]{:S(2)}, u32[]{:S(2)}) async-start(bf16[16,128,128]{1,2,0:T(8,128)(2,1)} %broadcast_select_fusion.7), calls=%async_computation.4 | async-start | bytes 1048576 | tf_op jit(solution)/shard_map/all_to_all | solution.py:40
  125.5 3.4 %copy-start.3 = (bf16[4,32,128,128]{3,2,1,0:T(8,128)(2,1)S(1)}, bf16[4,32,128,128]{3,2,1,0:T(8,128)(2,1)}, u32[]{:S(2)}) copy-start(bf16[4,32,128,128]{3,2,1,0:T(8,128)(2,1)} %param.12) | copy-start | bytes 12582916
  133.6 17.5 %all-to-all-start.5 = ((bf16[16,128,128]{1,2,0:T(8,128)(2,1)}), bf16[16,128,128]{1,2,0:T(8,128)(2,1)S(1)}, u32[]{:S(2)}, u32[]{:S(2)}) async-start(bf16[16,128,128]{1,2,0:T(8,128)(2,1)} %broadcast_select_fusion.4), calls=%async_computation.5 | async-start | bytes 1048576 | tf_op jit(solution)/shard_map/all_to_all | solution.py:57

commit v2 on v1

v2 whole, which is shorter than its diff:
```python
import jax
import jax.numpy as jnp
from jax import lax
from jax.sharding import PartitionSpec as P

STEPS = 4


def on_device(vectors, blocks, scales, columns, owners, center, half_width):
    local_rows = blocks.shape[0]
    per_row = blocks.shape[1]
    orbitals = blocks.shape[2]
    group_width = vectors.shape[1]

    def gather_all(panels):
        return lax.all_gather(panels, "rows", axis=0, tiled=True)

    def apply_blocks(panels):
        everything = gather_all(panels)
        operand = jnp.take(everything, columns.reshape(-1), axis=0).reshape(
            local_rows, per_row, orbitals, group_width
        )
        partial_value = jnp.einsum(
            "rkij,rkjv->rkiv", blocks, operand, preferred_element_type=jnp.float32
        )
        return jnp.sum(partial_value * scales[:, :, None, None], axis=1)

    shift = center[0]
    width = half_width[0]
    previous = vectors.reshape(local_rows, orbitals, group_width)
    current = ((apply_blocks(previous) - shift * previous.astype(jnp.float32)) / width).astype(
        jnp.bfloat16
    )
    for step in range(STEPS - 1):
        image = apply_blocks(current)
        upcoming = (
            2.0 * (image - shift * current.astype(jnp.float32)) / width
            - previous.astype(jnp.float32)
        ).astype(jnp.bfloat16)
        previous, current = (current, upcoming)
    placed = jnp.take(gather_all(current), owners, axis=0)
    return placed.reshape(local_rows * orbitals, group_width)


def solution(mesh):
    in_specs = (
        P("rows", "vecs"),
        P("rows", None, None, None),
        P("rows", None),
        P("rows", None),
        P("rows"),
        P(),
        P(),
    )
    out_specs = P("rows", "vecs")
    return jax.shard_map(
        on_device, mesh=mesh, in_specs=in_specs, out_specs=out_specs, check_vma=False
    )
```

time: 153 us -> 370 us (2.42)
  waiting for transfers between devices: 38.1 us -> 301 us
  blocking collectives: 50.4 us -> 0 us
  between operations: 1.55 us -> 14.6 us
  starting transfers between devices: 11.3 us -> 0.35 us
  local copies, waits for them, and re-layouts: 21.6 us -> 28.2 us
  other arithmetic: 17.4 us -> 12.2 us
    all_gather x0 -> x5, waiting for transfers between devices: none -> 301 us  [gather_all(): return lax.all_gather(panels, 'rows', axis=0, tiled=True)]
    all_to_all x3 -> x0, blocking collectives: 50.4 us -> none  [the longest x2 35 us: apply_blocks(): lax.all_to_all(outgoing, 'rows', split_axis=0, concat_axis=0, tiled=True)]
    all_to_all x3 -> x0, waiting for transfers between devices: 38.1 us -> none  [the longest x2 24.6 us: apply_blocks(): lax.all_to_all(outgoing, 'rows', split_axis=0, concat_axis=0, tiled=True)]
    all_to_all x3 -> x0, starting transfers between devices: 11.3 us -> none  [the longest x2 7.42 us: apply_blocks(): lax.all_to_all(outgoing, 'rows', split_axis=0, concat_axis=0, tiled=True)]
    select_n x15 -> x7, other arithmetic: 16.2 us -> 11.9 us  [the longest x5 11.1 us: apply_blocks(): jnp.take(everything, columns.reshape(-1), axis=0)]
    gather x11 -> x5, local copies, waits for them, and re-layouts: 16.9 us -> 20.6 us  [the longest x4 18.5 us: apply_blocks(): jnp.take(everything, columns.reshape(-1), axis=0)]
  transfers between devices with their start and end apart: 3 -> 5, of which waited for: 3 -> 5; matrix products, arithmetic and copies ran while one was open for 1% -> 1% of each run, Pallas kernels for 0% -> 0%
where the time goes in v2:
time: 370 us; the launch traced here: 369 us
  waiting for transfers between devices  301 us (81%)
  local copies, waits for them, and re-layouts  28.2 us (8%)
  between operations  14.6 us (4%)
  matrix products  12.6 us (3%)
  other arithmetic  12.2 us (3%)
    all_gather x5, waiting for transfers between devices, gather_all(): return lax.all_gather(panels, 'rows', axis=0, tiled=True)  301 us
    gather x4, local copies, waits for them, and re-layouts, apply_blocks(): jnp.take(everything, columns.reshape(-1), axis=0)  18.5 us
    dot_general x4, matrix products, apply_blocks(): jnp.einsum('rkij,rkjv->rkiv', blocks, operand, preferred_element_type=jnp...  12.6 us
    select_n x5, other arithmetic, apply_blocks(): jnp.take(everything, columns.reshape(-1), axis=0)  11.1 us
  transfers between devices with their start and end apart: 5, of which 5 were waited for; matrix products, arithmetic and copies ran while one was open for 1% of the time, Pallas kernels for 0%

profile of v2, /device:TPU:0, one launch (start us, length us, event | category | flops | bytes accessed | tf_op | source)
XLA Modules:
  0.0 369.5 jit_solution(10198902864211018663)
XLA Ops:
  6.5 0.7 all-gather.6.cloned.1.call-update
  7.3 1.0 copy.22
  8.3 0.8 reshape.36
  10.4 63.1 %all-gather.6.cloned.1.call-done = bf16[64,128,128]{2,1,0:T(8,128)(2,1)} async-done(((bf16[4,128,128]{2,1,0:T(8,128)(2,1)}), bf16[64,128,128]{2,1,0:T(8,128)(2,1)}) %all-gather.6.cloned.1.call-update) | async-done | bytes 2097168 | tf_op jit(solution)/shard_map/all_gather | solution.py:16
  73.6 4.6 %gather_fusion.1 = bf16[128,128,128]{2,1,0:T(8,128)(2,1)} fusion(bf16[64,128,128]{2,1,0:T(8,128)(2,1)} %all-gather.6.cloned.1.call-done, s32[1024]{0:T(1024)S(1)} %pad_clamp_fusion.1), kind=kCustom, calls=%fused_computation.clone | custom fusion | bytes 8389120 | tf_op jit(solution)/shard_map/jit(_take)/gather | solution.py:20
  78.2 2.8 broadcast_select_fusion
  81.0 0.7 copy-done
  81.6 3.2 multiply_reduce_fusion.3
  84.8 0.8 copy.23
  85.7 59.5 %all-gather.8.cloned.1.call-done = bf16[64,128,128]{2,1,0:T(8,128)(2,1)} async-done(((bf16[4,128,128]{2,1,0:T(8,128)(2,1)}), bf16[64,128,128]{2,1,0:T(8,128)(2,1)}) %all-gather.8.cloned.1.call-update) | async-done | bytes 2097168 | tf_op jit(solution)/shard_map/all_gather | solution.py:16
  145.2 4.6 %gather_fusion.2 = bf16[128,128,128]{2,1,0:T(8,128)(2,1)} fusion(bf16[64,128,128]{2,1,0:T(8,128)(2,1)} %all-gather.8.cloned.1.call-done, s32[1024]{0:T(1024)S(1)} %pad_clamp_fusion.1), kind=kCustom, calls=%fused_computation.1.clone | custom fusion | bytes 8389120 | tf_op jit(solution)/shard_map/jit(_take)/gather | solution.py:20
  149.8 2.8 broadcast_select_fusion.1
  152.6 0.7 copy-done.1
  153.2 3.1 multiply_reduce_fusion.2
  156.5 0.8 copy.25
  157.3 59.5 %all-gather.10.cloned.1.call-done = bf16[64,128,128]{2,1,0:T(8,128)(2,1)} async-done(((bf16[4,128,128]{2,1,0:T(8,128)(2,1)}), bf16[64,128,128]{2,1,0:T(8,128)(2,1)}) %all-gather.10.cloned.1.call-update) | async-done | bytes 2097168 | tf_op jit(solution)/shard_map/all_gather | solution.py:16
  216.8 4.6 %gather_fusion.3 = bf16[128,128,128]{2,1,0:T(8,128)(2,1)} fusion(bf16[64,128,128]{2,1,0:T(8,128)(2,1)} %all-gather.10.cloned.1.call-done, s32[1024]{0:T(1024)S(1)} %pad_clamp_fusion.1), kind=kCustom, calls=%fused_computation.2.clone | custom fusion | bytes 8389120 | tf_op jit(solution)/shard_map/jit(_take)/gather | solution.py:20
  221.4 2.8 broadcast_select_fusion.2
  224.2 0.7 copy-done.2
  224.8 3.1 multiply_reduce_fusion.1
  228.1 0.8 copy.27
  228.9 0.2 all-gather.14.cloned.1.call-start
  229.1 59.3 %all-gather.12.cloned.1.call-done = bf16[64,128,128]{2,1,0:T(8,128)(2,1)} async-done(((bf16[4,128,128]{2,1,0:T(8,128)(2,1)}), bf16[64,128,128]{2,1,0:T(8,128)(2,1)}) %all-gather.12.cloned.1.call-update) | async-done | bytes 2097168 | tf_op jit(solution)/shard_map/all_gather | solution.py:16
  288.4 4.6 %gather_fusion.4 = bf16[128,128,128]{2,1,0:T(8,128)(2,1)} fusion(bf16[64,128,128]{2,1,0:T(8,128)(2,1)} %all-gather.12.cloned.1.call-done, s32[1024]{0:T(1024)S(1)} %pad_clamp_fusion.1), kind=kCustom, calls=%fused_computation.3.clone | custom fusion | bytes 8389120 | tf_op jit(solution)/shard_map/jit(_take)/gather | solution.py:20
  293.0 2.8 broadcast_select_fusion.3
  295.8 0.7 copy-done.3
  296.4 3.1 multiply_reduce_fusion
  299.6 0.1 fusion.11
  299.7 0.8 copy.29
  300.6 59.4 %all-gather.14.cloned.1.call-done = bf16[64,128,128]{2,1,0:T(8,128)(2,1)} async-done(((bf16[4,128,128]{2,1,0:T(8,128)(2,1)}), bf16[64,128,128]{2,1,0:T(8,128)(2,1)}) %all-gather.14.cloned.1.call-update) | async-done | bytes 2097168 | tf_op jit(solution)/shard_map/all_gather | solution.py:16
  360.0 2.2 gather_fusion
  362.2 0.8 bitcast_select_fusion
  (26 shorter events, 0.5 us)
Async XLA Ops:
  6.5 67.0 %all-gather.6.cloned.1.call-start = ((), (), s32[]{:S(2)}) async-start(), calls=%async_computation | async-start | bytes 2228224 | tf_op jit(solution)/shard_map/all_gather | solution.py:16
  7.3 137.9 %all-gather.8.cloned.1.call-start = ((), (), s32[]{:S(2)}) async-start(), calls=%async_computation.1 | async-start | bytes 2228224 | tf_op jit(solution)/shard_map/all_gather | solution.py:16
  78.2 3.4 copy-start
  78.2 3.4 copy-start.4
  85.6 131.1 %all-gather.10.cloned.1.call-start = ((), (), s32[]{:S(2)}) async-start(), calls=%async_computation.2 | async-start | bytes 2228224 | tf_op jit(solution)/shard_map/all_gather | solution.py:16
  149.8 3.4 copy-start.1
  157.3 131.1 %all-gather.12.cloned.1.call-start = ((), (), s32[]{:S(2)}) async-start(), calls=%async_computation.3 | async-start | bytes 2228224 | tf_op jit(solution)/shard_map/all_gather | solution.py:16
  221.4 3.4 copy-start.2
  228.9 131.1 %all-gather.14.cloned.1.call-start = ((), (), s32[]{:S(2)}) async-start(), calls=%async_computation.4 | async-start | bytes 2228224 | tf_op jit(solution)/shard_map/all_gather | solution.py:16
  293.0 3.4 copy-start.3
  296.4 4.0 %copy-start.5 = (s32[4]{0:T(128)S(1)}, s32[4]{0:T(128)}, u32[]{:S(2)}) copy-start(s32[4]{0:T(128)} %param.13) | copy-start | bytes 52
Sparse Core Ops, SparseCore 0:
  10.1 63.3 all-gather.5
  85.8 59.3 all-gather.7
  157.4 59.3 all-gather.9
  229.0 59.3 all-gather.11
  300.6 59.3 all-gather.13

commit v3 on v1

v3 whole, which is shorter than its diff:
```python
import functools

import jax
import jax.numpy as jnp
from jax import lax
from jax.experimental import pallas as pl
from jax.experimental.pallas import tpu as pltpu
from jax.sharding import PartitionSpec as P

STEPS = 4


def requests(index, nrows, local_rows):
    flat = index.reshape(-1)
    hit = (flat // local_rows)[None, :] == jnp.arange(nrows, dtype=flat.dtype)[:, None]
    return jnp.max(jnp.where(hit, (flat % local_rows)[None, :], 0), axis=1)


def step_kernel(first, per_row, slot_ref, scl_ref, sw_ref, recv_ref, blk_ref, cur_ref, *rest):
    if first:
        (out_ref,) = rest
    else:
        prev_ref, out_ref = rest
    r = pl.program_id(0)

    def body(k, acc):
        s = slot_ref[r * per_row + k]
        prod = jnp.dot(blk_ref[0, k], recv_ref[s], preferred_element_type=jnp.float32)
        return acc + scl_ref[r, k] * prod

    acc = lax.fori_loop(
        0, per_row, body, jnp.zeros(out_ref.shape[1:], jnp.float32), unroll=True
    )
    shift = sw_ref[0]
    width = sw_ref[1]
    cur = cur_ref[0].astype(jnp.float32)
    if first:
        new = (acc - shift * cur) / width
    else:
        new = 2.0 * (acc - shift * cur) / width - prev_ref[0].astype(jnp.float32)
    out_ref[0] = new.astype(out_ref.dtype)


def chebyshev_step(slot, scales, sw, received, blocks, cur, prev):
    local_rows, per_row, orbitals, _ = blocks.shape
    width = cur.shape[2]
    first = prev is None
    row_spec = pl.BlockSpec((1, orbitals, width), lambda r, s: (r, 0, 0))
    in_specs = [
        pl.BlockSpec(memory_space=pltpu.SMEM),
        pl.BlockSpec(memory_space=pltpu.SMEM),
        pl.BlockSpec(received.shape, lambda r, s: (0, 0, 0)),
        pl.BlockSpec((1, per_row, orbitals, orbitals), lambda r, s: (r, 0, 0, 0)),
        row_spec,
    ]
    args = [scales, sw, received, blocks, cur]
    if not first:
        in_specs.append(row_spec)
        args.append(prev)
    flops = 2 * local_rows * per_row * orbitals * orbitals * width
    nbytes = blocks.size * 2 + received.size * 2 + 3 * cur.size * 2
    return pl.pallas_call(
        functools.partial(step_kernel, first, per_row),
        out_shape=jax.ShapeDtypeStruct(cur.shape, jnp.bfloat16),
        grid_spec=pltpu.PrefetchScalarGridSpec(
            num_scalar_prefetch=1,
            grid=(local_rows,),
            in_specs=in_specs,
            out_specs=row_spec,
        ),
        cost_estimate=pl.CostEstimate(flops=flops, bytes_accessed=nbytes, transcendentals=0),
    )(slot, *args)


def on_device(vectors, blocks, scales, columns, owners, center, half_width):
    nrows = lax.axis_size("rows")
    local_rows = blocks.shape[0]
    orbitals = blocks.shape[2]
    group_width = vectors.shape[1]
    asked = jnp.stack(
        [requests(columns, nrows, local_rows), requests(owners, nrows, local_rows)], axis=1
    )
    granted = lax.all_to_all(asked, "rows", split_axis=0, concat_axis=0, tiled=True)
    wanted = granted[:, 0]
    relay_want = granted[:, 1]
    slot = (columns // local_rows).reshape(-1)
    sw = jnp.concatenate([center, half_width])

    def exchange(panels):
        outgoing = jnp.take(panels, wanted, axis=0)
        return lax.all_to_all(outgoing, "rows", split_axis=0, concat_axis=0, tiled=True)

    previous = vectors.reshape(local_rows, orbitals, group_width)
    current = chebyshev_step(slot, scales, sw, exchange(previous), blocks, previous, None)
    for step in range(STEPS - 1):
        upcoming = chebyshev_step(slot, scales, sw, exchange(current), blocks, current, previous)
        previous, current = (current, upcoming)
    sending = jnp.take(current, relay_want, axis=0)
    arrived = lax.all_to_all(sending, "rows", split_axis=0, concat_axis=0, tiled=True)
    placed = jnp.take(arrived, owners // local_rows, axis=0)
    return placed.reshape(local_rows * orbitals, group_width)


def solution(mesh):
    in_specs = (
        P("rows", "vecs"),
        P("rows", None, None, None),
        P("rows", None),
        P("rows", None),
        P("rows"),
        P(),
        P(),
    )
    out_specs = P("rows", "vecs")
    return jax.shard_map(
        on_device, mesh=mesh, in_specs=in_specs, out_specs=out_specs, check_vma=False
    )
```

time: 153 us -> 143 us (0.935)
  Pallas kernels: 0 us -> 22.1 us
  matrix products: 12.2 us -> 0 us
  other arithmetic: 17.4 us -> 6.67 us
  local copies, waits for them, and re-layouts: 21.6 us -> 11.5 us
    pallas_call x0 -> x4, Pallas kernels: none -> 22.1 us  [chebyshev_step(): pl.pallas_call(functools.partial(step_kernel, first, per_row), out_shape=...]
    dot_general x4 -> x0, matrix products: 12.2 us -> none  [product(): jnp.einsum('rkij,rkjv->rkiv', blocks, operand, preferred_element_type=jnp...]
    select_n x10 -> x5, other arithmetic: 13.9 us -> 2.72 us  [the longest x4 2.03 us: exchange(): outgoing = jnp.take(panels, wanted, axis=0)]
    gather x8 -> x4, local copies, waits for them, and re-layouts: 15.5 us -> 6.2 us  [exchange(): outgoing = jnp.take(panels, wanted, axis=0)]
where the time goes in v3:
time: 143 us; the launch traced here: 142 us
  blocking collectives  50.6 us (35%)
  waiting for transfers between devices  38.1 us (27%)
  Pallas kernels  22.1 us (15%)
  local copies, waits for them, and re-layouts  11.5 us (8%)
  starting transfers between devices  11.3 us (8%)
  other arithmetic  6.67 us (5%)
  between operations  1.44 us (1%)
    all_to_all x2, blocking collectives, exchange(): lax.all_to_all(outgoing, 'rows', split_axis=0, concat_axis=0, tiled=True)  35.2 us
    all_to_all x2, waiting for transfers between devices, exchange(): lax.all_to_all(outgoing, 'rows', split_axis=0, concat_axis=0, tiled=True)  24.5 us
    pallas_call x4, Pallas kernels, chebyshev_step(): pl.pallas_call(functools.partial(step_kernel, first, per_row), out_shape=...  22.1 us
    all_to_all x1, blocking collectives, on_device(): lax.all_to_all(asked, 'rows', split_axis=0, concat_axis=0, tiled=True)  15.4 us
    all_to_all x1, waiting for transfers between devices, on_device(): lax.all_to_all(sending, 'rows', split_axis=0, concat_axis=0, tiled=True)  13.6 us
    all_to_all x2, starting transfers between devices, exchange(): lax.all_to_all(outgoing, 'rows', split_axis=0, concat_axis=0, tiled=True)  7.42 us
    gather x4, local copies, waits for them, and re-layouts, exchange(): outgoing = jnp.take(panels, wanted, axis=0)  6.2 us
    all_to_all x1, starting transfers between devices, on_device(): lax.all_to_all(sending, 'rows', split_axis=0, concat_axis=0, tiled=True)  3.84 us
  transfers between devices with their start and end apart: 3, of which 3 were waited for; matrix products, arithmetic and copies ran while one was open for 1% of the time, Pallas kernels for 0%

profile of v3, /device:TPU:0, one launch (start us, length us, event | category | flops | bytes accessed | tf_op | source)
XLA Modules:
  0.0 141.6 jit_solution(13866856454518616298)
XLA Ops:
  0.0 0.7 compare_and_fusion.2
  0.7 0.7 and_select_fusion
  1.3 0.8 reshape.77
  2.1 0.1 select_reduce_fusion
  2.4 15.4 %all_to_all.37 = s32[16,1,2]{2,1,0:T(1,128)S(1)} all-to-all(s32[16,1,2]{2,1,0:T(1,128)S(1)} %copy.10), channel_id=1, replica_groups=mesh['rows'=16,'vecs'=2] {'rows'}, dimensions={0} | all-to-all | bytes 256 | tf_op jit(solution)/shard_map/all_to_all | solution.py:83
  17.9 1.6 %gather_fusion.1 = bf16[16,128,128]{2,1,0:T(8,128)(2,1)S(1)} fusion(bf16[4,128,128]{2,1,0:T(8,128)(2,1)} %bitcast.16, s32[1024]{0:T(1024)S(1)} %pad_clamp_fusion.2), kind=kCustom, calls=%fused_computation.clone | custom fusion | bytes 1048640 | tf_op jit(solution)/shard_map/jit(_take)/gather | solution.py:90
  19.5 0.9 broadcast_select_fusion.1
  20.4 3.6 %all-to-all-start.1 = ((bf16[16,128,128]{2,1,0:T(8,128)(2,1)}), bf16[16,128,128]{2,1,0:T(8,128)(2,1)S(1)}, u32[]{:S(2)}, u32[]{:S(2)}) async-start(bf16[16,128,128]{2,1,0:T(8,128)(2,1)} %broadcast_select_fusion.1), calls=%async_computation.1 | async-start | bytes 1048576 | tf_op jit(solution)/shard_map/all_to_all | solution.py:91
  23.9 0.7 add_select_fusion
  24.6 0.6 reshape.75.slot_ref
  26.5 0.7 pad_maximum_fusion.sw_ref
  27.2 10.7 %all-to-all-done.1.recv_ref = bf16[16,128,128]{2,1,0:T(8,128)(2,1)S(1)} async-done(((bf16[16,128,128]{2,1,0:T(8,128)(2,1)}), bf16[16,128,128]{2,1,0:T(8,128)(2,1)S(1)}, u32[]{:S(2)}, u32[]{:S(2)}) %all-to-all-start.1) | async-done | bytes 524320 | tf_op jit(solution)/shard_map/all_to_all | solution.py:91
  37.9 0.8 copy-done
  38.7 5.5 %shard_map.73.cur_ref.rest_0_ = bf16[4,128,128]{2,1,0:T(8,128)(2,1)} custom-call(s32[128]{0:T(128)} %reshape.75.slot_ref, f32[4,32]{1,0:T(4,128)} %scl_ref.7, f32[2]{0:T(128)} %pad_maximum_fusion.sw_ref, bf16[16,128,128]{2,1,0:T(8,128)(2,1)} %copy-done, bf16[4,32,128,128]{3,2,1,0:T(8,128)(2,1)} %blk_ref.7, bf16[4,128,128]{2,1,0:T(8,128)(2,1)} %bitcast.17), custom_call_target="tpu_custom_call" | custom-call | flops 536870912 | bytes 5111808 | tf_op jit(solution)/shard_map/pallas_call | solution.py:62
  44.2 1.5 %gather_fusion.2 = bf16[16,128,128]{2,1,0:T(8,128)(2,1)S(1)} fusion(bf16[4,128,128]{2,1,0:T(8,128)(2,1)} %shard_map.73.cur_ref.rest_0_, s32[1024]{0:T(1024)S(1)} %pad_clamp_fusion.2), kind=kCustom, calls=%fused_computation.1.clone | custom fusion | bytes 1048640 | tf_op jit(solution)/shard_map/jit(_take)/gather | solution.py:90
  45.9 17.7 %all_to_all.38.recv_ref = bf16[16,128,128]{2,1,0:T(8,128)(2,1)} all-to-all(bf16[16,128,128]{2,1,0:T(8,128)(2,1)S(1)} %broadcast_select_fusion.2), channel_id=1, replica_groups=mesh['rows'=16,'vecs'=2] {'rows'}, dimensions={0} | all-to-all | bytes 1048576 | tf_op jit(solution)/shard_map/all_to_all | solution.py:91
  63.5 5.5 %shard_map.74.cur_ref.rest_0_ = bf16[4,128,128]{2,1,0:T(8,128)(2,1)} custom-call(s32[128]{0:T(128)} %reshape.75.slot_ref, f32[4,32]{1,0:T(4,128)} %scl_ref.7, f32[2]{0:T(128)} %pad_maximum_fusion.sw_ref, bf16[16,128,128]{2,1,0:T(8,128)(2,1)} %all_to_all.38.recv_ref, bf16[4,32,128,128]{3,2,1,0:T(8,128)(2,1)} %blk_ref.7, ...), custom_call_target="tpu_custom_call" | custom-call | flops 536870912 | bytes 5111808 | tf_op jit(solution)/shard_map/pallas_call | solution.py:62
  69.0 1.5 %gather_fusion.3 = bf16[16,128,128]{2,1,0:T(8,128)(2,1)S(1)} fusion(bf16[4,128,128]{2,1,0:T(8,128)(2,1)} %shard_map.74.cur_ref.rest_0_, s32[1024]{0:T(1024)S(1)} %pad_clamp_fusion.2), kind=kCustom, calls=%fused_computation.2.clone | custom fusion | bytes 1048640 | tf_op jit(solution)/shard_map/jit(_take)/gather | solution.py:90
  70.7 17.6 %all_to_all.39.recv_ref = bf16[16,128,128]{2,1,0:T(8,128)(2,1)} all-to-all(bf16[16,128,128]{2,1,0:T(8,128)(2,1)S(1)} %broadcast_select_fusion.3), channel_id=1, replica_groups=mesh['rows'=16,'vecs'=2] {'rows'}, dimensions={0} | all-to-all | bytes 1048576 | tf_op jit(solution)/shard_map/all_to_all | solution.py:91
  88.3 5.5 %shard_map.75.cur_ref = bf16[4,128,128]{2,1,0:T(8,128)(2,1)} custom-call(s32[128]{0:T(128)} %reshape.75.slot_ref, f32[4,32]{1,0:T(4,128)} %scl_ref.7, f32[2]{0:T(128)} %pad_maximum_fusion.sw_ref, bf16[16,128,128]{2,1,0:T(8,128)(2,1)} %all_to_all.39.recv_ref, bf16[4,32,128,128]{3,2,1,0:T(8,128)(2,1)} %blk_ref.7, ...), custom_call_target="tpu_custom_call" | custom-call | flops 536870912 | bytes 5111808 | tf_op jit(solution)/shard_map/pallas_call | solution.py:62
  93.8 1.5 %gather_fusion.4 = bf16[16,128,128]{2,1,0:T(8,128)(2,1)S(1)} fusion(bf16[4,128,128]{2,1,0:T(8,128)(2,1)} %shard_map.75.cur_ref, s32[1024]{0:T(1024)S(1)} %pad_clamp_fusion.2), kind=kCustom, calls=%fused_computation.3.clone | custom fusion | bytes 1048640 | tf_op jit(solution)/shard_map/jit(_take)/gather | solution.py:90
  95.4 0.9 broadcast_select_fusion.4
  96.3 3.9 %all-to-all-start.4 = ((bf16[16,128,128]{2,1,0:T(8,128)(2,1)}), bf16[16,128,128]{2,1,0:T(8,128)(2,1)S(1)}, u32[]{:S(2)}, u32[]{:S(2)}) async-start(bf16[16,128,128]{2,1,0:T(8,128)(2,1)} %broadcast_select_fusion.4), calls=%async_computation.4 | async-start | bytes 1048576 | tf_op jit(solution)/shard_map/all_to_all | solution.py:91
  100.2 13.7 %all-to-all-done.4.recv_ref = bf16[16,128,128]{2,1,0:T(8,128)(2,1)S(1)} async-done(((bf16[16,128,128]{2,1,0:T(8,128)(2,1)}), bf16[16,128,128]{2,1,0:T(8,128)(2,1)S(1)}, u32[]{:S(2)}, u32[]{:S(2)}) %all-to-all-start.4) | async-done | bytes 524320 | tf_op jit(solution)/shard_map/all_to_all | solution.py:91
  113.9 0.8 copy-done.1
  114.7 5.5 %shard_map.76 = bf16[4,128,128]{2,1,0:T(8,128)(2,1)} custom-call(s32[128]{0:T(128)} %reshape.75.slot_ref, f32[4,32]{1,0:T(4,128)} %scl_ref.7, f32[2]{0:T(128)} %pad_maximum_fusion.sw_ref, bf16[16,128,128]{2,1,0:T(8,128)(2,1)} %copy-done.1, bf16[4,32,128,128]{3,2,1,0:T(8,128)(2,1)} %blk_ref.7, bf16[4,128,128]{2,1,0:T(8,128)(2,1)} %shard_map.75.cur_ref, ...), custom_call_target="tpu_custom_call" | custom-call | flops 536870912 | bytes 5111808 | tf_op jit(solution)/shard_map/pallas_call | solution.py:62
  120.2 1.5 %gather_fusion.5 = bf16[16,128,128]{2,1,0:T(8,128)(2,1)S(1)} fusion(bf16[4,128,128]{2,1,0:T(8,128)(2,1)} %shard_map.76, s32[1024]{0:T(1024)S(1)} %pad_clamp_fusion.1), kind=kCustom, calls=%fused_computation.4.clone | custom fusion | bytes 1048640 | tf_op jit(solution)/shard_map/jit(_take)/gather | solution.py:98
  121.8 0.9 broadcast_select_fusion
  122.7 3.8 %all-to-all-start.5 = ((bf16[16,128,128]{2,1,0:T(8,128)(2,1)}), bf16[16,128,128]{2,1,0:T(8,128)(2,1)S(1)}, u32[]{:S(2)}, u32[]{:S(2)}) async-start(bf16[16,128,128]{2,1,0:T(8,128)(2,1)} %broadcast_select_fusion), calls=%async_computation.5 | async-start | bytes 1048576 | tf_op jit(solution)/shard_map/all_to_all | solution.py:99
  126.6 13.6 %all-to-all-done.5 = bf16[16,128,128]{2,1,0:T(8,128)(2,1)S(1)} async-done(((bf16[16,128,128]{2,1,0:T(8,128)(2,1)}), bf16[16,128,128]{2,1,0:T(8,128)(2,1)S(1)}, u32[]{:S(2)}, u32[]{:S(2)}) %all-to-all-start.5) | async-done | bytes 524320 | tf_op jit(solution)/shard_map/all_to_all | solution.py:99
  140.2 0.6 gather_fusion
  140.8 0.8 bitcast_select_fusion
  (15 shorter events, 0.6 us)
Async XLA Ops:
  20.4 17.6 %all-to-all-start.1 = ((bf16[16,128,128]{2,1,0:T(8,128)(2,1)}), bf16[16,128,128]{2,1,0:T(8,128)(2,1)S(1)}, u32[]{:S(2)}, u32[]{:S(2)}) async-start(bf16[16,128,128]{2,1,0:T(8,128)(2,1)} %broadcast_select_fusion.1), calls=%async_computation.1 | async-start | bytes 1048576 | tf_op jit(solution)/shard_map/all_to_all | solution.py:91
  37.9 0.8 copy-start
  96.3 17.6 %all-to-all-start.4 = ((bf16[16,128,128]{2,1,0:T(8,128)(2,1)}), bf16[16,128,128]{2,1,0:T(8,128)(2,1)S(1)}, u32[]{:S(2)}, u32[]{:S(2)}) async-start(bf16[16,128,128]{2,1,0:T(8,128)(2,1)} %broadcast_select_fusion.4), calls=%async_computation.4 | async-start | bytes 1048576 | tf_op jit(solution)/shard_map/all_to_all | solution.py:91
  113.9 0.8 copy-start.1
  122.7 17.5 %all-to-all-start.5 = ((bf16[16,128,128]{2,1,0:T(8,128)(2,1)}), bf16[16,128,128]{2,1,0:T(8,128)(2,1)S(1)}, u32[]{:S(2)}, u32[]{:S(2)}) async-start(bf16[16,128,128]{2,1,0:T(8,128)(2,1)} %broadcast_select_fusion), calls=%async_computation.5 | async-start | bytes 1048576 | tf_op jit(solution)/shard_map/all_to_all | solution.py:99

commit v4 on v3

v4 whole, which is shorter than its diff:
```python
import functools

import jax
import jax.numpy as jnp
from jax import lax
from jax.experimental import pallas as pl
from jax.experimental.pallas import tpu as pltpu
from jax.sharding import PartitionSpec as P

STEPS = 4


def requests(index, nrows, local_rows):
    flat = index.reshape(-1)
    hit = (flat // local_rows)[None, :] == jnp.arange(nrows, dtype=flat.dtype)[:, None]
    return jnp.max(jnp.where(hit, (flat % local_rows)[None, :], 0), axis=1)


def step_kernel(first, cols_ref, pick_ref, scl_ref, c_ref, w_ref, recv_ref, blk_ref, cur_ref, *rest):
    if first:
        out_ref, go_ref, rows_ref = rest
    else:
        prev_ref, out_ref, go_ref, rows_ref = rest
    r = pl.program_id(0)
    local_rows, per_row = cols_ref.shape

    def body(k, acc):
        s = cols_ref[r, k] // local_rows
        prod = jnp.dot(blk_ref[0, k], recv_ref[s], preferred_element_type=jnp.float32)
        return acc + scl_ref[r, k] * prod

    acc = lax.fori_loop(
        0, per_row, body, jnp.zeros(out_ref.shape[1:], jnp.float32), unroll=True
    )
    shift = c_ref[0]
    width = w_ref[0]
    cur = cur_ref[0].astype(jnp.float32)
    if first:
        new = (acc - shift * cur) / width
    else:
        new = 2.0 * (acc - shift * cur) / width - prev_ref[0].astype(jnp.float32)
    new = new.astype(out_ref.dtype)
    out_ref[0] = new
    rows_ref[r] = new

    @pl.when(r == local_rows - 1)
    def _():
        def put(e, carry):
            go_ref[e] = rows_ref[pick_ref[e]]
            return carry

        lax.fori_loop(0, go_ref.shape[0], put, 0)


def chebyshev_step(columns, pick, scales, center, half_width, received, blocks, cur, prev):
    local_rows, per_row, orbitals, _ = blocks.shape
    width = cur.shape[2]
    nrows = pick.shape[0]
    first = prev is None
    row_spec = pl.BlockSpec((1, orbitals, width), lambda r, c, p: (r, 0, 0))
    smem = pl.BlockSpec(memory_space=pltpu.SMEM)
    in_specs = [
        smem,
        smem,
        smem,
        pl.BlockSpec(received.shape, lambda r, c, p: (0, 0, 0)),
        pl.BlockSpec((1, per_row, orbitals, orbitals), lambda r, c, p: (r, 0, 0, 0)),
        row_spec,
    ]
    args = [scales, center, half_width, received, blocks, cur]
    if not first:
        in_specs.append(row_spec)
        args.append(prev)
    flops = 2 * local_rows * per_row * orbitals * orbitals * width
    nbytes = blocks.size * 2 + 2 * received.size * 2 + 3 * cur.size * 2
    return pl.pallas_call(
        functools.partial(step_kernel, first),
        out_shape=(
            jax.ShapeDtypeStruct(cur.shape, jnp.bfloat16),
            jax.ShapeDtypeStruct((nrows, orbitals, width), jnp.bfloat16),
        ),
        grid_spec=pltpu.PrefetchScalarGridSpec(
            num_scalar_prefetch=2,
            grid=(local_rows,),
            in_specs=in_specs,
            out_specs=(row_spec, pl.BlockSpec((nrows, orbitals, width), lambda r, c, p: (0, 0, 0))),
            scratch_shapes=[pltpu.VMEM(cur.shape, jnp.bfloat16)],
        ),
        cost_estimate=pl.CostEstimate(flops=flops, bytes_accessed=nbytes, transcendentals=0),
    )(columns, pick, *args)


def on_device(vectors, blocks, scales, columns, owners, center, half_width):
    nrows = lax.axis_size("rows")
    local_rows = blocks.shape[0]
    orbitals = blocks.shape[2]
    group_width = vectors.shape[1]
    asked = jnp.stack(
        [requests(columns, nrows, local_rows), requests(owners, nrows, local_rows)], axis=1
    )
    granted = lax.all_to_all(asked, "rows", split_axis=0, concat_axis=0, tiled=True)
    wanted = granted[:, 0]
    relay_want = granted[:, 1]

    def exchange(outgoing):
        return lax.all_to_all(outgoing, "rows", split_axis=0, concat_axis=0, tiled=True)

    previous = vectors.reshape(local_rows, orbitals, group_width)
    current, outgoing = chebyshev_step(
        columns, wanted, scales, center, half_width,
        exchange(jnp.take(previous, wanted, axis=0)), blocks, previous, None,
    )
    for step in range(1, STEPS):
        pick = relay_want if step == STEPS - 1 else wanted
        upcoming, outgoing = chebyshev_step(
            columns, pick, scales, center, half_width, exchange(outgoing), blocks, current, previous
        )
        previous, current = (current, upcoming)
    arrived = exchange(outgoing)
    placed = jnp.take(arrived, owners // local_rows, axis=0)
    return placed.reshape(local_rows * orbitals, group_width)


def solution(mesh):
    in_specs = (
        P("rows", "vecs"),
        P("rows", None, None, None),
        P("rows", None),
        P("rows", None),
        P("rows"),
        P(),
        P(),
    )
    out_specs = P("rows", "vecs")
    return jax.shard_map(
        on_device, mesh=mesh, in_specs=in_specs, out_specs=out_specs, check_vma=False
    )
```

time: 143 us -> 137 us (0.958)
  blocking collectives: 50.6 us -> 68.7 us
  waiting for transfers between devices: 38.1 us -> 26.4 us
  local copies, waits for them, and re-layouts: 11.5 us -> 3.92 us
  starting transfers between devices: 11.3 us -> 7.41 us
  other arithmetic: 6.67 us -> 3.87 us
  Pallas kernels: 22.1 us -> 23.9 us
    all_to_all x2 -> x3, blocking collectives: 35.2 us -> 53.4 us  [exchange(): lax.all_to_all(outgoing, 'rows', split_axis=0, concat_axis=0, tiled=True)]
    all_to_all x1 -> x0, waiting for transfers between devices: 13.6 us -> none  [on_device(): lax.all_to_all(sending, 'rows', split_axis=0, concat_axis=0, tiled=True)]
    gather x5 -> x1, local copies, waits for them, and re-layouts: 7.75 us -> 1.55 us  [on_device(): jnp.take(previous, wanted, axis=0)]
    all_to_all x1 -> x0, starting transfers between devices: 3.84 us -> none  [on_device(): lax.all_to_all(sending, 'rows', split_axis=0, concat_axis=0, tiled=True)]
    select_n x6 -> x2, other arithmetic: 3.63 us -> 1.49 us  [on_device(): jnp.take(previous, wanted, axis=0)]
    all_to_all x2, waiting for transfers between devices: 24.5 us -> 26.4 us  [exchange(): lax.all_to_all(outgoing, 'rows', split_axis=0, concat_axis=0, tiled=True)]
    pallas_call x4, Pallas kernels: 22.1 us -> 23.9 us  [chebyshev_step(): pl.pallas_call(functools.partial(step_kernel, first), out_shape=(jax.Shap...]
  transfers between devices with their start and end apart: 3 -> 2, of which waited for: 3 -> 2; matrix products, arithmetic and copies ran while one was open for 1% -> 0% of each run, Pallas kernels for 0% -> 0%
where the time goes in v4:
time: 137 us; the launch traced here: 136 us
  blocking collectives  68.7 us (50%)
  waiting for transfers between devices  26.4 us (19%)
  Pallas kernels  23.9 us (17%)
  starting transfers between devices  7.41 us (5%)
  local copies, waits for them, and re-layouts  3.92 us (3%)
  other arithmetic  3.87 us (3%)
    all_to_all x3, blocking collectives, exchange(): lax.all_to_all(outgoing, 'rows', split_axis=0, concat_axis=0, tiled=True)  53.4 us
    all_to_all x2, waiting for transfers between devices, exchange(): lax.all_to_all(outgoing, 'rows', split_axis=0, concat_axis=0, tiled=True)  26.4 us
    pallas_call x4, Pallas kernels, chebyshev_step(): pl.pallas_call(functools.partial(step_kernel, first), out_shape=(jax.Shap...  23.9 us
    all_to_all x1, blocking collectives, on_device(): lax.all_to_all(asked, 'rows', split_axis=0, concat_axis=0, tiled=True)  15.4 us
    all_to_all x2, starting transfers between devices, exchange(): lax.all_to_all(outgoing, 'rows', split_axis=0, concat_axis=0, tiled=True)  7.41 us
  transfers between devices with their start and end apart: 2, of which 2 were waited for; matrix products, arithmetic and copies ran while one was open for 0% of the time, Pallas kernels for 0%

profile of v4, /device:TPU:0, one launch (start us, length us, event | category | flops | bytes accessed | tf_op | source)
XLA Modules:
  0.0 135.6 jit_solution(9290346464649320686)
XLA Ops:
  0.0 0.7 and_select_fusion
  0.7 0.7 compare_and_fusion
  1.3 0.8 reshape.71
  2.1 0.1 select_reduce_fusion.1
  2.2 0.1 select_reduce_fusion
  2.3 0.1 copy.10
  2.4 15.4 %all_to_all.37 = s32[16,1,2]{2,1,0:T(1,128)S(1)} all-to-all(s32[16,1,2]{2,1,0:T(1,128)S(1)} %copy.10), channel_id=1, replica_groups=mesh['rows'=16,'vecs'=2] {'rows'}, dimensions={0} | all-to-all | bytes 256 | tf_op jit(solution)/shard_map/all_to_all | solution.py:101
  17.8 0.1 copy.11
  17.9 0.6 fusion
  18.5 1.6 %gather_fusion = bf16[16,128,128]{2,1,0:T(8,128)(2,1)S(1)} fusion(bf16[4,128,128]{2,1,0:T(8,128)(2,1)} %bitcast.18, s32[1024]{0:T(1024)S(1)} %pad_clamp_fusion.1), kind=kCustom, calls=%fused_computation | custom fusion | bytes 1048640 | tf_op jit(solution)/shard_map/jit(_take)/gather | solution.py:111
  20.0 0.9 broadcast_select_fusion
  20.9 3.6 %all-to-all-start.1 = ((bf16[16,128,128]{2,1,0:T(8,128)(2,1)}), bf16[16,128,128]{2,1,0:T(8,128)(2,1)S(1)}, u32[]{:S(2)}, u32[]{:S(2)}) async-start(bf16[16,128,128]{2,1,0:T(8,128)(2,1)} %broadcast_select_fusion), calls=%async_computation.1 | async-start | bytes 1048576 | tf_op jit(solution)/shard_map/all_to_all | solution.py:106
  25.8 12.7 %all-to-all-done.1.recv_ref = bf16[16,128,128]{2,1,0:T(8,128)(2,1)S(1)} async-done(((bf16[16,128,128]{2,1,0:T(8,128)(2,1)}), bf16[16,128,128]{2,1,0:T(8,128)(2,1)S(1)}, u32[]{:S(2)}, u32[]{:S(2)}) %all-to-all-start.1) | async-done | bytes 524320 | tf_op jit(solution)/shard_map/all_to_all | solution.py:106
  38.5 0.0 copy-start
  38.5 0.8 copy-done
  39.3 6.2 %shard_map.73 = (bf16[4,128,128]{2,1,0:T(8,128)(2,1)}, bf16[16,128,128]{2,1,0:T(8,128)(2,1)}) custom-call(s32[4,32]{1,0:T(4,128)} %cols_ref.7, s32[16]{0:T(128)} %get-tuple-element.22.pick_ref, f32[4,32]{1,0:T(4,128)} %scl_ref.7, f32[1]{0:T(128)S(6)} %copy.12.c_ref, f32[1]{0:T(128)S(6)} %copy.13.w_ref, bf16[16,128,128]{2,1,0:T(8,128)(2,1)} %copy-done, ...), custom_call_target="tpu_custom_call" | custom-call | flops 536870912 | bytes 5636096 | tf_op jit(solution)/shard_map/pallas_call | solution.py:76
  45.5 17.9 %all_to_all.38.recv_ref = bf16[16,128,128]{2,1,0:T(8,128)(2,1)} all-to-all(bf16[16,128,128]{2,1,0:T(8,128)(2,1)} %get-tuple-element.12), channel_id=1, replica_groups=mesh['rows'=16,'vecs'=2] {'rows'}, dimensions={0} | all-to-all | bytes 1048576 | tf_op jit(solution)/shard_map/all_to_all | solution.py:106
  63.3 5.9 %shard_map.74 = (bf16[4,128,128]{2,1,0:T(8,128)(2,1)}, bf16[16,128,128]{2,1,0:T(8,128)(2,1)}) custom-call(s32[4,32]{1,0:T(4,128)} %cols_ref.7, s32[16]{0:T(128)} %get-tuple-element.22.pick_ref, f32[4,32]{1,0:T(4,128)} %scl_ref.7, f32[1]{0:T(128)S(6)} %copy.12.c_ref, f32[1]{0:T(128)S(6)} %copy.13.w_ref, bf16[16,128,128]{2,1,0:T(8,128)(2,1)} %all_to_all.38.recv_ref, ...), custom_call_target="tpu_custom_call" | custom-call | flops 536870912 | bytes 5636096 | tf_op jit(solution)/shard_map/pallas_call | solution.py:76
  69.2 17.7 %all_to_all.39.recv_ref = bf16[16,128,128]{2,1,0:T(8,128)(2,1)} all-to-all(bf16[16,128,128]{2,1,0:T(8,128)(2,1)} %get-tuple-element.14), channel_id=1, replica_groups=mesh['rows'=16,'vecs'=2] {'rows'}, dimensions={0} | all-to-all | bytes 1048576 | tf_op jit(solution)/shard_map/all_to_all | solution.py:106
  87.0 5.9 %shard_map.75 = (bf16[4,128,128]{2,1,0:T(8,128)(2,1)}, bf16[16,128,128]{2,1,0:T(8,128)(2,1)}) custom-call(s32[4,32]{1,0:T(4,128)} %cols_ref.7, s32[16]{0:T(128)} %get-tuple-element.22.pick_ref, f32[4,32]{1,0:T(4,128)} %scl_ref.7, f32[1]{0:T(128)S(6)} %copy.12.c_ref, f32[1]{0:T(128)S(6)} %copy.13.w_ref, bf16[16,128,128]{2,1,0:T(8,128)(2,1)} %all_to_all.39.recv_ref, ...), custom_call_target="tpu_custom_call" | custom-call | flops 536870912 | bytes 5636096 | tf_op jit(solution)/shard_map/pallas_call | solution.py:76
  92.9 17.8 %all_to_all.40.recv_ref = bf16[16,128,128]{2,1,0:T(8,128)(2,1)} all-to-all(bf16[16,128,128]{2,1,0:T(8,128)(2,1)} %get-tuple-element.16), channel_id=1, replica_groups=mesh['rows'=16,'vecs'=2] {'rows'}, dimensions={0} | all-to-all | bytes 1048576 | tf_op jit(solution)/shard_map/all_to_all | solution.py:106
  110.6 5.9 %shard_map.76 = (bf16[4,128,128]{2,1,0:T(8,128)(2,1)}, bf16[16,128,128]{2,1,0:T(8,128)(2,1)}) custom-call(s32[4,32]{1,0:T(4,128)} %cols_ref.7, s32[16]{0:T(128)} %get-tuple-element.23.pick_ref, f32[4,32]{1,0:T(4,128)} %scl_ref.7, f32[1]{0:T(128)S(6)} %copy.12.c_ref, f32[1]{0:T(128)S(6)} %copy.13.w_ref, bf16[16,128,128]{2,1,0:T(8,128)(2,1)} %all_to_all.40.recv_ref, ...), custom_call_target="tpu_custom_call" | custom-call | flops 536870912 | bytes 5636096 | tf_op jit(solution)/shard_map/pallas_call | solution.py:76
  116.5 3.8 %all-to-all-start.5 = ((bf16[16,128,128]{2,1,0:T(8,128)(2,1)}), bf16[16,128,128]{2,1,0:T(8,128)(2,1)S(1)}, u32[]{:S(2)}, u32[]{:S(2)}) async-start(bf16[16,128,128]{2,1,0:T(8,128)(2,1)} %get-tuple-element.18), calls=%async_computation.5 | async-start | bytes 1048576 | tf_op jit(solution)/shard_map/all_to_all | solution.py:106
  120.4 0.1 broadcast_bitcast_fusion
  120.5 13.7 %all-to-all-done.5 = bf16[16,128,128]{2,1,0:T(8,128)(2,1)S(1)} async-done(((bf16[16,128,128]{2,1,0:T(8,128)(2,1)}), bf16[16,128,128]{2,1,0:T(8,128)(2,1)S(1)}, u32[]{:S(2)}, u32[]{:S(2)}) %all-to-all-start.5) | async-done | bytes 524320 | tf_op jit(solution)/shard_map/all_to_all | solution.py:106
  134.2 0.6 gather_fusion.1
  134.8 0.8 bitcast_select_fusion
  (6 shorter events, 0.0 us)
Async XLA Ops:
  20.9 17.6 %all-to-all-start.1 = ((bf16[16,128,128]{2,1,0:T(8,128)(2,1)}), bf16[16,128,128]{2,1,0:T(8,128)(2,1)S(1)}, u32[]{:S(2)}, u32[]{:S(2)}) async-start(bf16[16,128,128]{2,1,0:T(8,128)(2,1)} %broadcast_select_fusion), calls=%async_computation.1 | async-start | bytes 1048576 | tf_op jit(solution)/shard_map/all_to_all | solution.py:106
  38.5 0.8 copy-start
  116.5 17.7 %all-to-all-start.5 = ((bf16[16,128,128]{2,1,0:T(8,128)(2,1)}), bf16[16,128,128]{2,1,0:T(8,128)(2,1)S(1)}, u32[]{:S(2)}, u32[]{:S(2)}) async-start(bf16[16,128,128]{2,1,0:T(8,128)(2,1)} %get-tuple-element.18), calls=%async_computation.5 | async-start | bytes 1048576 | tf_op jit(solution)/shard_map/all_to_all | solution.py:106

commit v5 on v4

--- a/solution.py
+++ b/solution.py
@@ -16,22 +16,23 @@
     return jnp.max(jnp.where(hit, (flat % local_rows)[None, :], 0), axis=1)
 
 
-def step_kernel(first, cols_ref, pick_ref, scl_ref, c_ref, w_ref, recv_ref, blk_ref, cur_ref, *rest):
+def step_kernel(first, cols_ref, pick_ref, c_ref, w_ref, recv_ref, blk_ref, cur_ref, *rest):
     if first:
-        out_ref, go_ref, rows_ref = rest
+        out_ref, go_ref, rows_ref, stack_ref = rest
     else:
-        prev_ref, out_ref, go_ref, rows_ref = rest
+        prev_ref, out_ref, go_ref, rows_ref, stack_ref = rest
     r = pl.program_id(0)
     local_rows, per_row = cols_ref.shape
+    orbitals = recv_ref.shape[1]
 
-    def body(k, acc):
-        s = cols_ref[r, k] // local_rows
-        prod = jnp.dot(blk_ref[0, k], recv_ref[s], preferred_element_type=jnp.float32)
-        return acc + scl_ref[r, k] * prod
+    def fill(k, carry):
+        start = pl.multiple_of(k * orbitals, orbitals)
+        stack_ref[pl.ds(start, orbitals), :] = recv_ref[cols_ref[r, k] // local_rows]
+        return carry
 
-    acc = lax.fori_loop(
-        0, per_row, body, jnp.zeros(out_ref.shape[1:], jnp.float32), unroll=True
-    )
+    lax.fori_loop(0, per_row, fill, 0, unroll=True)
+    both = jnp.dot(blk_ref[0], stack_ref[...], preferred_element_type=jnp.float32)
+    acc = both[:orbitals] + both[orbitals:]
     shift = c_ref[0]
     width = w_ref[0]
     cur = cur_ref[0].astype(jnp.float32)
@@ -52,8 +53,9 @@
         lax.fori_loop(0, go_ref.shape[0], put, 0)
 
 
-def chebyshev_step(columns, pick, scales, center, half_width, received, blocks, cur, prev):
-    local_rows, per_row, orbitals, _ = blocks.shape
+def chebyshev_step(columns, pick, center, half_width, received, matrix, cur, prev):
+    local_rows, parts, depth = matrix.shape
+    orbitals = cur.shape[1]
     width = cur.shape[2]
     nrows = pick.shape[0]
     first = prev is None
@@ -62,17 +64,16 @@
     in_specs = [
         smem,
         smem,
-        smem,
         pl.BlockSpec(received.shape, lambda r, c, p: (0, 0, 0)),
-        pl.BlockSpec((1, per_row, orbitals, orbitals), lambda r, c, p: (r, 0, 0, 0)),
+        pl.BlockSpec((1, parts, depth), lambda r, c, p: (r, 0, 0)),
         row_spec,
     ]
-    args = [scales, center, half_width, received, blocks, cur]
+    args = [center, half_width, received, matrix, cur]
     if not first:
         in_specs.append(row_spec)
         args.append(prev)
-    flops = 2 * local_rows * per_row * orbitals * orbitals * width
-    nbytes = blocks.size * 2 + 2 * received.size * 2 + 3 * cur.size * 2
+    flops = 2 * local_rows * parts * depth * width
+    nbytes = matrix.size * 2 + 2 * received.size * 2 + 3 * cur.size * 2
     return pl.pallas_call(
         functools.partial(step_kernel, first),
         out_shape=(
@@ -84,7 +85,10 @@
             grid=(local_rows,),
             in_specs=in_specs,
             out_specs=(row_spec, pl.BlockSpec((nrows, orbitals, width), lambda r, c, p: (0, 0, 0))),
-            scratch_shapes=[pltpu.VMEM(cur.shape, jnp.bfloat16)],
+            scratch_shapes=[
+                pltpu.VMEM(cur.shape, jnp.bfloat16),
+                pltpu.VMEM((depth, width), jnp.bfloat16),
+            ],
         ),
         cost_estimate=pl.CostEstimate(flops=flops, bytes_accessed=nbytes, transcendentals=0),
     )(columns, pick, *args)
@@ -105,15 +109,24 @@
     def exchange(outgoing):
         return lax.all_to_all(outgoing, "rows", split_axis=0, concat_axis=0, tiled=True)
 
+    per_row = blocks.shape[1]
+    entries = blocks.astype(jnp.float32) * scales[:, :, None, None]
+    high = lax.reduce_precision(entries, exponent_bits=8, mantissa_bits=7)
+    low = entries - high
+    matrix = (
+        jnp.stack([high.astype(jnp.bfloat16), low.astype(jnp.bfloat16)], axis=1)
+        .transpose(0, 1, 3, 2, 4)
+        .reshape(local_rows, 2 * orbitals, per_row * orbitals)
+    )
     previous = vectors.reshape(local_rows, orbitals, group_width)
     current, outgoing = chebyshev_step(
-        columns, wanted, scales, center, half_width,
-        exchange(jnp.take(previous, wanted, axis=0)), blocks, previous, None,
+        columns, wanted, center, half_width,
+        exchange(jnp.take(previous, wanted, axis=0)), matrix, previous, None,
     )
     for step in range(1, STEPS):
         pick = relay_want if step == STEPS - 1 else wanted
         upcoming, outgoing = chebyshev_step(
-            columns, pick, scales, center, half_width, exchange(outgoing), blocks, current, previous
+            columns, pick, center, half_width, exchange(outgoing), matrix, current, previous
         )
         previous, current = (current, upcoming)
     arrived = exchange(outgoing)

time: 137 us -> 170 us (1.24)
  local copies, waits for them, and re-layouts: 3.92 us -> 29.3 us
  waiting for transfers between devices: 26.4 us -> 13.7 us
  other arithmetic: 3.87 us -> 15.5 us
  Pallas kernels: 23.9 us -> 29.8 us
  blocking collectives: 68.7 us -> 71.3 us
    reshape x0 -> x1, local copies, waits for them, and re-layouts: none -> 13.3 us  [on_device(): matrix = jnp.stack([high.astype(jnp.bfloat16), low.astype(jnp.bfloat16)],...]
    all_to_all x2, waiting for transfers between devices: 26.4 us -> 13.7 us  [exchange(): lax.all_to_all(outgoing, 'rows', split_axis=0, concat_axis=0, tiled=True)]
    transpose x0 -> x1, local copies, waits for them, and re-layouts: none -> 12 us  [on_device(): matrix = jnp.stack([high.astype(jnp.bfloat16), low.astype(jnp.bfloat16)],...]
    transpose x0 -> x1, other arithmetic: none -> 6.19 us  [on_device(): matrix = jnp.stack([high.astype(jnp.bfloat16), low.astype(jnp.bfloat16)],...]
    pallas_call x4, Pallas kernels: 23.9 us -> 29.8 us  [chebyshev_step(): pl.pallas_call(functools.partial(step_kernel, first), out_shape=(jax.Shap...]
    another operation x0 -> x1, other arithmetic: none -> 5.46 us  [on_device(): jnp.stack([high.astype(jnp.bfloat16), low.astype(jnp.bfloat16)], axis=1)]
    all_to_all x3, blocking collectives: 53.4 us -> 55.9 us  [exchange(): lax.all_to_all(outgoing, 'rows', split_axis=0, concat_axis=0, tiled=True)]
  transfers between devices with their start and end apart: 2 -> 2, of which waited for: 2 -> 1; matrix products, arithmetic and copies ran while one was open for 0% -> 22% of each run, Pallas kernels for 0% -> 0%
where the time goes in v5:
time: 170 us; the launch traced here: 168 us
  blocking collectives  71.3 us (42%)
  Pallas kernels  29.8 us (18%)
  local copies, waits for them, and re-layouts  29.3 us (17%)
  other arithmetic  15.5 us (9%)
  waiting for transfers between devices  13.7 us (8%)
  starting transfers between devices  7.42 us (4%)
    all_to_all x3, blocking collectives, exchange(): lax.all_to_all(outgoing, 'rows', split_axis=0, concat_axis=0, tiled=True)  55.9 us
    pallas_call x4, Pallas kernels, chebyshev_step(): pl.pallas_call(functools.partial(step_kernel, first), out_shape=(jax.Shap...  29.8 us
    all_to_all x1, blocking collectives, on_device(): lax.all_to_all(asked, 'rows', split_axis=0, concat_axis=0, tiled=True)  15.4 us
    all_to_all x2, waiting for transfers between devices, exchange(): lax.all_to_all(outgoing, 'rows', split_axis=0, concat_axis=0, tiled=True)  13.7 us
    reshape x1, local copies, waits for them, and re-layouts, on_device(): matrix = jnp.stack([high.astype(jnp.bfloat16), low.astype(jnp.bfloat16)],...  13.3 us
    transpose x1, local copies, waits for them, and re-layouts, on_device(): matrix = jnp.stack([high.astype(jnp.bfloat16), low.astype(jnp.bfloat16)],...  12 us
    all_to_all x2, starting transfers between devices, exchange(): lax.all_to_all(outgoing, 'rows', split_axis=0, concat_axis=0, tiled=True)  7.42 us
    transpose x1, other arithmetic, on_device(): matrix = jnp.stack([high.astype(jnp.bfloat16), low.astype(jnp.bfloat16)],...  6.19 us
  transfers between devices with their start and end apart: 2, of which 1 were waited for; matrix products, arithmetic and copies ran while one was open for 22% of the time, Pallas kernels for 0%

profile of v5, /device:TPU:0, one launch (start us, length us, event | category | flops | bytes accessed | tf_op | source)
XLA Modules:
  0.0 168.4 jit_solution(1161073059442738649)
XLA Ops:
  0.0 0.7 compare_and_fusion
  0.7 0.7 and_select_fusion
  1.3 0.8 reshape.75
  2.1 0.1 select_reduce_fusion
  2.2 0.1 select_reduce_fusion.1
  2.3 0.1 copy.12
  2.4 15.4 %all_to_all.37 = s32[16,1,2]{2,1,0:T(1,128)S(1)} all-to-all(s32[16,1,2]{2,1,0:T(1,128)S(1)} %copy.12), channel_id=1, replica_groups=mesh['rows'=16,'vecs'=2] {'rows'}, dimensions={0} | all-to-all | bytes 256 | tf_op jit(solution)/shard_map/all_to_all | solution.py:105
  17.8 0.1 copy.13
  17.9 0.6 fusion.3
  18.5 1.6 gather_fusion
  20.0 0.9 broadcast_select_fusion
  20.9 3.6 %all-to-all-start.1 = ((bf16[16,128,128]{2,1,0:T(8,128)(2,1)}), bf16[16,128,128]{2,1,0:T(8,128)(2,1)S(1)}, u32[]{:S(2)}, u32[]{:S(2)}) async-start(bf16[16,128,128]{2,1,0:T(8,128)(2,1)} %broadcast_select_fusion), calls=%async_computation.1 | async-start | bytes 1048576 | tf_op jit(solution)/shard_map/all_to_all | solution.py:110
  24.5 5.5 %fusion.2 = (bf16[4,1,32,128,128]{4,3,2,0,1:T(8,128)(2,1)S(1)}, bf16[4,1,32,128,128]{4,3,2,0,1:T(8,128)(2,1)}) fusion(bf16[4,32,128,128]{3,2,1,0:T(8,128)(2,1)} %param.8, f32[4,32]{1,0:T(4,128)} %param.9), kind=kLoop, calls=%fused_computation.8 | loop fusion | flops 12582912 | bytes 12583424 | tf_op jit(solution)/shard_map/stack | solution.py:117
  30.0 6.2 %maximum_bitcast_fusion = bf16[4,2,128,32,128]{4,2,3,0,1:T(8,128)(2,1)} fusion(bf16[4,1,32,128,128]{4,3,2,0,1:T(8,128)(2,1)} %get-tuple-element.22, bf16[4,1,32,128,128]{4,3,2,0,1:T(8,128)(2,1)S(1)} %get-tuple-element.21), kind=kLoop, calls=%fused_computation.5 | loop fusion | flops 4194304 | bytes 16777216 | tf_op jit(solution)/shard_map/transpose | solution.py:118
  36.2 12.0 %copy.14 = bf16[4,2,128,32,128]{4,3,2,1,0:T(8,128)(2,1)} copy(bf16[4,2,128,32,128]{4,2,3,0,1:T(8,128)(2,1)} %maximum_bitcast_fusion) | data formatting | bytes 16777216 | tf_op jit(solution)/shard_map/transpose | solution.py:118
  48.2 13.3 %reshape.77.blk_ref = bf16[4,256,4096]{2,1,0:T(8,128)(2,1)} reshape(bf16[4,2,128,32,128]{4,3,2,1,0:T(8,128)(2,1)} %copy.14) | data formatting | bytes 16777216 | tf_op jit(solution)/shard_map/reshape | solution.py:119
  62.8 0.0 all-to-all-done.1.recv_ref
  62.8 0.0 copy-start
  62.8 0.8 copy-done
  63.7 7.4 %shard_map.73 = (bf16[4,128,128]{2,1,0:T(8,128)(2,1)}, bf16[16,128,128]{2,1,0:T(8,128)(2,1)}) custom-call(s32[4,32]{1,0:T(4,128)} %cols_ref.7, s32[16]{0:T(128)} %get-tuple-element.24.pick_ref, f32[1]{0:T(128)S(6)} %copy.15.c_ref, f32[1]{0:T(128)S(6)} %copy.16.w_ref, bf16[16,128,128]{2,1,0:T(8,128)(2,1)} %copy-done, bf16[4,256,4096]{2,1,0:T(8,128)(2,1)} %reshape.77.blk_ref, ...), custom_call_target="tpu_custom_call" | custom-call | flops 1073741824 | bytes 9830400 | tf_op jit(solution)/shard_map/pallas_call | solution.py:77
  71.1 20.5 %all_to_all.38.recv_ref = bf16[16,128,128]{2,1,0:T(8,128)(2,1)} all-to-all(bf16[16,128,128]{2,1,0:T(8,128)(2,1)} %get-tuple-element.12), channel_id=1, replica_groups=mesh['rows'=16,'vecs'=2] {'rows'}, dimensions={0} | all-to-all | bytes 1048576 | tf_op jit(solution)/shard_map/all_to_all | solution.py:110
  91.5 7.5 %shard_map.74 = (bf16[4,128,128]{2,1,0:T(8,128)(2,1)}, bf16[16,128,128]{2,1,0:T(8,128)(2,1)}) custom-call(s32[4,32]{1,0:T(4,128)} %cols_ref.7, s32[16]{0:T(128)} %get-tuple-element.24.pick_ref, f32[1]{0:T(128)S(6)} %copy.15.c_ref, f32[1]{0:T(128)S(6)} %copy.16.w_ref, bf16[16,128,128]{2,1,0:T(8,128)(2,1)} %all_to_all.38.recv_ref, ...), custom_call_target="tpu_custom_call" | custom-call | flops 1073741824 | bytes 9830400 | tf_op jit(solution)/shard_map/pallas_call | solution.py:77
  99.0 17.7 %all_to_all.39.recv_ref = bf16[16,128,128]{2,1,0:T(8,128)(2,1)} all-to-all(bf16[16,128,128]{2,1,0:T(8,128)(2,1)} %get-tuple-element.14), channel_id=1, replica_groups=mesh['rows'=16,'vecs'=2] {'rows'}, dimensions={0} | all-to-all | bytes 1048576 | tf_op jit(solution)/shard_map/all_to_all | solution.py:110
  116.7 7.5 %shard_map.75 = (bf16[4,128,128]{2,1,0:T(8,128)(2,1)}, bf16[16,128,128]{2,1,0:T(8,128)(2,1)}) custom-call(s32[4,32]{1,0:T(4,128)} %cols_ref.7, s32[16]{0:T(128)} %get-tuple-element.24.pick_ref, f32[1]{0:T(128)S(6)} %copy.15.c_ref, f32[1]{0:T(128)S(6)} %copy.16.w_ref, bf16[16,128,128]{2,1,0:T(8,128)(2,1)} %all_to_all.39.recv_ref, ...), custom_call_target="tpu_custom_call" | custom-call | flops 1073741824 | bytes 9830400 | tf_op jit(solution)/shard_map/pallas_call | solution.py:77
  124.1 17.8 %all_to_all.40.recv_ref = bf16[16,128,128]{2,1,0:T(8,128)(2,1)} all-to-all(bf16[16,128,128]{2,1,0:T(8,128)(2,1)} %get-tuple-element.16), channel_id=1, replica_groups=mesh['rows'=16,'vecs'=2] {'rows'}, dimensions={0} | all-to-all | bytes 1048576 | tf_op jit(solution)/shard_map/all_to_all | solution.py:110
  141.9 7.5 %shard_map.76 = (bf16[4,128,128]{2,1,0:T(8,128)(2,1)}, bf16[16,128,128]{2,1,0:T(8,128)(2,1)}) custom-call(s32[4,32]{1,0:T(4,128)} %cols_ref.7, s32[16]{0:T(128)} %get-tuple-element.25.pick_ref, f32[1]{0:T(128)S(6)} %copy.15.c_ref, f32[1]{0:T(128)S(6)} %copy.16.w_ref, bf16[16,128,128]{2,1,0:T(8,128)(2,1)} %all_to_all.40.recv_ref, ...), custom_call_target="tpu_custom_call" | custom-call | flops 1073741824 | bytes 9830400 | tf_op jit(solution)/shard_map/pallas_call | solution.py:77
  149.3 3.8 %all-to-all-start.5 = ((bf16[16,128,128]{2,1,0:T(8,128)(2,1)}), bf16[16,128,128]{2,1,0:T(8,128)(2,1)S(1)}, u32[]{:S(2)}, u32[]{:S(2)}) async-start(bf16[16,128,128]{2,1,0:T(8,128)(2,1)} %get-tuple-element.18), calls=%async_computation.5 | async-start | bytes 1048576 | tf_op jit(solution)/shard_map/all_to_all | solution.py:110
  153.2 0.1 broadcast_bitcast_fusion
  153.3 13.7 %all-to-all-done.5 = bf16[16,128,128]{2,1,0:T(8,128)(2,1)S(1)} async-done(((bf16[16,128,128]{2,1,0:T(8,128)(2,1)}), bf16[16,128,128]{2,1,0:T(8,128)(2,1)S(1)}, u32[]{:S(2)}, u32[]{:S(2)}) %all-to-all-start.5) | async-done | bytes 524320 | tf_op jit(solution)/shard_map/all_to_all | solution.py:110
  167.0 0.6 gather_fusion.1
  167.6 0.8 bitcast_select_fusion
  (6 shorter events, 0.0 us)
Async XLA Ops:
  20.9 41.9 %all-to-all-start.1 = ((bf16[16,128,128]{2,1,0:T(8,128)(2,1)}), bf16[16,128,128]{2,1,0:T(8,128)(2,1)S(1)}, u32[]{:S(2)}, u32[]{:S(2)}) async-start(bf16[16,128,128]{2,1,0:T(8,128)(2,1)} %broadcast_select_fusion), calls=%async_computation.1 | async-start | bytes 1048576 | tf_op jit(solution)/shard_map/all_to_all | solution.py:110
  62.8 0.8 copy-start
  149.3 17.7 %all-to-all-start.5 = ((bf16[16,128,128]{2,1,0:T(8,128)(2,1)}), bf16[16,128,128]{2,1,0:T(8,128)(2,1)S(1)}, u32[]{:S(2)}, u32[]{:S(2)}) async-start(bf16[16,128,128]{2,1,0:T(8,128)(2,1)} %get-tuple-element.18), calls=%async_computation.5 | async-start | bytes 1048576 | tf_op jit(solution)/shard_map/all_to_all | solution.py:110

commit v6 on v4

--- a/solution.py
+++ b/solution.py
@@ -10,13 +10,63 @@
 STEPS = 4
 
 
-def requests(index, nrows, local_rows):
-    flat = index.reshape(-1)
-    hit = (flat // local_rows)[None, :] == jnp.arange(nrows, dtype=flat.dtype)[:, None]
-    return jnp.max(jnp.where(hit, (flat % local_rows)[None, :], 0), axis=1)
+def requests_kernel(cols_ref, own_ref, out_ref):
+    local_rows, per_row = cols_ref.shape
+
+    def clear(e, carry):
+        out_ref[e, 0] = 0
+        out_ref[e, 1] = 0
+        return carry
+
+    lax.fori_loop(0, out_ref.shape[0], clear, 0)
+
+    def read(i, carry):
+        c = cols_ref[i // per_row, i % per_row]
+        out_ref[c // local_rows, 0] = c % local_rows
+        return carry
+
+    lax.fori_loop(0, local_rows * per_row, read, 0)
+
+    def place(i, carry):
+        o = own_ref[i]
+        out_ref[o // local_rows, 1] = o % local_rows
+        return carry
+
+    lax.fori_loop(0, own_ref.shape[0], place, 0)
 
 
-def step_kernel(first, cols_ref, pick_ref, scl_ref, c_ref, w_ref, recv_ref, blk_ref, cur_ref, *rest):
+def requests(columns, owners, nrows):
+    smem = pl.BlockSpec(memory_space=pltpu.SMEM)
+    return pl.pallas_call(
+        requests_kernel,
+        out_shape=jax.ShapeDtypeStruct((nrows, 2), jnp.int32),
+        in_specs=[smem, smem],
+        out_specs=smem,
+    )(columns, owners)
+
+
+def pick_kernel(which, table_ref, src_ref, out_ref):
+    def put(e, carry):
+        out_ref[e] = src_ref[table_ref[e, which]]
+        return carry
+
+    lax.fori_loop(0, out_ref.shape[0], put, 0)
+
+
+def pick_rows(table, which, source, count):
+    return pl.pallas_call(
+        functools.partial(pick_kernel, which),
+        out_shape=jax.ShapeDtypeStruct((count,) + source.shape[1:], source.dtype),
+        grid_spec=pltpu.PrefetchScalarGridSpec(
+            num_scalar_prefetch=1,
+            grid=(1,),
+            in_specs=[pl.BlockSpec(source.shape, lambda i, t: (0, 0, 0))],
+            out_specs=pl.BlockSpec((count,) + source.shape[1:], lambda i, t: (0, 0, 0)),
+        ),
+    )(table, source)
+
+
+def step_kernel(first, which, cols_ref, pick_ref, scl_ref, c_ref, w_ref, recv_ref, blk_ref, cur_ref, *rest):
     if first:
         out_ref, go_ref, rows_ref = rest
     else:
@@ -46,13 +96,13 @@
     @pl.when(r == local_rows - 1)
     def _():
         def put(e, carry):
-            go_ref[e] = rows_ref[pick_ref[e]]
+            go_ref[e] = rows_ref[pick_ref[e, which]]
             return carry
 
         lax.fori_loop(0, go_ref.shape[0], put, 0)
 
 
-def chebyshev_step(columns, pick, scales, center, half_width, received, blocks, cur, prev):
+def chebyshev_step(columns, pick, which, scales, center, half_width, received, blocks, cur, prev):
     local_rows, per_row, orbitals, _ = blocks.shape
     width = cur.shape[2]
     nrows = pick.shape[0]
@@ -74,7 +124,7 @@
     flops = 2 * local_rows * per_row * orbitals * orbitals * width
     nbytes = blocks.size * 2 + 2 * received.size * 2 + 3 * cur.size * 2
     return pl.pallas_call(
-        functools.partial(step_kernel, first),
+        functools.partial(step_kernel, first, which),
         out_shape=(
             jax.ShapeDtypeStruct(cur.shape, jnp.bfloat16),
             jax.ShapeDtypeStruct((nrows, orbitals, width), jnp.bfloat16),
@@ -95,29 +145,27 @@
     local_rows = blocks.shape[0]
     orbitals = blocks.shape[2]
     group_width = vectors.shape[1]
-    asked = jnp.stack(
-        [requests(columns, nrows, local_rows), requests(owners, nrows, local_rows)], axis=1
-    )
+    asked = requests(columns, owners, nrows)
     granted = lax.all_to_all(asked, "rows", split_axis=0, concat_axis=0, tiled=True)
-    wanted = granted[:, 0]
-    relay_want = granted[:, 1]
 
     def exchange(outgoing):
         return lax.all_to_all(outgoing, "rows", split_axis=0, concat_axis=0, tiled=True)
 
     previous = vectors.reshape(local_rows, orbitals, group_width)
     current, outgoing = chebyshev_step(
-        columns, wanted, scales, center, half_width,
-        exchange(jnp.take(previous, wanted, axis=0)), blocks, previous, None,
+        columns, granted, 0, scales, center, half_width,
+        exchange(pick_rows(granted, 0, previous, nrows)), blocks, previous, None,
     )
     for step in range(1, STEPS):
-        pick = relay_want if step == STEPS - 1 else wanted
+        which = 1 if step == STEPS - 1 else 0
         upcoming, outgoing = chebyshev_step(
-            columns, pick, scales, center, half_width, exchange(outgoing), blocks, current, previous
+            columns, granted, which, scales, center, half_width, exchange(outgoing), blocks, current, previous
         )
         previous, current = (current, upcoming)
     arrived = exchange(outgoing)
-    placed = jnp.take(arrived, owners // local_rows, axis=0)
+    placed = pick_rows(
+        jnp.stack([owners // local_rows, owners], axis=1), 0, arrived, local_rows
+    )
     return placed.reshape(local_rows * orbitals, group_width)
 
 

time: 137 us -> 141 us (1.029)
  Pallas kernels: 23.9 us -> 33.3 us
  other arithmetic: 3.87 us -> 0.67 us
  local copies, waits for them, and re-layouts: 3.92 us -> 1.77 us
    pallas_call x4 -> x7, Pallas kernels: 23.9 us -> 33.3 us  [the longest x4 24.4 us: chebyshev_step(): pl.pallas_call(functools.partial(step_kernel, first, which), out_shape=(j...]
    select_n x6 -> x0, other arithmetic: 2.97 us -> none  [the longest x2 1.49 us: on_device(): jnp.take(previous, wanted, axis=0)]
    gather x2 -> x0, local copies, waits for them, and re-layouts: 2.12 us -> none  [the longest x1 1.55 us: on_device(): jnp.take(previous, wanted, axis=0)]
  transfers between devices with their start and end apart: 2 -> 2, of which waited for: 2 -> 2; matrix products, arithmetic and copies ran while one was open for 0% -> 1% of each run, Pallas kernels for 0% -> 0%
where the time goes in v6:
time: 141 us; the launch traced here: 139 us
  blocking collectives  68.9 us (49%)
  Pallas kernels  33.3 us (24%)
  waiting for transfers between devices  25.8 us (18%)
  starting transfers between devices  7.42 us (5%)
  local copies, waits for them, and re-layouts  1.77 us (1%)
    all_to_all x3, blocking collectives, exchange(): lax.all_to_all(outgoing, 'rows', split_axis=0, concat_axis=0, tiled=True)  53.5 us
    all_to_all x2, waiting for transfers between devices, exchange(): lax.all_to_all(outgoing, 'rows', split_axis=0, concat_axis=0, tiled=True)  25.8 us
    pallas_call x4, Pallas kernels, chebyshev_step(): pl.pallas_call(functools.partial(step_kernel, first, which), out_shape=(j...  24.4 us
    all_to_all x1, blocking collectives, on_device(): lax.all_to_all(asked, 'rows', split_axis=0, concat_axis=0, tiled=True)  15.5 us
    all_to_all x2, starting transfers between devices, exchange(): lax.all_to_all(outgoing, 'rows', split_axis=0, concat_axis=0, tiled=True)  7.42 us
    pallas_call x2, Pallas kernels, pick_rows(): pl.pallas_call(functools.partial(pick_kernel, which), out_shape=jax.Shape...  4.97 us
    pallas_call x1, Pallas kernels, requests(): pl.pallas_call(requests_kernel, out_shape=jax.ShapeDtypeStruct((nrows, 2)...  3.92 us
  transfers between devices with their start and end apart: 2, of which 2 were waited for; matrix products, arithmetic and copies ran while one was open for 1% of the time, Pallas kernels for 0%

profile of v6, /device:TPU:0, one launch (start us, length us, event | category | flops | bytes accessed | tf_op | source)
XLA Modules:
  0.0 139.2 jit_solution(3247328015389744874)
XLA Ops:
  0.0 3.9 %shard_map.73 = s32[16,2]{1,0:T(8,128)} custom-call(s32[4,32]{1,0:T(4,128)} %cols_ref.9, s32[4]{0:T(128)} %own_ref.1), custom_call_target="tpu_custom_call" | custom-call | tf_op jit(solution)/shard_map/pallas_call | solution.py:40
  3.9 15.5 %all_to_all.36 = s32[16,1,2]{2,1,0:T(1,128)} all-to-all(s32[16,1,2]{2,1,0:T(1,128)} %bitcast.17), channel_id=1, replica_groups=mesh['rows'=16,'vecs'=2] {'rows'}, dimensions={0} | all-to-all | bytes 256 | tf_op jit(solution)/shard_map/all_to_all | solution.py:149
  19.4 2.6 %shard_map.74 = bf16[16,128,128]{2,1,0:T(8,128)(2,1)} custom-call(s32[16,2]{1,0:T(8,128)} %bitcast.12, bf16[4,128,128]{2,1,0:T(8,128)(2,1)} %bitcast.9), custom_call_target="tpu_custom_call" | custom-call | tf_op jit(solution)/shard_map/pallas_call | solution.py:57
  22.0 3.6 %all-to-all-start.1 = ((bf16[16,128,128]{2,1,0:T(8,128)(2,1)}), bf16[16,128,128]{2,1,0:T(8,128)(2,1)S(1)}, u32[]{:S(2)}, u32[]{:S(2)}) async-start(bf16[16,128,128]{2,1,0:T(8,128)(2,1)} %shard_map.74), calls=%async_computation.1 | async-start | bytes 1048576 | tf_op jit(solution)/shard_map/all_to_all | solution.py:152
  26.9 12.8 %all-to-all-done.1.recv_ref = bf16[16,128,128]{2,1,0:T(8,128)(2,1)S(1)} async-done(((bf16[16,128,128]{2,1,0:T(8,128)(2,1)}), bf16[16,128,128]{2,1,0:T(8,128)(2,1)S(1)}, u32[]{:S(2)}, u32[]{:S(2)}) %all-to-all-start.1) | async-done | bytes 524320 | tf_op jit(solution)/shard_map/all_to_all | solution.py:152
  39.7 0.0 copy-start
  39.7 0.8 copy-done
  40.5 6.3 %shard_map.75 = (bf16[4,128,128]{2,1,0:T(8,128)(2,1)}, bf16[16,128,128]{2,1,0:T(8,128)(2,1)}) custom-call(s32[4,32]{1,0:T(4,128)} %cols_ref.9, s32[16,2]{1,0:T(8,128)} %bitcast.13, f32[4,32]{1,0:T(4,128)} %scl_ref.7, f32[1]{0:T(128)S(6)} %copy.29.c_ref, f32[1]{0:T(128)S(6)} %copy.30.w_ref, bf16[16,128,128]{2,1,0:T(8,128)(2,1)} %copy-done, ...), custom_call_target="tpu_custom_call" | custom-call | flops 536870912 | bytes 5636096 | tf_op jit(solution)/shard_map/pallas_call | solution.py:126
  46.8 18.0 %all_to_all.37.recv_ref = bf16[16,128,128]{2,1,0:T(8,128)(2,1)} all-to-all(bf16[16,128,128]{2,1,0:T(8,128)(2,1)} %get-tuple-element.12), channel_id=1, replica_groups=mesh['rows'=16,'vecs'=2] {'rows'}, dimensions={0} | all-to-all | bytes 1048576 | tf_op jit(solution)/shard_map/all_to_all | solution.py:152
  64.8 6.0 %shard_map.76 = (bf16[4,128,128]{2,1,0:T(8,128)(2,1)}, bf16[16,128,128]{2,1,0:T(8,128)(2,1)}) custom-call(s32[4,32]{1,0:T(4,128)} %cols_ref.9, s32[16,2]{1,0:T(8,128)} %bitcast.14, f32[4,32]{1,0:T(4,128)} %scl_ref.7, f32[1]{0:T(128)S(6)} %copy.29.c_ref, f32[1]{0:T(128)S(6)} %copy.30.w_ref, bf16[16,128,128]{2,1,0:T(8,128)(2,1)} %all_to_all.37.recv_ref, ...), custom_call_target="tpu_custom_call" | custom-call | flops 536870912 | bytes 5636096 | tf_op jit(solution)/shard_map/pallas_call | solution.py:126
  70.8 17.7 %all_to_all.38.recv_ref = bf16[16,128,128]{2,1,0:T(8,128)(2,1)} all-to-all(bf16[16,128,128]{2,1,0:T(8,128)(2,1)} %get-tuple-element.14), channel_id=1, replica_groups=mesh['rows'=16,'vecs'=2] {'rows'}, dimensions={0} | all-to-all | bytes 1048576 | tf_op jit(solution)/shard_map/all_to_all | solution.py:152
  88.5 6.0 %shard_map.77 = (bf16[4,128,128]{2,1,0:T(8,128)(2,1)}, bf16[16,128,128]{2,1,0:T(8,128)(2,1)}) custom-call(s32[4,32]{1,0:T(4,128)} %cols_ref.9, s32[16,2]{1,0:T(8,128)} %bitcast.15, f32[4,32]{1,0:T(4,128)} %scl_ref.7, f32[1]{0:T(128)S(6)} %copy.29.c_ref, f32[1]{0:T(128)S(6)} %copy.30.w_ref, bf16[16,128,128]{2,1,0:T(8,128)(2,1)} %all_to_all.38.recv_ref, ...), custom_call_target="tpu_custom_call" | custom-call | flops 536870912 | bytes 5636096 | tf_op jit(solution)/shard_map/pallas_call | solution.py:126
  94.5 0.0 copy-start.2
  94.6 17.8 %all_to_all.39.recv_ref = bf16[16,128,128]{2,1,0:T(8,128)(2,1)} all-to-all(bf16[16,128,128]{2,1,0:T(8,128)(2,1)} %get-tuple-element.16), channel_id=1, replica_groups=mesh['rows'=16,'vecs'=2] {'rows'}, dimensions={0} | all-to-all | bytes 1048576 | tf_op jit(solution)/shard_map/all_to_all | solution.py:152
  112.3 6.0 %shard_map.78 = (bf16[4,128,128]{2,1,0:T(8,128)(2,1)}, bf16[16,128,128]{2,1,0:T(8,128)(2,1)}) custom-call(s32[4,32]{1,0:T(4,128)} %cols_ref.9, s32[16,2]{1,0:T(8,128)} %bitcast.16, f32[4,32]{1,0:T(4,128)} %scl_ref.7, f32[1]{0:T(128)S(6)} %copy.29.c_ref, f32[1]{0:T(128)S(6)} %copy.30.w_ref, bf16[16,128,128]{2,1,0:T(8,128)(2,1)} %all_to_all.39.recv_ref, ...), custom_call_target="tpu_custom_call" | custom-call | flops 536870912 | bytes 5636096 | tf_op jit(solution)/shard_map/pallas_call | solution.py:126
  118.4 3.8 %all-to-all-start.5 = ((bf16[16,128,128]{2,1,0:T(8,128)(2,1)}), bf16[16,128,128]{2,1,0:T(8,128)(2,1)S(1)}, u32[]{:S(2)}, u32[]{:S(2)}) async-start(bf16[16,128,128]{2,1,0:T(8,128)(2,1)} %get-tuple-element.18), calls=%async_computation.5 | async-start | bytes 1048576 | tf_op jit(solution)/shard_map/all_to_all | solution.py:152
  122.2 0.0 copy-done.2
  122.2 0.1 copy.16
  122.3 0.1 copy.17
  122.4 0.7 pad_add_fusion.table_ref
  123.1 12.9 %all-to-all-done.5.src_ref = bf16[16,128,128]{2,1,0:T(8,128)(2,1)S(1)} async-done(((bf16[16,128,128]{2,1,0:T(8,128)(2,1)}), bf16[16,128,128]{2,1,0:T(8,128)(2,1)S(1)}, u32[]{:S(2)}, u32[]{:S(2)}) %all-to-all-start.5) | async-done | bytes 524320 | tf_op jit(solution)/shard_map/all_to_all | solution.py:152
  136.0 0.0 copy-start.1
  136.0 0.8 copy-done.1
  136.8 2.4 %shard_map.79 = bf16[4,128,128]{2,1,0:T(8,128)(2,1)} custom-call(s32[4,2]{1,0:T(4,128)} %pad_add_fusion.table_ref, bf16[16,128,128]{2,1,0:T(8,128)(2,1)} %copy-done.1), custom_call_target="tpu_custom_call" | custom-call | tf_op jit(solution)/shard_map/pallas_call | solution.py:57
  (1 shorter events, 0.0 us)
Async XLA Ops:
  22.0 17.7 %all-to-all-start.1 = ((bf16[16,128,128]{2,1,0:T(8,128)(2,1)}), bf16[16,128,128]{2,1,0:T(8,128)(2,1)S(1)}, u32[]{:S(2)}, u32[]{:S(2)}) async-start(bf16[16,128,128]{2,1,0:T(8,128)(2,1)} %shard_map.74), calls=%async_computation.1 | async-start | bytes 1048576 | tf_op jit(solution)/shard_map/all_to_all | solution.py:152
  39.7 0.8 copy-start
  94.5 27.7 %copy-start.2 = (s32[4]{0:T(128)S(1)}, s32[4]{0:T(128)}, u32[]{:S(2)}) copy-start(s32[4]{0:T(128)} %own_ref.1) | copy-start | bytes 52
  118.4 17.7 %all-to-all-start.5 = ((bf16[16,128,128]{2,1,0:T(8,128)(2,1)}), bf16[16,128,128]{2,1,0:T(8,128)(2,1)S(1)}, u32[]{:S(2)}, u32[]{:S(2)}) async-start(bf16[16,128,128]{2,1,0:T(8,128)(2,1)} %get-tuple-element.18), calls=%async_computation.5 | async-start | bytes 1048576 | tf_op jit(solution)/shard_map/all_to_all | solution.py:152
  136.0 0.8 copy-start.1

commit v7 on v4

--- a/solution.py
+++ b/solution.py
@@ -18,38 +18,34 @@
 
 def step_kernel(first, cols_ref, pick_ref, scl_ref, c_ref, w_ref, recv_ref, blk_ref, cur_ref, *rest):
     if first:
-        out_ref, go_ref, rows_ref = rest
+        out_ref, go_ref = rest
     else:
-        prev_ref, out_ref, go_ref, rows_ref = rest
-    r = pl.program_id(0)
+        prev_ref, out_ref, go_ref = rest
     local_rows, per_row = cols_ref.shape
-
-    def body(k, acc):
-        s = cols_ref[r, k] // local_rows
-        prod = jnp.dot(blk_ref[0, k], recv_ref[s], preferred_element_type=jnp.float32)
-        return acc + scl_ref[r, k] * prod
-
-    acc = lax.fori_loop(
-        0, per_row, body, jnp.zeros(out_ref.shape[1:], jnp.float32), unroll=True
-    )
     shift = c_ref[0]
     width = w_ref[0]
-    cur = cur_ref[0].astype(jnp.float32)
-    if first:
-        new = (acc - shift * cur) / width
-    else:
-        new = 2.0 * (acc - shift * cur) / width - prev_ref[0].astype(jnp.float32)
-    new = new.astype(out_ref.dtype)
-    out_ref[0] = new
-    rows_ref[r] = new
+    for r in range(local_rows):
 
-    @pl.when(r == local_rows - 1)
-    def _():
-        def put(e, carry):
-            go_ref[e] = rows_ref[pick_ref[e]]
-            return carry
+        def body(k, acc):
+            s = cols_ref[r, k] // local_rows
+            prod = jnp.dot(blk_ref[r, k], recv_ref[s], preferred_element_type=jnp.float32)
+            return acc + scl_ref[r, k] * prod
 
-        lax.fori_loop(0, go_ref.shape[0], put, 0)
+        acc = lax.fori_loop(
+            0, per_row, body, jnp.zeros(out_ref.shape[1:], jnp.float32), unroll=True
+        )
+        cur = cur_ref[r].astype(jnp.float32)
+        if first:
+            new = (acc - shift * cur) / width
+        else:
+            new = 2.0 * (acc - shift * cur) / width - prev_ref[r].astype(jnp.float32)
+        out_ref[r] = new.astype(out_ref.dtype)
+
+    def put(e, carry):
+        go_ref[e] = out_ref[pick_ref[e]]
+        return carry
+
+    lax.fori_loop(0, go_ref.shape[0], put, 0)
 
 
 def chebyshev_step(columns, pick, scales, center, half_width, received, blocks, cur, prev):
@@ -57,19 +53,10 @@
     width = cur.shape[2]
     nrows = pick.shape[0]
     first = prev is None
-    row_spec = pl.BlockSpec((1, orbitals, width), lambda r, c, p: (r, 0, 0))
     smem = pl.BlockSpec(memory_space=pltpu.SMEM)
-    in_specs = [
-        smem,
-        smem,
-        smem,
-        pl.BlockSpec(received.shape, lambda r, c, p: (0, 0, 0)),
-        pl.BlockSpec((1, per_row, orbitals, orbitals), lambda r, c, p: (r, 0, 0, 0)),
-        row_spec,
-    ]
-    args = [scales, center, half_width, received, blocks, cur]
+    vmem = pl.BlockSpec(memory_space=pltpu.VMEM)
+    args = [columns, pick, scales, center, half_width, received, blocks, cur]
     if not first:
-        in_specs.append(row_spec)
         args.append(prev)
     flops = 2 * local_rows * per_row * orbitals * orbitals * width
     nbytes = blocks.size * 2 + 2 * received.size * 2 + 3 * cur.size * 2
@@ -79,15 +66,11 @@
             jax.ShapeDtypeStruct(cur.shape, jnp.bfloat16),
             jax.ShapeDtypeStruct((nrows, orbitals, width), jnp.bfloat16),
         ),
-        grid_spec=pltpu.PrefetchScalarGridSpec(
-            num_scalar_prefetch=2,
-            grid=(local_rows,),
-            in_specs=in_specs,
-            out_specs=(row_spec, pl.BlockSpec((nrows, orbitals, width), lambda r, c, p: (0, 0, 0))),
-            scratch_shapes=[pltpu.VMEM(cur.shape, jnp.bfloat16)],
-        ),
+        in_specs=[smem] * 5 + [vmem] * (len(args) - 5),
+        out_specs=(vmem, vmem),
+        compiler_params=pltpu.CompilerParams(vmem_limit_bytes=8 * 1024 * 1024),
         cost_estimate=pl.CostEstimate(flops=flops, bytes_accessed=nbytes, transcendentals=0),
-    )(columns, pick, *args)
+    )(*args)
 
 
 def on_device(vectors, blocks, scales, columns, owners, center, half_width):
@@ -105,6 +88,7 @@
     def exchange(outgoing):
         return lax.all_to_all(outgoing, "rows", split_axis=0, concat_axis=0, tiled=True)
 
+    blocks = pltpu.with_memory_space_constraint(blocks, pltpu.VMEM)
     previous = vectors.reshape(local_rows, orbitals, group_width)
     current, outgoing = chebyshev_step(
         columns, wanted, scales, center, half_width,

time: 137 us -> 124 us (0.905)
  Pallas kernels: 23.9 us -> 9.18 us
  local copies, waits for them, and re-layouts: 3.92 us -> 7.6 us
    pallas_call x4, Pallas kernels: 23.9 us -> 9.18 us  [chebyshev_step(): pl.pallas_call(functools.partial(step_kernel, first), out_shape=(jax.Shap...]
    unnamed x2 -> x14, local copies, waits for them, and re-layouts: 0.79 us -> 4.47 us
where the time goes in v7:
time: 124 us; the launch traced here: 123 us
  blocking collectives  67.8 us (55%)
  waiting for transfers between devices  26.3 us (21%)
  Pallas kernels  9.18 us (7%)
  local copies, waits for them, and re-layouts  7.6 us (6%)
  starting transfers between devices  7.43 us (6%)
  other arithmetic  3.3 us (3%)
  between operations  1.41 us (1%)
    all_to_all x3, blocking collectives, exchange(): lax.all_to_all(outgoing, 'rows', split_axis=0, concat_axis=0, tiled=True)  52.4 us
    all_to_all x2, waiting for transfers between devices, exchange(): lax.all_to_all(outgoing, 'rows', split_axis=0, concat_axis=0, tiled=True)  26.3 us
    all_to_all x1, blocking collectives, on_device(): lax.all_to_all(asked, 'rows', split_axis=0, concat_axis=0, tiled=True)  15.4 us
    pallas_call x4, Pallas kernels, chebyshev_step(): pl.pallas_call(functools.partial(step_kernel, first), out_shape=(jax.Shap...  9.18 us
    all_to_all x2, starting transfers between devices, exchange(): lax.all_to_all(outgoing, 'rows', split_axis=0, concat_axis=0, tiled=True)  7.43 us
    unnamed x14, local copies, waits for them, and re-layouts  4.47 us
  transfers between devices with their start and end apart: 2, of which 2 were waited for; matrix products, arithmetic and copies ran while one was open for 0% of the time, Pallas kernels for 0%

profile of v7, /device:TPU:0, one launch (start us, length us, event | category | flops | bytes accessed | tf_op | source)
XLA Modules:
  0.0 123.0 jit_solution(7661692313173076292)
XLA Ops:
  0.0 0.7 and_select_fusion
  0.7 0.7 compare_and_fusion
  1.3 0.8 reshape.71
  2.1 0.1 select_reduce_fusion.1
  2.2 0.1 select_reduce_fusion
  2.3 0.1 copy.10
  2.4 15.4 %all_to_all.37 = s32[16,1,2]{2,1,0:T(1,128)S(1)} all-to-all(s32[16,1,2]{2,1,0:T(1,128)S(1)} %copy.10), channel_id=1, replica_groups=mesh['rows'=16,'vecs'=2] {'rows'}, dimensions={0} | all-to-all | bytes 256 | tf_op jit(solution)/shard_map/all_to_all | solution.py:84
  17.8 0.1 copy.11
  17.9 1.6 %gather_fusion = bf16[16,128,128]{2,1,0:T(8,128)(2,1)S(1)} fusion(bf16[4,128,128]{2,1,0:T(8,128)(2,1)} %bitcast.18, s32[1024]{0:T(1024)S(1)} %pad_clamp_fusion.1), kind=kCustom, calls=%fused_computation | custom fusion | bytes 1048640 | tf_op jit(solution)/shard_map/jit(_take)/gather | solution.py:95
  19.5 0.0 copy-start.3
  19.5 0.0 copy-start.6
  19.5 0.9 broadcast_select_fusion
  20.4 3.6 %all-to-all-start.1 = ((bf16[16,128,128]{2,1,0:T(8,128)(2,1)}), bf16[16,128,128]{2,1,0:T(8,128)(2,1)S(1)}, u32[]{:S(2)}, u32[]{:S(2)}) async-start(bf16[16,128,128]{2,1,0:T(8,128)(2,1)} %broadcast_select_fusion), calls=%async_computation.1 | async-start | bytes 1048576 | tf_op jit(solution)/shard_map/all_to_all | solution.py:89
  25.3 12.7 %all-to-all-done.1.recv_ref = bf16[16,128,128]{2,1,0:T(8,128)(2,1)S(1)} async-done(((bf16[16,128,128]{2,1,0:T(8,128)(2,1)}), bf16[16,128,128]{2,1,0:T(8,128)(2,1)S(1)}, u32[]{:S(2)}, u32[]{:S(2)}) %all-to-all-start.1) | async-done | bytes 524320 | tf_op jit(solution)/shard_map/all_to_all | solution.py:89
  38.0 2.2 %copy-done = bf16[4,32,128,128]{3,2,1,0:T(8,128)(2,1)S(1)} copy-done((bf16[4,32,128,128]{3,2,1,0:T(8,128)(2,1)S(1)}, bf16[4,32,128,128]{3,2,1,0:T(8,128)(2,1)}, u32[]{:S(2)}) %copy-start) | copy-done | bytes 4194328
  40.2 0.9 copy-done.2
  41.1 0.7 copy-done.4
  41.7 0.7 copy-done.5
  42.4 2.1 %shard_map.73 = (bf16[4,128,128]{2,1,0:T(8,128)(2,1)S(1)}, bf16[16,128,128]{2,1,0:T(8,128)(2,1)S(1)}) custom-call(s32[4,32]{1,0:T(4,128)S(1)} %copy-done.4, s32[16]{0:T(128)S(1)} %get-tuple-element.22.pick_ref, f32[4,32]{1,0:T(4,128)S(1)} %copy-done.5, f32[1]{0:T(128)S(6)} %copy.12.c_ref, f32[1]{0:T(128)S(6)} %copy.13.w_ref, ...), custom_call_target="tpu_custom_call" | custom-call | flops 536870912 | bytes 5636096 | tf_op jit(solution)/shard_map/pallas_call | solution.py:63
  44.5 17.5 %all_to_all.38.recv_ref = bf16[16,128,128]{2,1,0:T(8,128)(2,1)S(1)} all-to-all(bf16[16,128,128]{2,1,0:T(8,128)(2,1)S(1)} %get-tuple-element.12), channel_id=1, replica_groups=mesh['rows'=16,'vecs'=2] {'rows'}, dimensions={0} | all-to-all | bytes 1048576 | tf_op jit(solution)/shard_map/all_to_all | solution.py:89
  62.1 0.0 copy-done.3
  62.1 0.0 copy-done.1
  62.1 2.1 %shard_map.74 = (bf16[4,128,128]{2,1,0:T(8,128)(2,1)S(1)}, bf16[16,128,128]{2,1,0:T(8,128)(2,1)S(1)}) custom-call(s32[4,32]{1,0:T(4,128)S(1)} %copy-done.4, s32[16]{0:T(128)S(1)} %get-tuple-element.22.pick_ref, f32[4,32]{1,0:T(4,128)S(1)} %copy-done.6, f32[1]{0:T(128)S(6)} %copy.12.c_ref, f32[1]{0:T(128)S(6)} %copy.13.w_ref, ...), custom_call_target="tpu_custom_call" | custom-call | flops 536870912 | bytes 5636096 | tf_op jit(solution)/shard_map/pallas_call | solution.py:63
  64.2 17.5 %all_to_all.39.recv_ref = bf16[16,128,128]{2,1,0:T(8,128)(2,1)S(1)} all-to-all(bf16[16,128,128]{2,1,0:T(8,128)(2,1)S(1)} %get-tuple-element.14), channel_id=1, replica_groups=mesh['rows'=16,'vecs'=2] {'rows'}, dimensions={0} | all-to-all | bytes 1048576 | tf_op jit(solution)/shard_map/all_to_all | solution.py:89
  81.7 2.1 %shard_map.75 = (bf16[4,128,128]{2,1,0:T(8,128)(2,1)S(1)}, bf16[16,128,128]{2,1,0:T(8,128)(2,1)S(1)}) custom-call(s32[4,32]{1,0:T(4,128)S(1)} %copy-done.4, s32[16]{0:T(128)S(1)} %get-tuple-element.22.pick_ref, f32[4,32]{1,0:T(4,128)S(1)} %copy-done.6, f32[1]{0:T(128)S(6)} %copy.12.c_ref, f32[1]{0:T(128)S(6)} %copy.13.w_ref, ...), custom_call_target="tpu_custom_call" | custom-call | flops 536870912 | bytes 5636096 | tf_op jit(solution)/shard_map/pallas_call | solution.py:63
  83.8 17.4 %all_to_all.40.recv_ref = bf16[16,128,128]{2,1,0:T(8,128)(2,1)S(1)} all-to-all(bf16[16,128,128]{2,1,0:T(8,128)(2,1)S(1)} %get-tuple-element.16), channel_id=1, replica_groups=mesh['rows'=16,'vecs'=2] {'rows'}, dimensions={0} | all-to-all | bytes 1048576 | tf_op jit(solution)/shard_map/all_to_all | solution.py:89
  101.2 2.9 %shard_map.76 = (bf16[4,128,128]{2,1,0:T(8,128)(2,1)}, bf16[16,128,128]{2,1,0:T(8,128)(2,1)}) custom-call(s32[4,32]{1,0:T(4,128)S(1)} %copy-done.4, s32[16]{0:T(128)S(1)} %get-tuple-element.23.pick_ref, f32[4,32]{1,0:T(4,128)S(1)} %copy-done.6, f32[1]{0:T(128)S(6)} %copy.12.c_ref, f32[1]{0:T(128)S(6)} %copy.13.w_ref, ...), custom_call_target="tpu_custom_call" | custom-call | flops 536870912 | bytes 5636096 | tf_op jit(solution)/shard_map/pallas_call | solution.py:63
  104.1 3.9 %all-to-all-start.5 = ((bf16[16,128,128]{2,1,0:T(8,128)(2,1)}), bf16[16,128,128]{2,1,0:T(8,128)(2,1)S(1)}, u32[]{:S(2)}, u32[]{:S(2)}) async-start(bf16[16,128,128]{2,1,0:T(8,128)(2,1)} %get-tuple-element.18), calls=%async_computation.5 | async-start | bytes 1048576 | tf_op jit(solution)/shard_map/all_to_all | solution.py:89
  108.0 0.1 broadcast_bitcast_fusion
  108.0 13.6 %all-to-all-done.5 = bf16[16,128,128]{2,1,0:T(8,128)(2,1)S(1)} async-done(((bf16[16,128,128]{2,1,0:T(8,128)(2,1)}), bf16[16,128,128]{2,1,0:T(8,128)(2,1)S(1)}, u32[]{:S(2)}, u32[]{:S(2)}) %all-to-all-start.5) | async-done | bytes 524320 | tf_op jit(solution)/shard_map/all_to_all | solution.py:89
  121.6 0.6 gather_fusion.1
  122.2 0.8 bitcast_select_fusion
  (13 shorter events, 0.1 us)
Async XLA Ops:
  19.5 42.6 %copy-start.3 = (bf16[512,128]{1,0:T(8,128)(2,1)S(1)}, bf16[512,128]{1,0:T(8,128)(2,1)}, u32[]{:S(2)}) copy-start(bf16[512,128]{1,0:T(8,128)(2,1)} %param.7) | copy-start | bytes 393220
  19.5 42.6 %copy-start.6 = (f32[4,32]{1,0:T(4,128)S(1)}, f32[4,32]{1,0:T(4,128)}, u32[]{:S(2)}) copy-start(f32[4,32]{1,0:T(4,128)} %scl_ref.7) | copy-start | bytes 1540
  20.4 17.6 %all-to-all-start.1 = ((bf16[16,128,128]{2,1,0:T(8,128)(2,1)}), bf16[16,128,128]{2,1,0:T(8,128)(2,1)S(1)}, u32[]{:S(2)}, u32[]{:S(2)}) async-start(bf16[16,128,128]{2,1,0:T(8,128)(2,1)} %broadcast_select_fusion), calls=%async_computation.1 | async-start | bytes 1048576 | tf_op jit(solution)/shard_map/all_to_all | solution.py:89
  38.0 2.2 %copy-start = (bf16[4,32,128,128]{3,2,1,0:T(8,128)(2,1)S(1)}, bf16[4,32,128,128]{3,2,1,0:T(8,128)(2,1)}, u32[]{:S(2)}) copy-start(bf16[4,32,128,128]{3,2,1,0:T(8,128)(2,1)} %blk_ref.7) | copy-start | bytes 12582916
  40.2 0.9 copy-start.2
  41.1 0.7 copy-start.4
  41.7 0.7 copy-start.5
  42.4 19.7 %copy-start.1 = (bf16[4,32,128,128]{3,2,1,0:T(8,128)(2,1)S(1)}, bf16[4,32,128,128]{3,2,1,0:T(8,128)(2,1)}, u32[]{:S(2)}) copy-start(bf16[4,32,128,128]{3,2,1,0:T(8,128)(2,1)} %blk_ref.7) | copy-start | bytes 12582916
  104.1 17.5 %all-to-all-start.5 = ((bf16[16,128,128]{2,1,0:T(8,128)(2,1)}), bf16[16,128,128]{2,1,0:T(8,128)(2,1)S(1)}, u32[]{:S(2)}, u32[]{:S(2)}) async-start(bf16[16,128,128]{2,1,0:T(8,128)(2,1)} %get-tuple-element.18), calls=%async_computation.5 | async-start | bytes 1048576 | tf_op jit(solution)/shard_map/all_to_all | solution.py:89

commit v8 on v7

--- a/solution.py
+++ b/solution.py
@@ -11,9 +11,9 @@
 
 
 def requests(index, nrows, local_rows):
-    flat = index.reshape(-1)
-    hit = (flat // local_rows)[None, :] == jnp.arange(nrows, dtype=flat.dtype)[:, None]
-    return jnp.max(jnp.where(hit, (flat % local_rows)[None, :], 0), axis=1)
+    devices = jnp.arange(nrows, dtype=index.dtype).reshape((nrows,) + (1,) * index.ndim)
+    hit = (index // local_rows)[None] == devices
+    return jnp.max(jnp.where(hit, (index % local_rows)[None], 0), axis=tuple(range(1, index.ndim + 1)))
 
 
 def step_kernel(first, cols_ref, pick_ref, scl_ref, c_ref, w_ref, recv_ref, blk_ref, cur_ref, *rest):
@@ -92,7 +92,7 @@
     previous = vectors.reshape(local_rows, orbitals, group_width)
     current, outgoing = chebyshev_step(
         columns, wanted, scales, center, half_width,
-        exchange(jnp.take(previous, wanted, axis=0)), blocks, previous, None,
+        exchange(jnp.take(previous, wanted, axis=0, mode="clip")), blocks, previous, None,
     )
     for step in range(1, STEPS):
         pick = relay_want if step == STEPS - 1 else wanted
@@ -101,7 +101,7 @@
         )
         previous, current = (current, upcoming)
     arrived = exchange(outgoing)
-    placed = jnp.take(arrived, owners // local_rows, axis=0)
+    placed = jnp.take(arrived, owners // local_rows, axis=0, mode="clip")
     return placed.reshape(local_rows * orbitals, group_width)
 
 

time: 124 us -> 123 us (level)
  other arithmetic: 3.3 us -> 1.62 us
    gather x2, local copies, waits for them, and re-layouts: 2.12 us -> 3.54 us  [the longest x1 2.32 us: on_device(): jnp.take(previous, wanted, axis=0, mode='clip')]
where the time goes in v8:
time: 123 us; the launch traced here: 122 us
  blocking collectives  67.8 us (55%)
  waiting for transfers between devices  26.3 us (21%)
  Pallas kernels  9.17 us (7%)
  local copies, waits for them, and re-layouts  8.18 us (7%)
  starting transfers between devices  7.43 us (6%)
  other arithmetic  1.62 us (1%)
  between operations  1.36 us (1%)
    all_to_all x3, blocking collectives, exchange(): lax.all_to_all(outgoing, 'rows', split_axis=0, concat_axis=0, tiled=True)  52.4 us
    all_to_all x2, waiting for transfers between devices, exchange(): lax.all_to_all(outgoing, 'rows', split_axis=0, concat_axis=0, tiled=True)  26.3 us
    all_to_all x1, blocking collectives, on_device(): lax.all_to_all(asked, 'rows', split_axis=0, concat_axis=0, tiled=True)  15.4 us
    pallas_call x4, Pallas kernels, chebyshev_step(): pl.pallas_call(functools.partial(step_kernel, first), out_shape=(jax.Shap...  9.17 us
    all_to_all x2, starting transfers between devices, exchange(): lax.all_to_all(outgoing, 'rows', split_axis=0, concat_axis=0, tiled=True)  7.43 us
    unnamed x14, local copies, waits for them, and re-layouts  4.46 us
  transfers between devices with their start and end apart: 2, of which 2 were waited for; matrix products, arithmetic and copies ran while one was open for 0% of the time, Pallas kernels for 0%

profile of v8, /device:TPU:0, one launch (start us, length us, event | category | flops | bytes accessed | tf_op | source)
XLA Modules:
  0.0 121.9 jit_solution(5118068349888988503)
XLA Ops:
  0.0 0.0 copy-start.3
  0.0 0.0 copy-start.6
  0.0 0.7 and_select_fusion.1
  0.7 0.7 add_select_fusion.1
  1.4 0.1 select_reduce_fusion.1
  1.5 0.1 select_reduce_fusion
  1.6 0.1 copy.10
  1.7 15.4 %all_to_all.37 = s32[16,1,2]{2,1,0:T(1,128)S(1)} all-to-all(s32[16,1,2]{2,1,0:T(1,128)S(1)} %copy.10), channel_id=1, replica_groups=mesh['rows'=16,'vecs'=2] {'rows'}, dimensions={0} | all-to-all | bytes 256 | tf_op jit(solution)/shard_map/all_to_all | solution.py:84
  17.1 0.1 copy.11
  17.2 2.3 %gather_fusion = bf16[16,128,128]{2,1,0:T(8,128)(2,1)} fusion(bf16[4,128,128]{2,1,0:T(8,128)(2,1)} %bitcast.11, s32[1024]{0:T(1024)S(1)} %pad_clamp_fusion.1), kind=kCustom, calls=%fused_computation | custom fusion | bytes 1048640 | tf_op jit(solution)/shard_map/jit(_take)/gather | solution.py:95
  19.5 3.6 %all-to-all-start.1 = ((bf16[16,128,128]{2,1,0:T(8,128)(2,1)}), bf16[16,128,128]{2,1,0:T(8,128)(2,1)S(1)}, u32[]{:S(2)}, u32[]{:S(2)}) async-start(bf16[16,128,128]{2,1,0:T(8,128)(2,1)} %gather_fusion), calls=%async_computation.1 | async-start | bytes 1048576 | tf_op jit(solution)/shard_map/all_to_all | solution.py:89
  24.4 12.7 %all-to-all-done.1.recv_ref = bf16[16,128,128]{2,1,0:T(8,128)(2,1)S(1)} async-done(((bf16[16,128,128]{2,1,0:T(8,128)(2,1)}), bf16[16,128,128]{2,1,0:T(8,128)(2,1)S(1)}, u32[]{:S(2)}, u32[]{:S(2)}) %all-to-all-start.1) | async-done | bytes 524320 | tf_op jit(solution)/shard_map/all_to_all | solution.py:89
  37.1 0.0 copy-start
  37.1 2.2 %copy-done = bf16[4,32,128,128]{3,2,1,0:T(8,128)(2,1)S(1)} copy-done((bf16[4,32,128,128]{3,2,1,0:T(8,128)(2,1)S(1)}, bf16[4,32,128,128]{3,2,1,0:T(8,128)(2,1)}, u32[]{:S(2)}) %copy-start) | copy-done | bytes 4194328
  39.2 0.0 copy-start.2
  39.2 0.9 copy-done.2
  40.1 0.0 copy-start.4
  40.1 0.7 copy-done.4
  40.8 0.7 copy-done.5
  41.5 2.1 %shard_map.73 = (bf16[4,128,128]{2,1,0:T(8,128)(2,1)S(1)}, bf16[16,128,128]{2,1,0:T(8,128)(2,1)S(1)}) custom-call(s32[4,32]{1,0:T(4,128)S(1)} %copy-done.4, s32[16]{0:T(128)S(1)} %get-tuple-element.21.pick_ref, f32[4,32]{1,0:T(4,128)S(1)} %copy-done.5, f32[1]{0:T(128)S(6)} %copy.12.c_ref, f32[1]{0:T(128)S(6)} %copy.13.w_ref, ...), custom_call_target="tpu_custom_call" | custom-call | flops 536870912 | bytes 5636096 | tf_op jit(solution)/shard_map/pallas_call | solution.py:63
  43.6 17.5 %all_to_all.38.recv_ref = bf16[16,128,128]{2,1,0:T(8,128)(2,1)S(1)} all-to-all(bf16[16,128,128]{2,1,0:T(8,128)(2,1)S(1)} %get-tuple-element.12), channel_id=1, replica_groups=mesh['rows'=16,'vecs'=2] {'rows'}, dimensions={0} | all-to-all | bytes 1048576 | tf_op jit(solution)/shard_map/all_to_all | solution.py:89
  61.2 0.0 copy-done.3
  61.2 0.0 copy-done.6
  61.2 0.0 copy-done.1
  61.2 2.1 %shard_map.74 = (bf16[4,128,128]{2,1,0:T(8,128)(2,1)S(1)}, bf16[16,128,128]{2,1,0:T(8,128)(2,1)S(1)}) custom-call(s32[4,32]{1,0:T(4,128)S(1)} %copy-done.4, s32[16]{0:T(128)S(1)} %get-tuple-element.21.pick_ref, f32[4,32]{1,0:T(4,128)S(1)} %copy-done.6, f32[1]{0:T(128)S(6)} %copy.12.c_ref, f32[1]{0:T(128)S(6)} %copy.13.w_ref, ...), custom_call_target="tpu_custom_call" | custom-call | flops 536870912 | bytes 5636096 | tf_op jit(solution)/shard_map/pallas_call | solution.py:63
  63.3 17.5 %all_to_all.39.recv_ref = bf16[16,128,128]{2,1,0:T(8,128)(2,1)S(1)} all-to-all(bf16[16,128,128]{2,1,0:T(8,128)(2,1)S(1)} %get-tuple-element.14), channel_id=1, replica_groups=mesh['rows'=16,'vecs'=2] {'rows'}, dimensions={0} | all-to-all | bytes 1048576 | tf_op jit(solution)/shard_map/all_to_all | solution.py:89
  80.8 2.1 %shard_map.75 = (bf16[4,128,128]{2,1,0:T(8,128)(2,1)S(1)}, bf16[16,128,128]{2,1,0:T(8,128)(2,1)S(1)}) custom-call(s32[4,32]{1,0:T(4,128)S(1)} %copy-done.4, s32[16]{0:T(128)S(1)} %get-tuple-element.21.pick_ref, f32[4,32]{1,0:T(4,128)S(1)} %copy-done.6, f32[1]{0:T(128)S(6)} %copy.12.c_ref, f32[1]{0:T(128)S(6)} %copy.13.w_ref, ...), custom_call_target="tpu_custom_call" | custom-call | flops 536870912 | bytes 5636096 | tf_op jit(solution)/shard_map/pallas_call | solution.py:63
  82.8 17.4 %all_to_all.40.recv_ref = bf16[16,128,128]{2,1,0:T(8,128)(2,1)S(1)} all-to-all(bf16[16,128,128]{2,1,0:T(8,128)(2,1)S(1)} %get-tuple-element.16), channel_id=1, replica_groups=mesh['rows'=16,'vecs'=2] {'rows'}, dimensions={0} | all-to-all | bytes 1048576 | tf_op jit(solution)/shard_map/all_to_all | solution.py:89
  100.2 2.9 %shard_map.76 = (bf16[4,128,128]{2,1,0:T(8,128)(2,1)}, bf16[16,128,128]{2,1,0:T(8,128)(2,1)}) custom-call(s32[4,32]{1,0:T(4,128)S(1)} %copy-done.4, s32[16]{0:T(128)S(1)} %get-tuple-element.22.pick_ref, f32[4,32]{1,0:T(4,128)S(1)} %copy-done.6, f32[1]{0:T(128)S(6)} %copy.12.c_ref, f32[1]{0:T(128)S(6)} %copy.13.w_ref, ...), custom_call_target="tpu_custom_call" | custom-call | flops 536870912 | bytes 5636096 | tf_op jit(solution)/shard_map/pallas_call | solution.py:63
  103.2 3.9 %all-to-all-start.5 = ((bf16[16,128,128]{2,1,0:T(8,128)(2,1)}), bf16[16,128,128]{2,1,0:T(8,128)(2,1)S(1)}, u32[]{:S(2)}, u32[]{:S(2)}) async-start(bf16[16,128,128]{2,1,0:T(8,128)(2,1)} %get-tuple-element.18), calls=%async_computation.5 | async-start | bytes 1048576 | tf_op jit(solution)/shard_map/all_to_all | solution.py:89
  107.0 13.7 %all-to-all-done.5 = bf16[16,128,128]{2,1,0:T(8,128)(2,1)S(1)} async-done(((bf16[16,128,128]{2,1,0:T(8,128)(2,1)}), bf16[16,128,128]{2,1,0:T(8,128)(2,1)S(1)}, u32[]{:S(2)}, u32[]{:S(2)}) %all-to-all-start.5) | async-done | bytes 524320 | tf_op jit(solution)/shard_map/all_to_all | solution.py:89
  120.7 1.2 gather_fusion.1
  (6 shorter events, 0.0 us)
Async XLA Ops:
  0.0 61.2 %copy-start.3 = (bf16[512,128]{1,0:T(8,128)(2,1)S(1)}, bf16[512,128]{1,0:T(8,128)(2,1)}, u32[]{:S(2)}) copy-start(bf16[512,128]{1,0:T(8,128)(2,1)} %param.7) | copy-start | bytes 393220
  0.0 61.2 %copy-start.6 = (f32[4,32]{1,0:T(4,128)S(1)}, f32[4,32]{1,0:T(4,128)}, u32[]{:S(2)}) copy-start(f32[4,32]{1,0:T(4,128)} %scl_ref.7) | copy-start | bytes 1540
  19.5 17.6 %all-to-all-start.1 = ((bf16[16,128,128]{2,1,0:T(8,128)(2,1)}), bf16[16,128,128]{2,1,0:T(8,128)(2,1)S(1)}, u32[]{:S(2)}, u32[]{:S(2)}) async-start(bf16[16,128,128]{2,1,0:T(8,128)(2,1)} %gather_fusion), calls=%async_computation.1 | async-start | bytes 1048576 | tf_op jit(solution)/shard_map/all_to_all | solution.py:89
  37.1 2.2 %copy-start = (bf16[4,32,128,128]{3,2,1,0:T(8,128)(2,1)S(1)}, bf16[4,32,128,128]{3,2,1,0:T(8,128)(2,1)}, u32[]{:S(2)}) copy-start(bf16[4,32,128,128]{3,2,1,0:T(8,128)(2,1)} %blk_ref.7) | copy-start | bytes 12582916
  39.2 0.9 copy-start.2
  40.1 0.7 copy-start.4
  40.8 0.7 copy-start.5
  41.5 19.7 %copy-start.1 = (bf16[4,32,128,128]{3,2,1,0:T(8,128)(2,1)S(1)}, bf16[4,32,128,128]{3,2,1,0:T(8,128)(2,1)}, u32[]{:S(2)}) copy-start(bf16[4,32,128,128]{3,2,1,0:T(8,128)(2,1)} %blk_ref.7) | copy-start | bytes 12582916
  103.2 17.5 %all-to-all-start.5 = ((bf16[16,128,128]{2,1,0:T(8,128)(2,1)}), bf16[16,128,128]{2,1,0:T(8,128)(2,1)S(1)}, u32[]{:S(2)}, u32[]{:S(2)}) async-start(bf16[16,128,128]{2,1,0:T(8,128)(2,1)} %get-tuple-element.18), calls=%async_computation.5 | async-start | bytes 1048576 | tf_op jit(solution)/shard_map/all_to_all | solution.py:89

commit v9 on v8

--- a/solution.py
+++ b/solution.py
@@ -73,6 +73,13 @@
     )(*args)
 
 
+def select_rows(panels, index):
+    chosen = jnp.broadcast_to(panels[0][None], (index.shape[0],) + panels.shape[1:])
+    for atom in range(1, panels.shape[0]):
+        chosen = jnp.where((index == atom)[:, None, None], panels[atom][None], chosen)
+    return chosen
+
+
 def on_device(vectors, blocks, scales, columns, owners, center, half_width):
     nrows = lax.axis_size("rows")
     local_rows = blocks.shape[0]
@@ -92,7 +99,7 @@
     previous = vectors.reshape(local_rows, orbitals, group_width)
     current, outgoing = chebyshev_step(
         columns, wanted, scales, center, half_width,
-        exchange(jnp.take(previous, wanted, axis=0, mode="clip")), blocks, previous, None,
+        exchange(select_rows(previous, wanted)), blocks, previous, None,
     )
     for step in range(1, STEPS):
         pick = relay_want if step == STEPS - 1 else wanted

time: 123 us -> 122 us (level)
  blocking collectives: 67.8 us -> 52.4 us
  starting transfers between devices: 7.43 us -> 15.7 us
  waiting for transfers between devices: 26.3 us -> 32.7 us
    all_to_all x1 -> x0, blocking collectives: 15.4 us -> none  [on_device(): lax.all_to_all(asked, 'rows', split_axis=0, concat_axis=0, tiled=True)]
    all_to_all x0 -> x1, starting transfers between devices: none -> 8.31 us  [on_device(): lax.all_to_all(asked, 'rows', split_axis=0, concat_axis=0, tiled=True)]
    all_to_all x0 -> x1, waiting for transfers between devices: none -> 6.37 us  [on_device(): lax.all_to_all(asked, 'rows', split_axis=0, concat_axis=0, tiled=True)]
    gather x1 -> x0, local copies, waits for them, and re-layouts: 2.32 us -> none  [on_device(): jnp.take(previous, wanted, axis=0, mode='clip')]
  transfers between devices with their start and end apart: 2 -> 3, of which waited for: 2 -> 3; matrix products, arithmetic and copies ran while one was open for 0% -> 1% of each run, Pallas kernels for 0% -> 0%
where the time goes in v9:
time: 122 us; the launch traced here: 121 us
  blocking collectives  52.4 us (43%)
  waiting for transfers between devices  32.7 us (27%)
  starting transfers between devices  15.7 us (13%)
  Pallas kernels  9.16 us (8%)
  local copies, waits for them, and re-layouts  7.27 us (6%)
  other arithmetic  2.6 us (2%)
  between operations  1.38 us (1%)
    all_to_all x3, blocking collectives, exchange(): lax.all_to_all(outgoing, 'rows', split_axis=0, concat_axis=0, tiled=True)  52.4 us
    all_to_all x2, waiting for transfers between devices, exchange(): lax.all_to_all(outgoing, 'rows', split_axis=0, concat_axis=0, tiled=True)  26.3 us
    pallas_call x4, Pallas kernels, chebyshev_step(): pl.pallas_call(functools.partial(step_kernel, first), out_shape=(jax.Shap...  9.16 us
    all_to_all x1, starting transfers between devices, on_device(): lax.all_to_all(asked, 'rows', split_axis=0, concat_axis=0, tiled=True)  8.31 us
    all_to_all x2, starting transfers between devices, exchange(): lax.all_to_all(outgoing, 'rows', split_axis=0, concat_axis=0, tiled=True)  7.42 us
    all_to_all x1, waiting for transfers between devices, on_device(): lax.all_to_all(asked, 'rows', split_axis=0, concat_axis=0, tiled=True)  6.37 us
    unnamed x14, local copies, waits for them, and re-layouts  4.46 us
  transfers between devices with their start and end apart: 3, of which 3 were waited for; matrix products, arithmetic and copies ran while one was open for 1% of the time, Pallas kernels for 0%

profile of v9, /device:TPU:0, one launch (start us, length us, event | category | flops | bytes accessed | tf_op | source)
XLA Modules:
  0.0 121.3 jit_solution(2195159301084862363)
XLA Ops:
  0.0 0.0 copy-start.3
  0.0 0.0 copy-start.6
  0.0 0.7 and_select_fusion.1
  0.7 0.7 add_select_fusion.1
  1.4 0.1 select_reduce_fusion.1
  1.5 0.1 select_reduce_fusion
  1.6 0.7 copy.10
  2.3 8.3 %all-to-all-start = ((s32[16,1,2]{2,1,0:T(1,128)}), s32[16,1,2]{2,1,0:T(1,128)S(1)}, u32[]{:S(2)}, u32[]{:S(2)}) async-start(s32[16,1,2]{2,1,0:T(1,128)} %copy.10), calls=%async_computation | async-start | bytes 16384 | tf_op jit(solution)/shard_map/all_to_all | solution.py:91
  10.6 0.8 fusion.1
  11.4 6.4 %all-to-all-done = s32[16,1,2]{2,1,0:T(1,128)S(1)} async-done(((s32[16,1,2]{2,1,0:T(1,128)}), s32[16,1,2]{2,1,0:T(1,128)S(1)}, u32[]{:S(2)}, u32[]{:S(2)}) %all-to-all-start) | async-done | bytes 160 | tf_op jit(solution)/shard_map/all_to_all | solution.py:91
  17.8 0.1 copy.11
  17.9 1.0 select_select_fusion
  18.9 3.6 %all-to-all-start.1 = ((bf16[16,128,128]{2,1,0:T(8,128)(2,1)}), bf16[16,128,128]{2,1,0:T(8,128)(2,1)S(1)}, u32[]{:S(2)}, u32[]{:S(2)}) async-start(bf16[16,128,128]{2,1,0:T(8,128)(2,1)} %select_select_fusion), calls=%async_computation.1 | async-start | bytes 1048576 | tf_op jit(solution)/shard_map/all_to_all | solution.py:96
  23.8 12.7 %all-to-all-done.1.recv_ref = bf16[16,128,128]{2,1,0:T(8,128)(2,1)S(1)} async-done(((bf16[16,128,128]{2,1,0:T(8,128)(2,1)}), bf16[16,128,128]{2,1,0:T(8,128)(2,1)S(1)}, u32[]{:S(2)}, u32[]{:S(2)}) %all-to-all-start.1) | async-done | bytes 524320 | tf_op jit(solution)/shard_map/all_to_all | solution.py:96
  36.4 2.2 %copy-done = bf16[4,32,128,128]{3,2,1,0:T(8,128)(2,1)S(1)} copy-done((bf16[4,32,128,128]{3,2,1,0:T(8,128)(2,1)S(1)}, bf16[4,32,128,128]{3,2,1,0:T(8,128)(2,1)}, u32[]{:S(2)}) %copy-start) | copy-done | bytes 4194328
  38.6 0.0 copy-start.2
  38.6 0.9 copy-done.2
  39.5 0.7 copy-done.4
  40.2 0.7 copy-done.5
  40.9 2.1 %shard_map.73 = (bf16[4,128,128]{2,1,0:T(8,128)(2,1)S(1)}, bf16[16,128,128]{2,1,0:T(8,128)(2,1)S(1)}) custom-call(s32[4,32]{1,0:T(4,128)S(1)} %copy-done.4, s32[16]{0:T(128)S(1)} %get-tuple-element.28.pick_ref, f32[4,32]{1,0:T(4,128)S(1)} %copy-done.5, f32[1]{0:T(128)S(6)} %copy.12.c_ref, f32[1]{0:T(128)S(6)} %copy.13.w_ref, ...), custom_call_target="tpu_custom_call" | custom-call | flops 536870912 | bytes 5636096 | tf_op jit(solution)/shard_map/pallas_call | solution.py:63
  43.0 17.5 %all_to_all.37.recv_ref = bf16[16,128,128]{2,1,0:T(8,128)(2,1)S(1)} all-to-all(bf16[16,128,128]{2,1,0:T(8,128)(2,1)S(1)} %get-tuple-element.12), channel_id=1, replica_groups=mesh['rows'=16,'vecs'=2] {'rows'}, dimensions={0} | all-to-all | bytes 1048576 | tf_op jit(solution)/shard_map/all_to_all | solution.py:96
  60.6 0.0 copy-done.3
  60.6 0.0 copy-done.6
  60.6 0.0 copy-done.1
  60.6 2.1 %shard_map.74 = (bf16[4,128,128]{2,1,0:T(8,128)(2,1)S(1)}, bf16[16,128,128]{2,1,0:T(8,128)(2,1)S(1)}) custom-call(s32[4,32]{1,0:T(4,128)S(1)} %copy-done.4, s32[16]{0:T(128)S(1)} %get-tuple-element.28.pick_ref, f32[4,32]{1,0:T(4,128)S(1)} %copy-done.6, f32[1]{0:T(128)S(6)} %copy.12.c_ref, f32[1]{0:T(128)S(6)} %copy.13.w_ref, ...), custom_call_target="tpu_custom_call" | custom-call | flops 536870912 | bytes 5636096 | tf_op jit(solution)/shard_map/pallas_call | solution.py:63
  62.7 17.5 %all_to_all.38.recv_ref = bf16[16,128,128]{2,1,0:T(8,128)(2,1)S(1)} all-to-all(bf16[16,128,128]{2,1,0:T(8,128)(2,1)S(1)} %get-tuple-element.14), channel_id=1, replica_groups=mesh['rows'=16,'vecs'=2] {'rows'}, dimensions={0} | all-to-all | bytes 1048576 | tf_op jit(solution)/shard_map/all_to_all | solution.py:96
  80.2 2.1 %shard_map.75 = (bf16[4,128,128]{2,1,0:T(8,128)(2,1)S(1)}, bf16[16,128,128]{2,1,0:T(8,128)(2,1)S(1)}) custom-call(s32[4,32]{1,0:T(4,128)S(1)} %copy-done.4, s32[16]{0:T(128)S(1)} %get-tuple-element.28.pick_ref, f32[4,32]{1,0:T(4,128)S(1)} %copy-done.6, f32[1]{0:T(128)S(6)} %copy.12.c_ref, f32[1]{0:T(128)S(6)} %copy.13.w_ref, ...), custom_call_target="tpu_custom_call" | custom-call | flops 536870912 | bytes 5636096 | tf_op jit(solution)/shard_map/pallas_call | solution.py:63
  82.2 17.4 %all_to_all.39.recv_ref = bf16[16,128,128]{2,1,0:T(8,128)(2,1)S(1)} all-to-all(bf16[16,128,128]{2,1,0:T(8,128)(2,1)S(1)} %get-tuple-element.16), channel_id=1, replica_groups=mesh['rows'=16,'vecs'=2] {'rows'}, dimensions={0} | all-to-all | bytes 1048576 | tf_op jit(solution)/shard_map/all_to_all | solution.py:96
  99.6 2.9 %shard_map.76 = (bf16[4,128,128]{2,1,0:T(8,128)(2,1)}, bf16[16,128,128]{2,1,0:T(8,128)(2,1)}) custom-call(s32[4,32]{1,0:T(4,128)S(1)} %copy-done.4, s32[16]{0:T(128)S(1)} %get-tuple-element.29.pick_ref, f32[4,32]{1,0:T(4,128)S(1)} %copy-done.6, f32[1]{0:T(128)S(6)} %copy.12.c_ref, f32[1]{0:T(128)S(6)} %copy.13.w_ref, ...), custom_call_target="tpu_custom_call" | custom-call | flops 536870912 | bytes 5636096 | tf_op jit(solution)/shard_map/pallas_call | solution.py:63
  102.5 3.9 %all-to-all-start.5 = ((bf16[16,128,128]{2,1,0:T(8,128)(2,1)}), bf16[16,128,128]{2,1,0:T(8,128)(2,1)S(1)}, u32[]{:S(2)}, u32[]{:S(2)}) async-start(bf16[16,128,128]{2,1,0:T(8,128)(2,1)} %get-tuple-element.18), calls=%async_computation.5 | async-start | bytes 1048576 | tf_op jit(solution)/shard_map/all_to_all | solution.py:96
  106.4 13.7 %all-to-all-done.5 = bf16[16,128,128]{2,1,0:T(8,128)(2,1)S(1)} async-done(((bf16[16,128,128]{2,1,0:T(8,128)(2,1)}), bf16[16,128,128]{2,1,0:T(8,128)(2,1)S(1)}, u32[]{:S(2)}, u32[]{:S(2)}) %all-to-all-start.5) | async-done | bytes 524320 | tf_op jit(solution)/shard_map/all_to_all | solution.py:96
  120.1 1.2 %gather_fusion = bf16[4,128,128]{2,1,0:T(8,128)(2,1)} fusion(bf16[16,128,128]{2,1,0:T(8,128)(2,1)S(1)} %all-to-all-done.5, s32[1024]{0:T(1024)S(1)} %pad_clamp_fusion), kind=kCustom, calls=%fused_computation | custom fusion | bytes 262160 | tf_op jit(solution)/shard_map/jit(_take)/gather | solution.py:111
  (8 shorter events, 0.0 us)
Async XLA Ops:
  0.0 60.6 %copy-start.3 = (bf16[512,128]{1,0:T(8,128)(2,1)S(1)}, bf16[512,128]{1,0:T(8,128)(2,1)}, u32[]{:S(2)}) copy-start(bf16[512,128]{1,0:T(8,128)(2,1)} %param.7) | copy-start | bytes 393220
  0.0 60.6 %copy-start.6 = (f32[4,32]{1,0:T(4,128)S(1)}, f32[4,32]{1,0:T(4,128)}, u32[]{:S(2)}) copy-start(f32[4,32]{1,0:T(4,128)} %scl_ref.7) | copy-start | bytes 1540
  2.3 15.5 %all-to-all-start = ((s32[16,1,2]{2,1,0:T(1,128)}), s32[16,1,2]{2,1,0:T(1,128)S(1)}, u32[]{:S(2)}, u32[]{:S(2)}) async-start(s32[16,1,2]{2,1,0:T(1,128)} %copy.10), calls=%async_computation | async-start | bytes 16384 | tf_op jit(solution)/shard_map/all_to_all | solution.py:91
  18.9 17.6 %all-to-all-start.1 = ((bf16[16,128,128]{2,1,0:T(8,128)(2,1)}), bf16[16,128,128]{2,1,0:T(8,128)(2,1)S(1)}, u32[]{:S(2)}, u32[]{:S(2)}) async-start(bf16[16,128,128]{2,1,0:T(8,128)(2,1)} %select_select_fusion), calls=%async_computation.1 | async-start | bytes 1048576 | tf_op jit(solution)/shard_map/all_to_all | solution.py:96
  36.4 2.2 %copy-start = (bf16[4,32,128,128]{3,2,1,0:T(8,128)(2,1)S(1)}, bf16[4,32,128,128]{3,2,1,0:T(8,128)(2,1)}, u32[]{:S(2)}) copy-start(bf16[4,32,128,128]{3,2,1,0:T(8,128)(2,1)} %blk_ref.7) | copy-start | bytes 12582916
  38.6 0.9 copy-start.2
  39.5 0.7 copy-start.4
  40.2 0.7 copy-start.5
  40.9 19.7 %copy-start.1 = (bf16[4,32,128,128]{3,2,1,0:T(8,128)(2,1)S(1)}, bf16[4,32,128,128]{3,2,1,0:T(8,128)(2,1)}, u32[]{:S(2)}) copy-start(bf16[4,32,128,128]{3,2,1,0:T(8,128)(2,1)} %blk_ref.7) | copy-start | bytes 12582916
  102.5 17.5 %all-to-all-start.5 = ((bf16[16,128,128]{2,1,0:T(8,128)(2,1)}), bf16[16,128,128]{2,1,0:T(8,128)(2,1)S(1)}, u32[]{:S(2)}, u32[]{:S(2)}) async-start(bf16[16,128,128]{2,1,0:T(8,128)(2,1)} %get-tuple-element.18), calls=%async_computation.5 | async-start | bytes 1048576 | tf_op jit(solution)/shard_map/all_to_all | solution.py:96

commit v10 on v9

--- a/solution.py
+++ b/solution.py
@@ -16,11 +16,20 @@
     return jnp.max(jnp.where(hit, (index % local_rows)[None], 0), axis=tuple(range(1, index.ndim + 1)))
 
 
-def step_kernel(first, cols_ref, pick_ref, scl_ref, c_ref, w_ref, recv_ref, blk_ref, cur_ref, *rest):
+def step_kernel(first, cols_hbm, pick_ref, scl_hbm, c_ref, w_ref, recv_ref, blk_ref, cur_hbm, *rest):
     if first:
-        out_ref, go_ref = rest
+        out_ref, go_ref, cols_ref, scl_ref, cur_ref, sems = rest
     else:
-        prev_ref, out_ref, go_ref = rest
+        prev_ref, out_ref, go_ref, cols_ref, scl_ref, cur_ref, sems = rest
+    copies = [
+        pltpu.make_async_copy(cols_hbm, cols_ref, sems.at[0]),
+        pltpu.make_async_copy(scl_hbm, scl_ref, sems.at[1]),
+        pltpu.make_async_copy(cur_hbm, cur_ref, sems.at[2]),
+    ]
+    for copy in copies:
+        copy.start()
+    copies[0].wait()
+    copies[1].wait()
     local_rows, per_row = cols_ref.shape
     shift = c_ref[0]
     width = w_ref[0]
@@ -34,6 +43,8 @@
         acc = lax.fori_loop(
             0, per_row, body, jnp.zeros(out_ref.shape[1:], jnp.float32), unroll=True
         )
+        if r == 0:
+            copies[2].wait()
         cur = cur_ref[r].astype(jnp.float32)
         if first:
             new = (acc - shift * cur) / width
@@ -55,9 +66,18 @@
     first = prev is None
     smem = pl.BlockSpec(memory_space=pltpu.SMEM)
     vmem = pl.BlockSpec(memory_space=pltpu.VMEM)
-    args = [columns, pick, scales, center, half_width, received, blocks, cur]
+    anywhere = pl.BlockSpec(memory_space=pl.ANY)
+    hbm = pltpu.MemorySpace.HBM
+    if first:
+        cur = pltpu.with_memory_space_constraint(cur, hbm)
+    args = [
+        pltpu.with_memory_space_constraint(columns, hbm), pick,
+        pltpu.with_memory_space_constraint(scales, hbm), center, half_width, received, blocks, cur,
+    ]
+    in_specs = [anywhere, smem, anywhere, smem, smem, vmem, vmem, anywhere]
     if not first:
         args.append(prev)
+        in_specs.append(vmem)
     flops = 2 * local_rows * per_row * orbitals * orbitals * width
     nbytes = blocks.size * 2 + 2 * received.size * 2 + 3 * cur.size * 2
     return pl.pallas_call(
@@ -66,8 +86,14 @@
             jax.ShapeDtypeStruct(cur.shape, jnp.bfloat16),
             jax.ShapeDtypeStruct((nrows, orbitals, width), jnp.bfloat16),
         ),
-        in_specs=[smem] * 5 + [vmem] * (len(args) - 5),
+        in_specs=in_specs,
         out_specs=(vmem, vmem),
+        scratch_shapes=[
+            pltpu.SMEM(columns.shape, columns.dtype),
+            pltpu.SMEM(scales.shape, scales.dtype),
+            pltpu.VMEM(cur.shape, cur.dtype),
+            pltpu.SemaphoreType.DMA((3,)),
+        ],
         compiler_params=pltpu.CompilerParams(vmem_limit_bytes=8 * 1024 * 1024),
         cost_estimate=pl.CostEstimate(flops=flops, bytes_accessed=nbytes, transcendentals=0),
     )(*args)

time: 122 us -> 123 us (level)
  Pallas kernels: 9.16 us -> 12.7 us
  local copies, waits for them, and re-layouts: 7.27 us -> 5 us
    pallas_call x4, Pallas kernels: 9.16 us -> 12.7 us  [chebyshev_step(): pl.pallas_call(functools.partial(step_kernel, first), out_shape=(jax.Shap...]
    unnamed x14 -> x6, local copies, waits for them, and re-layouts: 4.46 us -> 2.2 us
where the time goes in v10:
time: 123 us
  blocking collectives  52.4 us (43%)
  waiting for transfers between devices  32.7 us (27%)
  starting transfers between devices  15.7 us (13%)
  Pallas kernels  12.7 us (10%)
  local copies, waits for them, and re-layouts  5 us (4%)
  other arithmetic  2.61 us (2%)
  between operations  1.38 us (1%)
    all_to_all x3, blocking collectives, exchange(): lax.all_to_all(outgoing, 'rows', split_axis=0, concat_axis=0, tiled=True)  52.4 us
    all_to_all x2, waiting for transfers between devices, exchange(): lax.all_to_all(outgoing, 'rows', split_axis=0, concat_axis=0, tiled=True)  26.3 us
    pallas_call x4, Pallas kernels, chebyshev_step(): pl.pallas_call(functools.partial(step_kernel, first), out_shape=(jax.Shap...  12.7 us
    all_to_all x1, starting transfers between devices, on_device(): lax.all_to_all(asked, 'rows', split_axis=0, concat_axis=0, tiled=True)  8.31 us
    all_to_all x2, starting transfers between devices, exchange(): lax.all_to_all(outgoing, 'rows', split_axis=0, concat_axis=0, tiled=True)  7.43 us
    all_to_all x1, waiting for transfers between devices, on_device(): lax.all_to_all(asked, 'rows', split_axis=0, concat_axis=0, tiled=True)  6.37 us
  transfers between devices with their start and end apart: 3, of which 3 were waited for; matrix products, arithmetic and copies ran while one was open for 1% of the time, Pallas kernels for 0%

profile of v10, /device:TPU:0, one launch (start us, length us, event | category | flops | bytes accessed | tf_op | source)
XLA Modules:
  0.0 122.6 jit_solution(2682855917644799013)
XLA Ops:
  0.0 0.0 copy-start.2
  0.0 0.7 and_select_fusion.1
  0.7 0.7 add_select_fusion.1
  1.4 0.1 select_reduce_fusion.1
  1.5 0.1 select_reduce_fusion
  1.6 0.7 copy.10
  2.3 8.3 %all-to-all-start = ((s32[16,1,2]{2,1,0:T(1,128)}), s32[16,1,2]{2,1,0:T(1,128)S(1)}, u32[]{:S(2)}, u32[]{:S(2)}) async-start(s32[16,1,2]{2,1,0:T(1,128)} %copy.10), calls=%async_computation | async-start | bytes 16384 | tf_op jit(solution)/shard_map/all_to_all | solution.py:117
  10.6 0.8 fusion.1
  11.4 6.4 %all-to-all-done = s32[16,1,2]{2,1,0:T(1,128)S(1)} async-done(((s32[16,1,2]{2,1,0:T(1,128)}), s32[16,1,2]{2,1,0:T(1,128)S(1)}, u32[]{:S(2)}, u32[]{:S(2)}) %all-to-all-start) | async-done | bytes 160 | tf_op jit(solution)/shard_map/all_to_all | solution.py:117
  17.8 0.1 copy.11
  17.9 1.0 select_select_fusion
  18.9 3.6 %all-to-all-start.1 = ((bf16[16,128,128]{2,1,0:T(8,128)(2,1)}), bf16[16,128,128]{2,1,0:T(8,128)(2,1)S(1)}, u32[]{:S(2)}, u32[]{:S(2)}) async-start(bf16[16,128,128]{2,1,0:T(8,128)(2,1)} %select_select_fusion), calls=%async_computation.1 | async-start | bytes 1048576 | tf_op jit(solution)/shard_map/all_to_all | solution.py:122
  23.8 12.7 %all-to-all-done.1.recv_ref = bf16[16,128,128]{2,1,0:T(8,128)(2,1)S(1)} async-done(((bf16[16,128,128]{2,1,0:T(8,128)(2,1)}), bf16[16,128,128]{2,1,0:T(8,128)(2,1)S(1)}, u32[]{:S(2)}, u32[]{:S(2)}) %all-to-all-start.1) | async-done | bytes 524320 | tf_op jit(solution)/shard_map/all_to_all | solution.py:122
  36.4 0.0 copy-start
  36.4 2.2 %copy-done = bf16[4,32,128,128]{3,2,1,0:T(8,128)(2,1)S(1)} copy-done((bf16[4,32,128,128]{3,2,1,0:T(8,128)(2,1)S(1)}, bf16[4,32,128,128]{3,2,1,0:T(8,128)(2,1)}, u32[]{:S(2)}) %copy-start) | copy-done | bytes 4194328
  38.6 0.0 copy-start.1
  38.6 3.1 %shard_map.73 = (bf16[4,128,128]{2,1,0:T(8,128)(2,1)S(1)}, bf16[16,128,128]{2,1,0:T(8,128)(2,1)S(1)}) custom-call(s32[4,32]{1,0:T(4,128)} %cols_hbm.7, s32[16]{0:T(128)S(1)} %get-tuple-element.28.pick_ref, f32[4,32]{1,0:T(4,128)} %scl_hbm.7, f32[1]{0:T(128)S(6)} %copy.12.c_ref, f32[1]{0:T(128)S(6)} %copy.13.w_ref, ...), custom_call_target="tpu_custom_call" | custom-call | flops 536870912 | bytes 5636096 | tf_op jit(solution)/shard_map/pallas_call | solution.py:83
  41.7 17.5 %all_to_all.37.recv_ref = bf16[16,128,128]{2,1,0:T(8,128)(2,1)S(1)} all-to-all(bf16[16,128,128]{2,1,0:T(8,128)(2,1)S(1)} %get-tuple-element.12), channel_id=1, replica_groups=mesh['rows'=16,'vecs'=2] {'rows'}, dimensions={0} | all-to-all | bytes 1048576 | tf_op jit(solution)/shard_map/all_to_all | solution.py:122
  59.3 0.0 copy-done.2
  59.3 0.0 copy-done.1
  59.3 2.9 %shard_map.74 = (bf16[4,128,128]{2,1,0:T(8,128)(2,1)S(1)}, bf16[16,128,128]{2,1,0:T(8,128)(2,1)S(1)}) custom-call(s32[4,32]{1,0:T(4,128)} %cols_hbm.7, s32[16]{0:T(128)S(1)} %get-tuple-element.28.pick_ref, f32[4,32]{1,0:T(4,128)} %scl_hbm.7, f32[1]{0:T(128)S(6)} %copy.12.c_ref, f32[1]{0:T(128)S(6)} %copy.13.w_ref, ...), custom_call_target="tpu_custom_call" | custom-call | flops 536870912 | bytes 5636096 | tf_op jit(solution)/shard_map/pallas_call | solution.py:83
  62.2 17.5 %all_to_all.38.recv_ref = bf16[16,128,128]{2,1,0:T(8,128)(2,1)S(1)} all-to-all(bf16[16,128,128]{2,1,0:T(8,128)(2,1)S(1)} %get-tuple-element.14), channel_id=1, replica_groups=mesh['rows'=16,'vecs'=2] {'rows'}, dimensions={0} | all-to-all | bytes 1048576 | tf_op jit(solution)/shard_map/all_to_all | solution.py:122
  79.7 2.9 %shard_map.75 = (bf16[4,128,128]{2,1,0:T(8,128)(2,1)S(1)}, bf16[16,128,128]{2,1,0:T(8,128)(2,1)S(1)}) custom-call(s32[4,32]{1,0:T(4,128)} %cols_hbm.7, s32[16]{0:T(128)S(1)} %get-tuple-element.28.pick_ref, f32[4,32]{1,0:T(4,128)} %scl_hbm.7, f32[1]{0:T(128)S(6)} %copy.12.c_ref, f32[1]{0:T(128)S(6)} %copy.13.w_ref, ...), custom_call_target="tpu_custom_call" | custom-call | flops 536870912 | bytes 5636096 | tf_op jit(solution)/shard_map/pallas_call | solution.py:83
  82.6 17.4 %all_to_all.39.recv_ref = bf16[16,128,128]{2,1,0:T(8,128)(2,1)S(1)} all-to-all(bf16[16,128,128]{2,1,0:T(8,128)(2,1)S(1)} %get-tuple-element.16), channel_id=1, replica_groups=mesh['rows'=16,'vecs'=2] {'rows'}, dimensions={0} | all-to-all | bytes 1048576 | tf_op jit(solution)/shard_map/all_to_all | solution.py:122
  100.0 3.8 %shard_map.76 = (bf16[4,128,128]{2,1,0:T(8,128)(2,1)}, bf16[16,128,128]{2,1,0:T(8,128)(2,1)}) custom-call(s32[4,32]{1,0:T(4,128)} %cols_hbm.7, s32[16]{0:T(128)S(1)} %get-tuple-element.29.pick_ref, f32[4,32]{1,0:T(4,128)} %scl_hbm.7, f32[1]{0:T(128)S(6)} %copy.12.c_ref, f32[1]{0:T(128)S(6)} %copy.13.w_ref, bf16[16,128,128]{2,1,0:T(8,128)(2,1)S(1)} %all_to_all.39.recv_ref, ...), custom_call_target="tpu_custom_call" | custom-call | flops 536870912 | bytes 5636096 | tf_op jit(solution)/shard_map/pallas_call | solution.py:83
  103.8 3.9 %all-to-all-start.5 = ((bf16[16,128,128]{2,1,0:T(8,128)(2,1)}), bf16[16,128,128]{2,1,0:T(8,128)(2,1)S(1)}, u32[]{:S(2)}, u32[]{:S(2)}) async-start(bf16[16,128,128]{2,1,0:T(8,128)(2,1)} %get-tuple-element.18), calls=%async_computation.5 | async-start | bytes 1048576 | tf_op jit(solution)/shard_map/all_to_all | solution.py:122
  107.7 13.7 %all-to-all-done.5 = bf16[16,128,128]{2,1,0:T(8,128)(2,1)S(1)} async-done(((bf16[16,128,128]{2,1,0:T(8,128)(2,1)}), bf16[16,128,128]{2,1,0:T(8,128)(2,1)S(1)}, u32[]{:S(2)}, u32[]{:S(2)}) %all-to-all-start.5) | async-done | bytes 524320 | tf_op jit(solution)/shard_map/all_to_all | solution.py:122
  121.3 1.2 gather_fusion
  (4 shorter events, 0.0 us)
Async XLA Ops:
  0.0 59.3 %copy-start.2 = (bf16[512,128]{1,0:T(8,128)(2,1)S(1)}, bf16[512,128]{1,0:T(8,128)(2,1)}, u32[]{:S(2)}) copy-start(bf16[512,128]{1,0:T(8,128)(2,1)} %param.7) | copy-start | bytes 393220
  2.3 15.5 %all-to-all-start = ((s32[16,1,2]{2,1,0:T(1,128)}), s32[16,1,2]{2,1,0:T(1,128)S(1)}, u32[]{:S(2)}, u32[]{:S(2)}) async-start(s32[16,1,2]{2,1,0:T(1,128)} %copy.10), calls=%async_computation | async-start | bytes 16384 | tf_op jit(solution)/shard_map/all_to_all | solution.py:117
  18.9 17.6 %all-to-all-start.1 = ((bf16[16,128,128]{2,1,0:T(8,128)(2,1)}), bf16[16,128,128]{2,1,0:T(8,128)(2,1)S(1)}, u32[]{:S(2)}, u32[]{:S(2)}) async-start(bf16[16,128,128]{2,1,0:T(8,128)(2,1)} %select_select_fusion), calls=%async_computation.1 | async-start | bytes 1048576 | tf_op jit(solution)/shard_map/all_to_all | solution.py:122
  36.4 2.2 %copy-start = (bf16[4,32,128,128]{3,2,1,0:T(8,128)(2,1)S(1)}, bf16[4,32,128,128]{3,2,1,0:T(8,128)(2,1)}, u32[]{:S(2)}) copy-start(bf16[4,32,128,128]{3,2,1,0:T(8,128)(2,1)} %blk_ref.7) | copy-start | bytes 12582916
  38.6 20.6 %copy-start.1 = (bf16[4,32,128,128]{3,2,1,0:T(8,128)(2,1)S(1)}, bf16[4,32,128,128]{3,2,1,0:T(8,128)(2,1)}, u32[]{:S(2)}) copy-start(bf16[4,32,128,128]{3,2,1,0:T(8,128)(2,1)} %blk_ref.7) | copy-start | bytes 12582916
  103.8 17.5 %all-to-all-start.5 = ((bf16[16,128,128]{2,1,0:T(8,128)(2,1)}), bf16[16,128,128]{2,1,0:T(8,128)(2,1)S(1)}, u32[]{:S(2)}, u32[]{:S(2)}) async-start(bf16[16,128,128]{2,1,0:T(8,128)(2,1)} %get-tuple-element.18), calls=%async_computation.5 | async-start | bytes 1048576 | tf_op jit(solution)/shard_map/all_to_all | solution.py:122

commit v11 on v10

--- a/solution.py
+++ b/solution.py
@@ -16,7 +16,39 @@
     return jnp.max(jnp.where(hit, (index % local_rows)[None], 0), axis=tuple(range(1, index.ndim + 1)))
 
 
-def step_kernel(first, cols_hbm, pick_ref, scl_hbm, c_ref, w_ref, recv_ref, blk_ref, cur_hbm, *rest):
+def step_kernel(first, cols_ref, pick_ref, scl_ref, c_ref, w_ref, recv_ref, blk_ref, cur_ref, *rest):
+    if first:
+        out_ref, go_ref = rest
+    else:
+        prev_ref, out_ref, go_ref = rest
+    local_rows, per_row = cols_ref.shape
+    shift = c_ref[0]
+    width = w_ref[0]
+    for r in range(local_rows):
+
+        def body(k, acc):
+            s = cols_ref[r, k] // local_rows
+            prod = jnp.dot(blk_ref[r, k], recv_ref[s], preferred_element_type=jnp.float32)
+            return acc + scl_ref[r, k] * prod
+
+        acc = lax.fori_loop(
+            0, per_row, body, jnp.zeros(out_ref.shape[1:], jnp.float32), unroll=True
+        )
+        cur = cur_ref[r].astype(jnp.float32)
+        if first:
+            new = (acc - shift * cur) / width
+        else:
+            new = 2.0 * (acc - shift * cur) / width - prev_ref[r].astype(jnp.float32)
+        out_ref[r] = new.astype(out_ref.dtype)
+
+    def put(e, carry):
+        go_ref[e] = out_ref[pick_ref[e]]
+        return carry
+
+    lax.fori_loop(0, go_ref.shape[0], put, 0)
+
+
+def first_step_kernel(first, cols_hbm, pick_ref, scl_hbm, c_ref, w_ref, recv_ref, blk_ref, cur_hbm, *rest):
     if first:
         out_ref, go_ref, cols_ref, scl_ref, cur_ref, sems = rest
     else:
@@ -60,6 +92,31 @@
 
 
 def chebyshev_step(columns, pick, scales, center, half_width, received, blocks, cur, prev):
+    local_rows, per_row, orbitals, _ = blocks.shape
+    width = cur.shape[2]
+    nrows = pick.shape[0]
+    first = prev is None
+    smem = pl.BlockSpec(memory_space=pltpu.SMEM)
+    vmem = pl.BlockSpec(memory_space=pltpu.VMEM)
+    args = [columns, pick, scales, center, half_width, received, blocks, cur]
+    if not first:
+        args.append(prev)
+    flops = 2 * local_rows * per_row * orbitals * orbitals * width
+    nbytes = blocks.size * 2 + 2 * received.size * 2 + 3 * cur.size * 2
+    return pl.pallas_call(
+        functools.partial(step_kernel, first),
+        out_shape=(
+            jax.ShapeDtypeStruct(cur.shape, jnp.bfloat16),
+            jax.ShapeDtypeStruct((nrows, orbitals, width), jnp.bfloat16),
+        ),
+        in_specs=[smem] * 5 + [vmem] * (len(args) - 5),
+        out_specs=(vmem, vmem),
+        compiler_params=pltpu.CompilerParams(vmem_limit_bytes=8 * 1024 * 1024),
+        cost_estimate=pl.CostEstimate(flops=flops, bytes_accessed=nbytes, transcendentals=0),
+    )(*args)
+
+
+def first_chebyshev_step(columns, pick, scales, center, half_width, received, blocks, cur, prev):
     local_rows, per_row, orbitals, _ = blocks.shape
     width = cur.shape[2]
     nrows = pick.shape[0]
@@ -81,7 +138,7 @@
     flops = 2 * local_rows * per_row * orbitals * orbitals * width
     nbytes = blocks.size * 2 + 2 * received.size * 2 + 3 * cur.size * 2
     return pl.pallas_call(
-        functools.partial(step_kernel, first),
+        functools.partial(first_step_kernel, first),
         out_shape=(
             jax.ShapeDtypeStruct(cur.shape, jnp.bfloat16),
             jax.ShapeDtypeStruct((nrows, orbitals, width), jnp.bfloat16),
@@ -123,7 +180,7 @@
 
     blocks = pltpu.with_memory_space_constraint(blocks, pltpu.VMEM)
     previous = vectors.reshape(local_rows, orbitals, group_width)
-    current, outgoing = chebyshev_step(
+    current, outgoing = first_chebyshev_step(
         columns, wanted, scales, center, half_width,
         exchange(select_rows(previous, wanted)), blocks, previous, None,
     )

time: 123 us -> 121 us (0.984)
  Pallas kernels: 12.7 us -> 10.1 us
    pallas_call x4 -> x3, Pallas kernels: 12.7 us -> 7.05 us  [chebyshev_step(): pl.pallas_call(functools.partial(step_kernel, first), out_shape=(jax.Shap...]
    pallas_call x0 -> x1, Pallas kernels: none -> 3.08 us  [first_chebyshev_step(): pl.pallas_call(functools.partial(first_step_kernel, first), out_shape=(ja...]
where the time goes in v11:
time: 121 us; the launch traced here: 120 us
  blocking collectives  52.4 us (43%)
  waiting for transfers between devices  32.7 us (27%)
  starting transfers between devices  15.7 us (13%)
  Pallas kernels  10.1 us (8%)
  local copies, waits for them, and re-layouts  5.01 us (4%)
  other arithmetic  2.59 us (2%)
  between operations  1.39 us (1%)
    all_to_all x3, blocking collectives, exchange(): lax.all_to_all(outgoing, 'rows', split_axis=0, concat_axis=0, tiled=True)  52.4 us
    all_to_all x2, waiting for transfers between devices, exchange(): lax.all_to_all(outgoing, 'rows', split_axis=0, concat_axis=0, tiled=True)  26.3 us
    all_to_all x1, starting transfers between devices, on_device(): lax.all_to_all(asked, 'rows', split_axis=0, concat_axis=0, tiled=True)  8.32 us
    all_to_all x2, starting transfers between devices, exchange(): lax.all_to_all(outgoing, 'rows', split_axis=0, concat_axis=0, tiled=True)  7.42 us
    pallas_call x3, Pallas kernels, chebyshev_step(): pl.pallas_call(functools.partial(step_kernel, first), out_shape=(jax.Shap...  7.05 us
    all_to_all x1, waiting for transfers between devices, on_device(): lax.all_to_all(asked, 'rows', split_axis=0, concat_axis=0, tiled=True)  6.37 us
    pallas_call x1, Pallas kernels, first_chebyshev_step(): pl.pallas_call(functools.partial(first_step_kernel, first), out_shape=(ja...  3.08 us
  transfers between devices with their start and end apart: 3, of which 3 were waited for; matrix products, arithmetic and copies ran while one was open for 1% of the time, Pallas kernels for 0%

profile of v11, /device:TPU:0, one launch (start us, length us, event | category | flops | bytes accessed | tf_op | source)
XLA Modules:
  0.0 120.0 jit_solution(14692592845187159088)
XLA Ops:
  0.0 0.0 copy-start.3
  0.0 0.0 copy-start.2
  0.0 0.0 copy-start.4
  0.0 0.7 and_select_fusion.1
  0.7 0.7 add_select_fusion.1
  1.4 0.1 select_reduce_fusion.1
  1.5 0.1 select_reduce_fusion
  1.6 0.7 copy.10
  2.3 8.3 %all-to-all-start = ((s32[16,1,2]{2,1,0:T(1,128)}), s32[16,1,2]{2,1,0:T(1,128)S(1)}, u32[]{:S(2)}, u32[]{:S(2)}) async-start(s32[16,1,2]{2,1,0:T(1,128)} %copy.10), calls=%async_computation | async-start | bytes 16384 | tf_op jit(solution)/shard_map/all_to_all | solution.py:174
  10.6 0.8 fusion.1
  11.5 6.4 %all-to-all-done = s32[16,1,2]{2,1,0:T(1,128)S(1)} async-done(((s32[16,1,2]{2,1,0:T(1,128)}), s32[16,1,2]{2,1,0:T(1,128)S(1)}, u32[]{:S(2)}, u32[]{:S(2)}) %all-to-all-start) | async-done | bytes 160 | tf_op jit(solution)/shard_map/all_to_all | solution.py:174
  17.8 0.1 copy.11
  17.9 1.0 select_select_fusion
  18.9 3.6 %all-to-all-start.1 = ((bf16[16,128,128]{2,1,0:T(8,128)(2,1)}), bf16[16,128,128]{2,1,0:T(8,128)(2,1)S(1)}, u32[]{:S(2)}, u32[]{:S(2)}) async-start(bf16[16,128,128]{2,1,0:T(8,128)(2,1)} %select_select_fusion), calls=%async_computation.1 | async-start | bytes 1048576 | tf_op jit(solution)/shard_map/all_to_all | solution.py:179
  23.8 12.7 %all-to-all-done.1.recv_ref = bf16[16,128,128]{2,1,0:T(8,128)(2,1)S(1)} async-done(((bf16[16,128,128]{2,1,0:T(8,128)(2,1)}), bf16[16,128,128]{2,1,0:T(8,128)(2,1)S(1)}, u32[]{:S(2)}, u32[]{:S(2)}) %all-to-all-start.1) | async-done | bytes 524320 | tf_op jit(solution)/shard_map/all_to_all | solution.py:179
  36.4 0.0 copy-start
  36.4 2.2 %copy-done = bf16[4,32,128,128]{3,2,1,0:T(8,128)(2,1)S(1)} copy-done((bf16[4,32,128,128]{3,2,1,0:T(8,128)(2,1)S(1)}, bf16[4,32,128,128]{3,2,1,0:T(8,128)(2,1)}, u32[]{:S(2)}) %copy-start) | copy-done | bytes 4194328
  38.6 0.0 copy-start.1
  38.6 3.1 %shard_map.73 = (bf16[4,128,128]{2,1,0:T(8,128)(2,1)S(1)}, bf16[16,128,128]{2,1,0:T(8,128)(2,1)S(1)}) custom-call(s32[4,32]{1,0:T(4,128)} %cols_ref.5, s32[16]{0:T(128)S(1)} %get-tuple-element.28.pick_ref, f32[4,32]{1,0:T(4,128)} %scl_ref.5, f32[1]{0:T(128)S(6)} %copy.12.c_ref, f32[1]{0:T(128)S(6)} %copy.13.w_ref, ...), custom_call_target="tpu_custom_call" | custom-call | flops 536870912 | bytes 5636096 | tf_op jit(solution)/shard_map/pallas_call | solution.py:140
  41.7 17.5 %all_to_all.37.recv_ref = bf16[16,128,128]{2,1,0:T(8,128)(2,1)S(1)} all-to-all(bf16[16,128,128]{2,1,0:T(8,128)(2,1)S(1)} %get-tuple-element.12), channel_id=1, replica_groups=mesh['rows'=16,'vecs'=2] {'rows'}, dimensions={0} | all-to-all | bytes 1048576 | tf_op jit(solution)/shard_map/all_to_all | solution.py:179
  59.3 0.0 copy-done.3
  59.3 0.0 copy-done.2
  59.3 0.0 copy-done.4
  59.3 0.0 copy-done.1
  59.3 2.1 %shard_map.74 = (bf16[4,128,128]{2,1,0:T(8,128)(2,1)S(1)}, bf16[16,128,128]{2,1,0:T(8,128)(2,1)S(1)}) custom-call(s32[4,32]{1,0:T(4,128)S(1)} %copy-done.3, s32[16]{0:T(128)S(1)} %get-tuple-element.28.pick_ref, f32[4,32]{1,0:T(4,128)S(1)} %copy-done.4, f32[1]{0:T(128)S(6)} %copy.12.c_ref, f32[1]{0:T(128)S(6)} %copy.13.w_ref, ...), custom_call_target="tpu_custom_call" | custom-call | flops 536870912 | bytes 5636096 | tf_op jit(solution)/shard_map/pallas_call | solution.py:106
  61.4 17.5 %all_to_all.38.recv_ref = bf16[16,128,128]{2,1,0:T(8,128)(2,1)S(1)} all-to-all(bf16[16,128,128]{2,1,0:T(8,128)(2,1)S(1)} %get-tuple-element.14), channel_id=1, replica_groups=mesh['rows'=16,'vecs'=2] {'rows'}, dimensions={0} | all-to-all | bytes 1048576 | tf_op jit(solution)/shard_map/all_to_all | solution.py:179
  78.9 2.1 %shard_map.75 = (bf16[4,128,128]{2,1,0:T(8,128)(2,1)S(1)}, bf16[16,128,128]{2,1,0:T(8,128)(2,1)S(1)}) custom-call(s32[4,32]{1,0:T(4,128)S(1)} %copy-done.3, s32[16]{0:T(128)S(1)} %get-tuple-element.28.pick_ref, f32[4,32]{1,0:T(4,128)S(1)} %copy-done.4, f32[1]{0:T(128)S(6)} %copy.12.c_ref, f32[1]{0:T(128)S(6)} %copy.13.w_ref, ...), custom_call_target="tpu_custom_call" | custom-call | flops 536870912 | bytes 5636096 | tf_op jit(solution)/shard_map/pallas_call | solution.py:106
  80.9 17.4 %all_to_all.39.recv_ref = bf16[16,128,128]{2,1,0:T(8,128)(2,1)S(1)} all-to-all(bf16[16,128,128]{2,1,0:T(8,128)(2,1)S(1)} %get-tuple-element.16), channel_id=1, replica_groups=mesh['rows'=16,'vecs'=2] {'rows'}, dimensions={0} | all-to-all | bytes 1048576 | tf_op jit(solution)/shard_map/all_to_all | solution.py:179
  98.3 2.9 %shard_map.76 = (bf16[4,128,128]{2,1,0:T(8,128)(2,1)}, bf16[16,128,128]{2,1,0:T(8,128)(2,1)}) custom-call(s32[4,32]{1,0:T(4,128)S(1)} %copy-done.3, s32[16]{0:T(128)S(1)} %get-tuple-element.29.pick_ref, f32[4,32]{1,0:T(4,128)S(1)} %copy-done.4, f32[1]{0:T(128)S(6)} %copy.12.c_ref, f32[1]{0:T(128)S(6)} %copy.13.w_ref, ...), custom_call_target="tpu_custom_call" | custom-call | flops 536870912 | bytes 5636096 | tf_op jit(solution)/shard_map/pallas_call | solution.py:106
  101.2 3.9 %all-to-all-start.5 = ((bf16[16,128,128]{2,1,0:T(8,128)(2,1)}), bf16[16,128,128]{2,1,0:T(8,128)(2,1)S(1)}, u32[]{:S(2)}, u32[]{:S(2)}) async-start(bf16[16,128,128]{2,1,0:T(8,128)(2,1)} %get-tuple-element.18), calls=%async_computation.5 | async-start | bytes 1048576 | tf_op jit(solution)/shard_map/all_to_all | solution.py:179
  105.1 13.7 %all-to-all-done.5 = bf16[16,128,128]{2,1,0:T(8,128)(2,1)S(1)} async-done(((bf16[16,128,128]{2,1,0:T(8,128)(2,1)}), bf16[16,128,128]{2,1,0:T(8,128)(2,1)S(1)}, u32[]{:S(2)}, u32[]{:S(2)}) %all-to-all-start.5) | async-done | bytes 524320 | tf_op jit(solution)/shard_map/all_to_all | solution.py:179
  118.8 1.2 %gather_fusion = bf16[4,128,128]{2,1,0:T(8,128)(2,1)} fusion(bf16[16,128,128]{2,1,0:T(8,128)(2,1)S(1)} %all-to-all-done.5, s32[1024]{0:T(1024)S(1)} %pad_clamp_fusion), kind=kCustom, calls=%fused_computation | custom fusion | bytes 262160 | tf_op jit(solution)/shard_map/jit(_take)/gather | solution.py:194
  (4 shorter events, 0.0 us)
Async XLA Ops:
  0.0 59.3 %copy-start.3 = (s32[4,32]{1,0:T(4,128)S(1)}, s32[4,32]{1,0:T(4,128)}, u32[]{:S(2)}) copy-start(s32[4,32]{1,0:T(4,128)} %cols_ref.5) | copy-start | bytes 1540
  0.0 59.3 %copy-start.2 = (bf16[512,128]{1,0:T(8,128)(2,1)S(1)}, bf16[512,128]{1,0:T(8,128)(2,1)}, u32[]{:S(2)}) copy-start(bf16[512,128]{1,0:T(8,128)(2,1)} %param.7) | copy-start | bytes 393220
  0.0 59.3 %copy-start.4 = (f32[4,32]{1,0:T(4,128)S(1)}, f32[4,32]{1,0:T(4,128)}, u32[]{:S(2)}) copy-start(f32[4,32]{1,0:T(4,128)} %scl_ref.5) | copy-start | bytes 1540
  2.3 15.5 %all-to-all-start = ((s32[16,1,2]{2,1,0:T(1,128)}), s32[16,1,2]{2,1,0:T(1,128)S(1)}, u32[]{:S(2)}, u32[]{:S(2)}) async-start(s32[16,1,2]{2,1,0:T(1,128)} %copy.10), calls=%async_computation | async-start | bytes 16384 | tf_op jit(solution)/shard_map/all_to_all | solution.py:174
  18.9 17.6 %all-to-all-start.1 = ((bf16[16,128,128]{2,1,0:T(8,128)(2,1)}), bf16[16,128,128]{2,1,0:T(8,128)(2,1)S(1)}, u32[]{:S(2)}, u32[]{:S(2)}) async-start(bf16[16,128,128]{2,1,0:T(8,128)(2,1)} %select_select_fusion), calls=%async_computation.1 | async-start | bytes 1048576 | tf_op jit(solution)/shard_map/all_to_all | solution.py:179
  36.4 2.2 %copy-start = (bf16[4,32,128,128]{3,2,1,0:T(8,128)(2,1)S(1)}, bf16[4,32,128,128]{3,2,1,0:T(8,128)(2,1)}, u32[]{:S(2)}) copy-start(bf16[4,32,128,128]{3,2,1,0:T(8,128)(2,1)} %blk_ref.7) | copy-start | bytes 12582916
  38.6 20.7 %copy-start.1 = (bf16[4,32,128,128]{3,2,1,0:T(8,128)(2,1)S(1)}, bf16[4,32,128,128]{3,2,1,0:T(8,128)(2,1)}, u32[]{:S(2)}) copy-start(bf16[4,32,128,128]{3,2,1,0:T(8,128)(2,1)} %blk_ref.7) | copy-start | bytes 12582916
  101.2 17.5 %all-to-all-start.5 = ((bf16[16,128,128]{2,1,0:T(8,128)(2,1)}), bf16[16,128,128]{2,1,0:T(8,128)(2,1)S(1)}, u32[]{:S(2)}, u32[]{:S(2)}) async-start(bf16[16,128,128]{2,1,0:T(8,128)(2,1)} %get-tuple-element.18), calls=%async_computation.5 | async-start | bytes 1048576 | tf_op jit(solution)/shard_map/all_to_all | solution.py:179

commit v12 on v11

--- a/solution.py
+++ b/solution.py
@@ -191,7 +191,7 @@
         )
         previous, current = (current, upcoming)
     arrived = exchange(outgoing)
-    placed = jnp.take(arrived, owners // local_rows, axis=0, mode="clip")
+    placed = select_rows(arrived, owners // local_rows)
     return placed.reshape(local_rows * orbitals, group_width)
 
 

time: 121 us -> 125 us (1.033)
  blocking collectives: 52.4 us -> 35 us
  waiting for transfers between devices: 32.7 us -> 45.9 us
  starting transfers between devices: 15.7 us -> 19.6 us
  other arithmetic: 2.59 us -> 5.07 us
  local copies, waits for them, and re-layouts: 5.01 us -> 6.6 us
    all_to_all x3 -> x2, blocking collectives: 52.4 us -> 35 us  [exchange(): lax.all_to_all(outgoing, 'rows', split_axis=0, concat_axis=0, tiled=True)]
    all_to_all x2 -> x3, waiting for transfers between devices: 26.3 us -> 39.5 us  [exchange(): lax.all_to_all(outgoing, 'rows', split_axis=0, concat_axis=0, tiled=True)]
    all_to_all x2 -> x3, starting transfers between devices: 7.42 us -> 11.3 us  [exchange(): lax.all_to_all(outgoing, 'rows', split_axis=0, concat_axis=0, tiled=True)]
    unnamed x10 -> x12, local copies, waits for them, and re-layouts: 2.2 us -> 4.39 us
    select_n x1 -> x2, other arithmetic: 0.97 us -> 2.77 us  [select_rows(): jnp.where((index == atom)[:, None, None], panels[atom][None], chosen)]
  transfers between devices with their start and end apart: 3 -> 4, of which waited for: 3 -> 4; matrix products, arithmetic and copies ran while one was open for 1% -> 1% of each run, Pallas kernels for 0% -> 0%
where the time goes in v12:
time: 125 us
  waiting for transfers between devices  45.9 us (37%)
  blocking collectives  35 us (28%)
  starting transfers between devices  19.6 us (16%)
  Pallas kernels  11 us (9%)
  local copies, waits for them, and re-layouts  6.6 us (5%)
  other arithmetic  5.07 us (4%)
  between operations  1.4 us (1%)
    all_to_all x3, waiting for transfers between devices, exchange(): lax.all_to_all(outgoing, 'rows', split_axis=0, concat_axis=0, tiled=True)  39.5 us
    all_to_all x2, blocking collectives, exchange(): lax.all_to_all(outgoing, 'rows', split_axis=0, concat_axis=0, tiled=True)  35 us
    all_to_all x3, starting transfers between devices, exchange(): lax.all_to_all(outgoing, 'rows', split_axis=0, concat_axis=0, tiled=True)  11.3 us
    all_to_all x1, starting transfers between devices, on_device(): lax.all_to_all(asked, 'rows', split_axis=0, concat_axis=0, tiled=True)  8.32 us
    pallas_call x3, Pallas kernels, chebyshev_step(): pl.pallas_call(functools.partial(step_kernel, first), out_shape=(jax.Shap...  7.91 us
    all_to_all x1, waiting for transfers between devices, on_device(): lax.all_to_all(asked, 'rows', split_axis=0, concat_axis=0, tiled=True)  6.37 us
    unnamed x12, local copies, waits for them, and re-layouts  4.39 us
    pallas_call x1, Pallas kernels, first_chebyshev_step(): pl.pallas_call(functools.partial(first_step_kernel, first), out_shape=(ja...  3.08 us
  transfers between devices with their start and end apart: 4, of which 4 were waited for; matrix products, arithmetic and copies ran while one was open for 1% of the time, Pallas kernels for 0%

profile of v12, /device:TPU:0, one launch (start us, length us, event | category | flops | bytes accessed | tf_op | source)
XLA Modules:
  0.0 124.6 jit_solution(1130349139901852193)
XLA Ops:
  0.0 0.7 broadcast_compare_fusion.15
  0.7 0.7 and_select_fusion
  1.4 0.7 add_select_fusion.1
  2.1 0.1 select_reduce_fusion
  2.2 0.1 select_reduce_fusion.1
  2.3 0.7 copy.10
  3.0 8.3 %all-to-all-start = ((s32[16,1,2]{2,1,0:T(1,128)}), s32[16,1,2]{2,1,0:T(1,128)S(1)}, u32[]{:S(2)}, u32[]{:S(2)}) async-start(s32[16,1,2]{2,1,0:T(1,128)} %copy.10), calls=%async_computation | async-start | bytes 16384 | tf_op jit(solution)/shard_map/all_to_all | solution.py:174
  11.3 0.8 fusion.15
  12.1 6.4 %all-to-all-done = s32[16,1,2]{2,1,0:T(1,128)S(1)} async-done(((s32[16,1,2]{2,1,0:T(1,128)}), s32[16,1,2]{2,1,0:T(1,128)S(1)}, u32[]{:S(2)}, u32[]{:S(2)}) %all-to-all-start) | async-done | bytes 160 | tf_op jit(solution)/shard_map/all_to_all | solution.py:174
  18.5 0.1 copy.11
  18.6 1.0 select_select_fusion
  19.6 3.6 %all-to-all-start.1 = ((bf16[16,128,128]{2,1,0:T(8,128)(2,1)}), bf16[16,128,128]{2,1,0:T(8,128)(2,1)S(1)}, u32[]{:S(2)}, u32[]{:S(2)}) async-start(bf16[16,128,128]{2,1,0:T(8,128)(2,1)} %select_select_fusion), calls=%async_computation.1 | async-start | bytes 1048576 | tf_op jit(solution)/shard_map/all_to_all | solution.py:179
  24.4 12.7 %all-to-all-done.1.recv_ref = bf16[16,128,128]{2,1,0:T(8,128)(2,1)S(1)} async-done(((bf16[16,128,128]{2,1,0:T(8,128)(2,1)}), bf16[16,128,128]{2,1,0:T(8,128)(2,1)S(1)}, u32[]{:S(2)}, u32[]{:S(2)}) %all-to-all-start.1) | async-done | bytes 524320 | tf_op jit(solution)/shard_map/all_to_all | solution.py:179
  37.1 2.2 %copy-done = bf16[4,32,128,128]{3,2,1,0:T(8,128)(2,1)S(1)} copy-done((bf16[4,32,128,128]{3,2,1,0:T(8,128)(2,1)S(1)}, bf16[4,32,128,128]{3,2,1,0:T(8,128)(2,1)}, u32[]{:S(2)}) %copy-start) | copy-done | bytes 4194328
  39.3 3.1 %shard_map.73 = (bf16[4,128,128]{2,1,0:T(8,128)(2,1)S(1)}, bf16[16,128,128]{2,1,0:T(8,128)(2,1)S(1)}) custom-call(s32[4,32]{1,0:T(4,128)} %cols_ref.5, s32[16]{0:T(128)S(1)} %get-tuple-element.46.pick_ref, f32[4,32]{1,0:T(4,128)} %scl_ref.5, f32[1]{0:T(128)S(6)} %copy.12.c_ref, f32[1]{0:T(128)S(6)} %copy.13.w_ref, ...), custom_call_target="tpu_custom_call" | custom-call | flops 536870912 | bytes 5636096 | tf_op jit(solution)/shard_map/pallas_call | solution.py:140
  42.4 17.5 %all_to_all.37.recv_ref = bf16[16,128,128]{2,1,0:T(8,128)(2,1)S(1)} all-to-all(bf16[16,128,128]{2,1,0:T(8,128)(2,1)S(1)} %get-tuple-element.12), channel_id=1, replica_groups=mesh['rows'=16,'vecs'=2] {'rows'}, dimensions={0} | all-to-all | bytes 1048576 | tf_op jit(solution)/shard_map/all_to_all | solution.py:179
  60.0 2.1 %shard_map.74 = (bf16[4,128,128]{2,1,0:T(8,128)(2,1)S(1)}, bf16[16,128,128]{2,1,0:T(8,128)(2,1)S(1)}) custom-call(s32[4,32]{1,0:T(4,128)S(1)} %copy-done.4, s32[16]{0:T(128)S(1)} %get-tuple-element.46.pick_ref, f32[4,32]{1,0:T(4,128)S(1)} %copy-done.5, f32[1]{0:T(128)S(6)} %copy.12.c_ref, f32[1]{0:T(128)S(6)} %copy.13.w_ref, ...), custom_call_target="tpu_custom_call" | custom-call | flops 536870912 | bytes 5636096 | tf_op jit(solution)/shard_map/pallas_call | solution.py:106
  62.0 17.5 %all_to_all.38.recv_ref = bf16[16,128,128]{2,1,0:T(8,128)(2,1)S(1)} all-to-all(bf16[16,128,128]{2,1,0:T(8,128)(2,1)S(1)} %get-tuple-element.14), channel_id=1, replica_groups=mesh['rows'=16,'vecs'=2] {'rows'}, dimensions={0} | all-to-all | bytes 1048576 | tf_op jit(solution)/shard_map/all_to_all | solution.py:179
  79.5 2.9 %shard_map.75 = (bf16[4,128,128]{2,1,0:T(8,128)(2,1)S(1)}, bf16[16,128,128]{2,1,0:T(8,128)(2,1)}) custom-call(s32[4,32]{1,0:T(4,128)S(1)} %copy-done.4, s32[16]{0:T(128)S(1)} %get-tuple-element.46.pick_ref, f32[4,32]{1,0:T(4,128)S(1)} %copy-done.5, f32[1]{0:T(128)S(6)} %copy.12.c_ref, f32[1]{0:T(128)S(6)} %copy.13.w_ref, ...), custom_call_target="tpu_custom_call" | custom-call | flops 536870912 | bytes 5636096 | tf_op jit(solution)/shard_map/pallas_call | solution.py:106
  82.4 3.8 %all-to-all-start.4 = ((bf16[16,128,128]{2,1,0:T(8,128)(2,1)}), bf16[16,128,128]{2,1,0:T(8,128)(2,1)S(1)}, u32[]{:S(2)}, u32[]{:S(2)}) async-start(bf16[16,128,128]{2,1,0:T(8,128)(2,1)} %get-tuple-element.16), calls=%async_computation.4 | async-start | bytes 1048576 | tf_op jit(solution)/shard_map/all_to_all | solution.py:179
  86.3 0.1 broadcast_bitcast_fusion.12
  86.4 0.1 broadcast_bitcast_fusion.10
  86.4 0.1 broadcast_bitcast_fusion.8
  86.5 13.5 %all-to-all-done.4.recv_ref = bf16[16,128,128]{2,1,0:T(8,128)(2,1)S(1)} async-done(((bf16[16,128,128]{2,1,0:T(8,128)(2,1)}), bf16[16,128,128]{2,1,0:T(8,128)(2,1)S(1)}, u32[]{:S(2)}, u32[]{:S(2)}) %all-to-all-start.4) | async-done | bytes 524320 | tf_op jit(solution)/shard_map/all_to_all | solution.py:179
  100.0 2.2 %copy-done.2 = bf16[4,32,128,128]{3,2,1,0:T(8,128)(2,1)S(1)} copy-done((bf16[4,32,128,128]{3,2,1,0:T(8,128)(2,1)S(1)}, bf16[4,32,128,128]{3,2,1,0:T(8,128)(2,1)}, u32[]{:S(2)}) %copy-start.2) | copy-done | bytes 4194328
  102.2 3.0 %shard_map.76 = (bf16[4,128,128]{2,1,0:T(8,128)(2,1)}, bf16[16,128,128]{2,1,0:T(8,128)(2,1)}) custom-call(s32[4,32]{1,0:T(4,128)S(1)} %copy-done.4, s32[16]{0:T(128)S(1)} %get-tuple-element.47.pick_ref, f32[4,32]{1,0:T(4,128)S(1)} %copy-done.5, f32[1]{0:T(128)S(6)} %copy.12.c_ref, f32[1]{0:T(128)S(6)} %copy.13.w_ref, ...), custom_call_target="tpu_custom_call" | custom-call | flops 536870912 | bytes 5636096 | tf_op jit(solution)/shard_map/pallas_call | solution.py:106
  105.2 3.8 %all-to-all-start.5 = ((bf16[16,128,128]{2,1,0:T(8,128)(2,1)}), bf16[16,128,128]{2,1,0:T(8,128)(2,1)S(1)}, u32[]{:S(2)}, u32[]{:S(2)}) async-start(bf16[16,128,128]{2,1,0:T(8,128)(2,1)} %get-tuple-element.18), calls=%async_computation.5 | async-start | bytes 1048576 | tf_op jit(solution)/shard_map/all_to_all | solution.py:179
  109.1 0.1 broadcast_bitcast_fusion.6
  109.2 0.1 broadcast_bitcast_fusion.4
  109.3 0.1 broadcast_bitcast_fusion.2
  109.4 13.3 %all-to-all-done.5 = bf16[16,128,128]{2,1,0:T(8,128)(2,1)S(1)} async-done(((bf16[16,128,128]{2,1,0:T(8,128)(2,1)}), bf16[16,128,128]{2,1,0:T(8,128)(2,1)S(1)}, u32[]{:S(2)}, u32[]{:S(2)}) %all-to-all-start.5) | async-done | bytes 524320 | tf_op jit(solution)/shard_map/all_to_all | solution.py:179
  122.8 1.8 %fusion.13 = bf16[512,128]{1,0:T(8,128)(2,1)} fusion(pred[512]{0:T(512)(128)(4,1)S(1)} %get-tuple-element.62, pred[512]{0:T(512)(128)(4,1)S(1)} %get-tuple-element.63, pred[512]{0:T(512)(128)(4,1)S(1)} %get-tuple-element.64, pred[512]{0:T(512)(128)(4,1)S(1)} %get-tuple-element.65, pred[512]{0:T(512)(128)(4,1)S(1)} %get-tuple-element.66, ...), kind=kLoop, calls=%fused_computation.15 | loop fusion | flops 983040 | bytes 663040 | tf_op jit(solution)/shard_map/jit(_where)/select_n | solution.py:162
  (17 shorter events, 0.2 us)
Async XLA Ops:
  0.0 59.9 %copy-start.4 = (s32[4,32]{1,0:T(4,128)S(1)}, s32[4,32]{1,0:T(4,128)}, u32[]{:S(2)}) copy-start(s32[4,32]{1,0:T(4,128)} %cols_ref.5) | copy-start | bytes 1540
  0.0 59.9 %copy-start.3 = (bf16[512,128]{1,0:T(8,128)(2,1)S(1)}, bf16[512,128]{1,0:T(8,128)(2,1)}, u32[]{:S(2)}) copy-start(bf16[512,128]{1,0:T(8,128)(2,1)} %param.7) | copy-start | bytes 393220
  0.0 60.0 %copy-start.5 = (f32[4,32]{1,0:T(4,128)S(1)}, f32[4,32]{1,0:T(4,128)}, u32[]{:S(2)}) copy-start(f32[4,32]{1,0:T(4,128)} %scl_ref.5) | copy-start | bytes 1540
  3.0 15.5 %all-to-all-start = ((s32[16,1,2]{2,1,0:T(1,128)}), s32[16,1,2]{2,1,0:T(1,128)S(1)}, u32[]{:S(2)}, u32[]{:S(2)}) async-start(s32[16,1,2]{2,1,0:T(1,128)} %copy.10), calls=%async_computation | async-start | bytes 16384 | tf_op jit(solution)/shard_map/all_to_all | solution.py:174
  19.6 17.6 %all-to-all-start.1 = ((bf16[16,128,128]{2,1,0:T(8,128)(2,1)}), bf16[16,128,128]{2,1,0:T(8,128)(2,1)S(1)}, u32[]{:S(2)}, u32[]{:S(2)}) async-start(bf16[16,128,128]{2,1,0:T(8,128)(2,1)} %select_select_fusion), calls=%async_computation.1 | async-start | bytes 1048576 | tf_op jit(solution)/shard_map/all_to_all | solution.py:179
  37.1 2.2 %copy-start = (bf16[4,32,128,128]{3,2,1,0:T(8,128)(2,1)S(1)}, bf16[4,32,128,128]{3,2,1,0:T(8,128)(2,1)}, u32[]{:S(2)}) copy-start(bf16[4,32,128,128]{3,2,1,0:T(8,128)(2,1)} %blk_ref.7) | copy-start | bytes 12582916
  39.3 20.7 %copy-start.1 = (bf16[4,32,128,128]{3,2,1,0:T(8,128)(2,1)S(1)}, bf16[4,32,128,128]{3,2,1,0:T(8,128)(2,1)}, u32[]{:S(2)}) copy-start(bf16[4,32,128,128]{3,2,1,0:T(8,128)(2,1)} %blk_ref.7) | copy-start | bytes 12582916
  82.4 17.6 %all-to-all-start.4 = ((bf16[16,128,128]{2,1,0:T(8,128)(2,1)}), bf16[16,128,128]{2,1,0:T(8,128)(2,1)S(1)}, u32[]{:S(2)}, u32[]{:S(2)}) async-start(bf16[16,128,128]{2,1,0:T(8,128)(2,1)} %get-tuple-element.16), calls=%async_computation.4 | async-start | bytes 1048576 | tf_op jit(solution)/shard_map/all_to_all | solution.py:179
  100.0 2.2 %copy-start.2 = (bf16[4,32,128,128]{3,2,1,0:T(8,128)(2,1)S(1)}, bf16[4,32,128,128]{3,2,1,0:T(8,128)(2,1)}, u32[]{:S(2)}) copy-start(bf16[4,32,128,128]{3,2,1,0:T(8,128)(2,1)} %blk_ref.7) | copy-start | bytes 12582916
  105.2 17.5 %all-to-all-start.5 = ((bf16[16,128,128]{2,1,0:T(8,128)(2,1)}), bf16[16,128,128]{2,1,0:T(8,128)(2,1)S(1)}, u32[]{:S(2)}, u32[]{:S(2)}) async-start(bf16[16,128,128]{2,1,0:T(8,128)(2,1)} %get-tuple-element.18), calls=%async_computation.5 | async-start | bytes 1048576 | tf_op jit(solution)/shard_map/all_to_all | solution.py:179

commit v13 on v11

--- a/solution.py
+++ b/solution.py
@@ -168,8 +168,11 @@
     local_rows = blocks.shape[0]
     orbitals = blocks.shape[2]
     group_width = vectors.shape[1]
-    asked = jnp.stack(
-        [requests(columns, nrows, local_rows), requests(owners, nrows, local_rows)], axis=1
+    lane = lax.broadcasted_iota(jnp.int32, (nrows, 128), 1)
+    asked = jnp.where(
+        lane == 0,
+        requests(columns, nrows, local_rows)[:, None],
+        jnp.where(lane == 1, requests(owners, nrows, local_rows)[:, None], 0),
     )
     granted = lax.all_to_all(asked, "rows", split_axis=0, concat_axis=0, tiled=True)
     wanted = granted[:, 0]

time: 121 us -> 121 us (level)
  no operation moved by 1% of the time
where the time goes in v13:
time: 121 us; the launch traced here: 120 us
  blocking collectives  52.4 us (43%)
  waiting for transfers between devices  32.7 us (27%)
  starting transfers between devices  15.7 us (13%)
  Pallas kernels  10.1 us (8%)
  local copies, waits for them, and re-layouts  4.42 us (4%)
  other arithmetic  3.32 us (3%)
  between operations  1.38 us (1%)
    all_to_all x3, blocking collectives, exchange(): lax.all_to_all(outgoing, 'rows', split_axis=0, concat_axis=0, tiled=True)  52.4 us
    all_to_all x2, waiting for transfers between devices, exchange(): lax.all_to_all(outgoing, 'rows', split_axis=0, concat_axis=0, tiled=True)  26.3 us
    all_to_all x1, starting transfers between devices, on_device(): lax.all_to_all(asked, 'rows', split_axis=0, concat_axis=0, tiled=True)  8.31 us
    all_to_all x2, starting transfers between devices, exchange(): lax.all_to_all(outgoing, 'rows', split_axis=0, concat_axis=0, tiled=True)  7.42 us
    pallas_call x3, Pallas kernels, chebyshev_step(): pl.pallas_call(functools.partial(step_kernel, first), out_shape=(jax.Shap...  7.05 us
    all_to_all x1, waiting for transfers between devices, on_device(): lax.all_to_all(asked, 'rows', split_axis=0, concat_axis=0, tiled=True)  6.37 us
    pallas_call x1, Pallas kernels, first_chebyshev_step(): pl.pallas_call(functools.partial(first_step_kernel, first), out_shape=(ja...  3.08 us
  transfers between devices with their start and end apart: 3, of which 3 were waited for; matrix products, arithmetic and copies ran while one was open for 1% of the time, Pallas kernels for 0%

profile of v13, /device:TPU:0, one launch (start us, length us, event | category | flops | bytes accessed | tf_op | source)
XLA Modules:
  0.0 120.2 jit_solution(1971149106843709146)
XLA Ops:
  0.0 0.0 copy-start.3
  0.0 0.0 copy-start.2
  0.0 0.0 copy-start.4
  0.0 0.8 add_select_fusion.1
  0.8 0.7 and_select_fusion.1
  1.4 0.1 select_reduce_fusion
  1.6 0.1 select_reduce_fusion.1
  1.6 0.7 broadcast_select_fusion.1
  2.3 8.3 %all-to-all-start = ((s32[16,1,128]{2,1,0:T(1,128)}), s32[16,1,128]{2,1,0:T(1,128)S(1)}, u32[]{:S(2)}, u32[]{:S(2)}) async-start(s32[16,1,128]{2,1,0:T(1,128)} %broadcast_select_fusion.1), calls=%async_computation | async-start | bytes 16384 | tf_op jit(solution)/shard_map/all_to_all | solution.py:177
  10.7 0.8 fusion.1
  11.5 6.4 %all-to-all-done = s32[16,1,128]{2,1,0:T(1,128)S(1)} async-done(((s32[16,1,128]{2,1,0:T(1,128)}), s32[16,1,128]{2,1,0:T(1,128)S(1)}, u32[]{:S(2)}, u32[]{:S(2)}) %all-to-all-start) | async-done | bytes 8224 | tf_op jit(solution)/shard_map/all_to_all | solution.py:177
  17.9 0.2 slice_reduce_fusion
  18.0 1.0 select_select_fusion
  19.0 3.6 %all-to-all-start.1 = ((bf16[16,128,128]{2,1,0:T(8,128)(2,1)}), bf16[16,128,128]{2,1,0:T(8,128)(2,1)S(1)}, u32[]{:S(2)}, u32[]{:S(2)}) async-start(bf16[16,128,128]{2,1,0:T(8,128)(2,1)} %select_select_fusion), calls=%async_computation.1 | async-start | bytes 1048576 | tf_op jit(solution)/shard_map/all_to_all | solution.py:182
  23.9 12.7 %all-to-all-done.1.recv_ref = bf16[16,128,128]{2,1,0:T(8,128)(2,1)S(1)} async-done(((bf16[16,128,128]{2,1,0:T(8,128)(2,1)}), bf16[16,128,128]{2,1,0:T(8,128)(2,1)S(1)}, u32[]{:S(2)}, u32[]{:S(2)}) %all-to-all-start.1) | async-done | bytes 524320 | tf_op jit(solution)/shard_map/all_to_all | solution.py:182
  36.6 0.0 copy-start
  36.6 2.2 %copy-done = bf16[4,32,128,128]{3,2,1,0:T(8,128)(2,1)S(1)} copy-done((bf16[4,32,128,128]{3,2,1,0:T(8,128)(2,1)S(1)}, bf16[4,32,128,128]{3,2,1,0:T(8,128)(2,1)}, u32[]{:S(2)}) %copy-start) | copy-done | bytes 4194328
  38.8 0.0 copy-start.1
  38.8 3.1 %shard_map.73 = (bf16[4,128,128]{2,1,0:T(8,128)(2,1)S(1)}, bf16[16,128,128]{2,1,0:T(8,128)(2,1)S(1)}) custom-call(s32[4,32]{1,0:T(4,128)} %cols_ref.5, s32[16]{0:T(128)S(1)} %get-tuple-element.19.pick_ref, f32[4,32]{1,0:T(4,128)} %scl_ref.5, f32[1]{0:T(128)S(6)} %copy.8.c_ref, f32[1]{0:T(128)S(6)} %copy.9.w_ref, ...), custom_call_target="tpu_custom_call" | custom-call | flops 536870912 | bytes 5636096 | tf_op jit(solution)/shard_map/pallas_call | solution.py:140
  41.9 17.5 %all_to_all.34.recv_ref = bf16[16,128,128]{2,1,0:T(8,128)(2,1)S(1)} all-to-all(bf16[16,128,128]{2,1,0:T(8,128)(2,1)S(1)} %get-tuple-element.12), channel_id=1, replica_groups=mesh['rows'=16,'vecs'=2] {'rows'}, dimensions={0} | all-to-all | bytes 1048576 | tf_op jit(solution)/shard_map/all_to_all | solution.py:182
  59.4 0.0 copy-done.3
  59.4 0.0 copy-done.2
  59.4 0.0 copy-done.4
  59.4 0.0 copy-done.1
  59.4 2.1 %shard_map.74 = (bf16[4,128,128]{2,1,0:T(8,128)(2,1)S(1)}, bf16[16,128,128]{2,1,0:T(8,128)(2,1)S(1)}) custom-call(s32[4,32]{1,0:T(4,128)S(1)} %copy-done.3, s32[16]{0:T(128)S(1)} %get-tuple-element.19.pick_ref, f32[4,32]{1,0:T(4,128)S(1)} %copy-done.4, f32[1]{0:T(128)S(6)} %copy.8.c_ref, f32[1]{0:T(128)S(6)} %copy.9.w_ref, ...), custom_call_target="tpu_custom_call" | custom-call | flops 536870912 | bytes 5636096 | tf_op jit(solution)/shard_map/pallas_call | solution.py:106
  61.5 17.5 %all_to_all.35.recv_ref = bf16[16,128,128]{2,1,0:T(8,128)(2,1)S(1)} all-to-all(bf16[16,128,128]{2,1,0:T(8,128)(2,1)S(1)} %get-tuple-element.14), channel_id=1, replica_groups=mesh['rows'=16,'vecs'=2] {'rows'}, dimensions={0} | all-to-all | bytes 1048576 | tf_op jit(solution)/shard_map/all_to_all | solution.py:182
  79.0 2.1 %shard_map.75 = (bf16[4,128,128]{2,1,0:T(8,128)(2,1)S(1)}, bf16[16,128,128]{2,1,0:T(8,128)(2,1)S(1)}) custom-call(s32[4,32]{1,0:T(4,128)S(1)} %copy-done.3, s32[16]{0:T(128)S(1)} %get-tuple-element.19.pick_ref, f32[4,32]{1,0:T(4,128)S(1)} %copy-done.4, f32[1]{0:T(128)S(6)} %copy.8.c_ref, f32[1]{0:T(128)S(6)} %copy.9.w_ref, ...), custom_call_target="tpu_custom_call" | custom-call | flops 536870912 | bytes 5636096 | tf_op jit(solution)/shard_map/pallas_call | solution.py:106
  81.1 17.4 %all_to_all.36.recv_ref = bf16[16,128,128]{2,1,0:T(8,128)(2,1)S(1)} all-to-all(bf16[16,128,128]{2,1,0:T(8,128)(2,1)S(1)} %get-tuple-element.16), channel_id=1, replica_groups=mesh['rows'=16,'vecs'=2] {'rows'}, dimensions={0} | all-to-all | bytes 1048576 | tf_op jit(solution)/shard_map/all_to_all | solution.py:182
  98.5 2.9 %shard_map.76 = (bf16[4,128,128]{2,1,0:T(8,128)(2,1)}, bf16[16,128,128]{2,1,0:T(8,128)(2,1)}) custom-call(s32[4,32]{1,0:T(4,128)S(1)} %copy-done.3, s32[16]{0:T(128)S(1)} %get-tuple-element.20.pick_ref, f32[4,32]{1,0:T(4,128)S(1)} %copy-done.4, f32[1]{0:T(128)S(6)} %copy.8.c_ref, f32[1]{0:T(128)S(6)} %copy.9.w_ref, ...), custom_call_target="tpu_custom_call" | custom-call | flops 536870912 | bytes 5636096 | tf_op jit(solution)/shard_map/pallas_call | solution.py:106
  101.4 3.9 %all-to-all-start.5 = ((bf16[16,128,128]{2,1,0:T(8,128)(2,1)}), bf16[16,128,128]{2,1,0:T(8,128)(2,1)S(1)}, u32[]{:S(2)}, u32[]{:S(2)}) async-start(bf16[16,128,128]{2,1,0:T(8,128)(2,1)} %get-tuple-element.18), calls=%async_computation.5 | async-start | bytes 1048576 | tf_op jit(solution)/shard_map/all_to_all | solution.py:182
  105.3 13.7 %all-to-all-done.5 = bf16[16,128,128]{2,1,0:T(8,128)(2,1)S(1)} async-done(((bf16[16,128,128]{2,1,0:T(8,128)(2,1)}), bf16[16,128,128]{2,1,0:T(8,128)(2,1)S(1)}, u32[]{:S(2)}, u32[]{:S(2)}) %all-to-all-start.5) | async-done | bytes 524320 | tf_op jit(solution)/shard_map/all_to_all | solution.py:182
  118.9 1.2 %gather_fusion = bf16[4,128,128]{2,1,0:T(8,128)(2,1)} fusion(bf16[16,128,128]{2,1,0:T(8,128)(2,1)S(1)} %all-to-all-done.5, s32[1024]{0:T(1024)S(1)} %pad_clamp_fusion), kind=kCustom, calls=%fused_computation | custom fusion | bytes 262160 | tf_op jit(solution)/shard_map/jit(_take)/gather | solution.py:197
  (3 shorter events, 0.0 us)
Async XLA Ops:
  0.0 59.4 %copy-start.3 = (s32[4,32]{1,0:T(4,128)S(1)}, s32[4,32]{1,0:T(4,128)}, u32[]{:S(2)}) copy-start(s32[4,32]{1,0:T(4,128)} %cols_ref.5) | copy-start | bytes 1540
  0.0 59.4 %copy-start.2 = (bf16[512,128]{1,0:T(8,128)(2,1)S(1)}, bf16[512,128]{1,0:T(8,128)(2,1)}, u32[]{:S(2)}) copy-start(bf16[512,128]{1,0:T(8,128)(2,1)} %param.7) | copy-start | bytes 393220
  0.0 59.4 %copy-start.4 = (f32[4,32]{1,0:T(4,128)S(1)}, f32[4,32]{1,0:T(4,128)}, u32[]{:S(2)}) copy-start(f32[4,32]{1,0:T(4,128)} %scl_ref.5) | copy-start | bytes 1540
  2.3 15.5 %all-to-all-start = ((s32[16,1,128]{2,1,0:T(1,128)}), s32[16,1,128]{2,1,0:T(1,128)S(1)}, u32[]{:S(2)}, u32[]{:S(2)}) async-start(s32[16,1,128]{2,1,0:T(1,128)} %broadcast_select_fusion.1), calls=%async_computation | async-start | bytes 16384 | tf_op jit(solution)/shard_map/all_to_all | solution.py:177
  19.0 17.6 %all-to-all-start.1 = ((bf16[16,128,128]{2,1,0:T(8,128)(2,1)}), bf16[16,128,128]{2,1,0:T(8,128)(2,1)S(1)}, u32[]{:S(2)}, u32[]{:S(2)}) async-start(bf16[16,128,128]{2,1,0:T(8,128)(2,1)} %select_select_fusion), calls=%async_computation.1 | async-start | bytes 1048576 | tf_op jit(solution)/shard_map/all_to_all | solution.py:182
  36.6 2.2 %copy-start = (bf16[4,32,128,128]{3,2,1,0:T(8,128)(2,1)S(1)}, bf16[4,32,128,128]{3,2,1,0:T(8,128)(2,1)}, u32[]{:S(2)}) copy-start(bf16[4,32,128,128]{3,2,1,0:T(8,128)(2,1)} %blk_ref.7) | copy-start | bytes 12582916
  38.8 20.6 %copy-start.1 = (bf16[4,32,128,128]{3,2,1,0:T(8,128)(2,1)S(1)}, bf16[4,32,128,128]{3,2,1,0:T(8,128)(2,1)}, u32[]{:S(2)}) copy-start(bf16[4,32,128,128]{3,2,1,0:T(8,128)(2,1)} %blk_ref.7) | copy-start | bytes 12582916
  101.4 17.5 %all-to-all-start.5 = ((bf16[16,128,128]{2,1,0:T(8,128)(2,1)}), bf16[16,128,128]{2,1,0:T(8,128)(2,1)S(1)}, u32[]{:S(2)}, u32[]{:S(2)}) async-start(bf16[16,128,128]{2,1,0:T(8,128)(2,1)} %get-tuple-element.18), calls=%async_computation.5 | async-start | bytes 1048576 | tf_op jit(solution)/shard_map/all_to_all | solution.py:182

commit v14 on v11

--- a/solution.py
+++ b/solution.py
@@ -16,9 +16,11 @@
     return jnp.max(jnp.where(hit, (index % local_rows)[None], 0), axis=tuple(range(1, index.ndim + 1)))
 
 
-def step_kernel(first, cols_ref, pick_ref, scl_ref, c_ref, w_ref, recv_ref, blk_ref, cur_ref, *rest):
+def step_kernel(first, last, cols_ref, pick_ref, scl_ref, c_ref, w_ref, recv_ref, blk_ref, cur_ref, *rest):
     if first:
         out_ref, go_ref = rest
+    elif last:
+        prev_ref, go_ref, out_ref = rest
     else:
         prev_ref, out_ref, go_ref = rest
     local_rows, per_row = cols_ref.shape
@@ -91,7 +93,7 @@
     lax.fori_loop(0, go_ref.shape[0], put, 0)
 
 
-def chebyshev_step(columns, pick, scales, center, half_width, received, blocks, cur, prev):
+def chebyshev_step(columns, pick, scales, center, half_width, received, blocks, cur, prev, last=False):
     local_rows, per_row, orbitals, _ = blocks.shape
     width = cur.shape[2]
     nrows = pick.shape[0]
@@ -104,13 +106,18 @@
     flops = 2 * local_rows * per_row * orbitals * orbitals * width
     nbytes = blocks.size * 2 + 2 * received.size * 2 + 3 * cur.size * 2
     return pl.pallas_call(
-        functools.partial(step_kernel, first),
+        functools.partial(step_kernel, first, last),
         out_shape=(
-            jax.ShapeDtypeStruct(cur.shape, jnp.bfloat16),
-            jax.ShapeDtypeStruct((nrows, orbitals, width), jnp.bfloat16),
+            (jax.ShapeDtypeStruct((nrows, orbitals, width), jnp.bfloat16),)
+            if last
+            else (
+                jax.ShapeDtypeStruct(cur.shape, jnp.bfloat16),
+                jax.ShapeDtypeStruct((nrows, orbitals, width), jnp.bfloat16),
+            )
         ),
         in_specs=[smem] * 5 + [vmem] * (len(args) - 5),
-        out_specs=(vmem, vmem),
+        out_specs=(vmem,) if last else (vmem, vmem),
+        scratch_shapes=[pltpu.VMEM(cur.shape, jnp.bfloat16)] if last else [],
         compiler_params=pltpu.CompilerParams(vmem_limit_bytes=8 * 1024 * 1024),
         cost_estimate=pl.CostEstimate(flops=flops, bytes_accessed=nbytes, transcendentals=0),
     )(*args)
@@ -184,12 +191,15 @@
         columns, wanted, scales, center, half_width,
         exchange(select_rows(previous, wanted)), blocks, previous, None,
     )
-    for step in range(1, STEPS):
-        pick = relay_want if step == STEPS - 1 else wanted
+    for step in range(1, STEPS - 1):
         upcoming, outgoing = chebyshev_step(
-            columns, pick, scales, center, half_width, exchange(outgoing), blocks, current, previous
+            columns, wanted, scales, center, half_width, exchange(outgoing), blocks, current, previous
         )
         previous, current = (current, upcoming)
+    (outgoing,) = chebyshev_step(
+        columns, relay_want, scales, center, half_width, exchange(outgoing), blocks, current,
+        previous, last=True,
+    )
     arrived = exchange(outgoing)
     placed = jnp.take(arrived, owners // local_rows, axis=0, mode="clip")
     return placed.reshape(local_rows * orbitals, group_width)

time: 121 us -> 121 us (level)
  no operation moved by 1% of the time
where the time goes in v14:
time: 121 us; the launch traced here: 120 us
  blocking collectives  52.4 us (43%)
  waiting for transfers between devices  32.7 us (27%)
  starting transfers between devices  15.7 us (13%)
  Pallas kernels  10.1 us (8%)
  local copies, waits for them, and re-layouts  5.01 us (4%)
  other arithmetic  2.6 us (2%)
  between operations  1.39 us (1%)
    all_to_all x3, blocking collectives, exchange(): lax.all_to_all(outgoing, 'rows', split_axis=0, concat_axis=0, tiled=True)  52.4 us
    all_to_all x2, waiting for transfers between devices, exchange(): lax.all_to_all(outgoing, 'rows', split_axis=0, concat_axis=0, tiled=True)  26.3 us
    all_to_all x1, starting transfers between devices, on_device(): lax.all_to_all(asked, 'rows', split_axis=0, concat_axis=0, tiled=True)  8.32 us
    all_to_all x2, starting transfers between devices, exchange(): lax.all_to_all(outgoing, 'rows', split_axis=0, concat_axis=0, tiled=True)  7.41 us
    pallas_call x3, Pallas kernels, chebyshev_step(): pl.pallas_call(functools.partial(step_kernel, first, last), out_shape=(ja...  7 us
    all_to_all x1, waiting for transfers between devices, on_device(): lax.all_to_all(asked, 'rows', split_axis=0, concat_axis=0, tiled=True)  6.37 us
    pallas_call x1, Pallas kernels, first_chebyshev_step(): pl.pallas_call(functools.partial(first_step_kernel, first), out_shape=(ja...  3.08 us
  transfers between devices with their start and end apart: 3, of which 3 were waited for; matrix products, arithmetic and copies ran while one was open for 1% of the time, Pallas kernels for 0%

profile of v14, /device:TPU:0, one launch (start us, length us, event | category | flops | bytes accessed | tf_op | source)
XLA Modules:
  0.0 120.0 jit_solution(6467799731395025750)
XLA Ops:
  0.0 0.0 copy-start.3
  0.0 0.0 copy-start.2
  0.0 0.0 copy-start.4
  0.0 0.7 and_select_fusion.1
  0.7 0.7 add_select_fusion.1
  1.4 0.1 select_reduce_fusion.1
  1.5 0.1 select_reduce_fusion
  1.6 0.7 copy.10
  2.3 8.3 %all-to-all-start = ((s32[16,1,2]{2,1,0:T(1,128)}), s32[16,1,2]{2,1,0:T(1,128)S(1)}, u32[]{:S(2)}, u32[]{:S(2)}) async-start(s32[16,1,2]{2,1,0:T(1,128)} %copy.10), calls=%async_computation | async-start | bytes 16384 | tf_op jit(solution)/shard_map/all_to_all | solution.py:181
  10.6 0.8 fusion.1
  11.5 6.4 %all-to-all-done = s32[16,1,2]{2,1,0:T(1,128)S(1)} async-done(((s32[16,1,2]{2,1,0:T(1,128)}), s32[16,1,2]{2,1,0:T(1,128)S(1)}, u32[]{:S(2)}, u32[]{:S(2)}) %all-to-all-start) | async-done | bytes 160 | tf_op jit(solution)/shard_map/all_to_all | solution.py:181
  17.8 0.1 copy.11
  17.9 1.0 select_select_fusion
  18.9 3.6 %all-to-all-start.1 = ((bf16[16,128,128]{2,1,0:T(8,128)(2,1)}), bf16[16,128,128]{2,1,0:T(8,128)(2,1)S(1)}, u32[]{:S(2)}, u32[]{:S(2)}) async-start(bf16[16,128,128]{2,1,0:T(8,128)(2,1)} %select_select_fusion), calls=%async_computation.1 | async-start | bytes 1048576 | tf_op jit(solution)/shard_map/all_to_all | solution.py:186
  23.8 12.7 %all-to-all-done.1.recv_ref = bf16[16,128,128]{2,1,0:T(8,128)(2,1)S(1)} async-done(((bf16[16,128,128]{2,1,0:T(8,128)(2,1)}), bf16[16,128,128]{2,1,0:T(8,128)(2,1)S(1)}, u32[]{:S(2)}, u32[]{:S(2)}) %all-to-all-start.1) | async-done | bytes 524320 | tf_op jit(solution)/shard_map/all_to_all | solution.py:186
  36.4 0.0 copy-start
  36.4 2.2 %copy-done = bf16[4,32,128,128]{3,2,1,0:T(8,128)(2,1)S(1)} copy-done((bf16[4,32,128,128]{3,2,1,0:T(8,128)(2,1)S(1)}, bf16[4,32,128,128]{3,2,1,0:T(8,128)(2,1)}, u32[]{:S(2)}) %copy-start) | copy-done | bytes 4194328
  38.6 0.0 copy-start.1
  38.6 3.1 %shard_map.73 = (bf16[4,128,128]{2,1,0:T(8,128)(2,1)S(1)}, bf16[16,128,128]{2,1,0:T(8,128)(2,1)S(1)}) custom-call(s32[4,32]{1,0:T(4,128)} %cols_ref.5, s32[16]{0:T(128)S(1)} %get-tuple-element.26.pick_ref, f32[4,32]{1,0:T(4,128)} %scl_ref.5, f32[1]{0:T(128)S(6)} %copy.12.c_ref, f32[1]{0:T(128)S(6)} %copy.13.w_ref, ...), custom_call_target="tpu_custom_call" | custom-call | flops 536870912 | bytes 5636096 | tf_op jit(solution)/shard_map/pallas_call | solution.py:147
  41.7 17.5 %all_to_all.37.recv_ref = bf16[16,128,128]{2,1,0:T(8,128)(2,1)S(1)} all-to-all(bf16[16,128,128]{2,1,0:T(8,128)(2,1)S(1)} %get-tuple-element.11), channel_id=1, replica_groups=mesh['rows'=16,'vecs'=2] {'rows'}, dimensions={0} | all-to-all | bytes 1048576 | tf_op jit(solution)/shard_map/all_to_all | solution.py:186
  59.3 0.0 copy-done.3
  59.3 0.0 copy-done.2
  59.3 0.0 copy-done.4
  59.3 0.0 copy-done.1
  59.3 2.1 %shard_map.74 = (bf16[4,128,128]{2,1,0:T(8,128)(2,1)S(1)}, bf16[16,128,128]{2,1,0:T(8,128)(2,1)S(1)}) custom-call(s32[4,32]{1,0:T(4,128)S(1)} %copy-done.3, s32[16]{0:T(128)S(1)} %get-tuple-element.26.pick_ref, f32[4,32]{1,0:T(4,128)S(1)} %copy-done.4, f32[1]{0:T(128)S(6)} %copy.12.c_ref, f32[1]{0:T(128)S(6)} %copy.13.w_ref, ...), custom_call_target="tpu_custom_call" | custom-call | flops 536870912 | bytes 5636096 | tf_op jit(solution)/shard_map/pallas_call | solution.py:108
  61.4 17.5 %all_to_all.38.recv_ref = bf16[16,128,128]{2,1,0:T(8,128)(2,1)S(1)} all-to-all(bf16[16,128,128]{2,1,0:T(8,128)(2,1)S(1)} %get-tuple-element.13), channel_id=1, replica_groups=mesh['rows'=16,'vecs'=2] {'rows'}, dimensions={0} | all-to-all | bytes 1048576 | tf_op jit(solution)/shard_map/all_to_all | solution.py:186
  78.9 2.1 %shard_map.75 = (bf16[4,128,128]{2,1,0:T(8,128)(2,1)S(1)}, bf16[16,128,128]{2,1,0:T(8,128)(2,1)S(1)}) custom-call(s32[4,32]{1,0:T(4,128)S(1)} %copy-done.3, s32[16]{0:T(128)S(1)} %get-tuple-element.26.pick_ref, f32[4,32]{1,0:T(4,128)S(1)} %copy-done.4, f32[1]{0:T(128)S(6)} %copy.12.c_ref, f32[1]{0:T(128)S(6)} %copy.13.w_ref, ...), custom_call_target="tpu_custom_call" | custom-call | flops 536870912 | bytes 5636096 | tf_op jit(solution)/shard_map/pallas_call | solution.py:108
  80.9 17.4 %all_to_all.39.recv_ref = bf16[16,128,128]{2,1,0:T(8,128)(2,1)S(1)} all-to-all(bf16[16,128,128]{2,1,0:T(8,128)(2,1)S(1)} %get-tuple-element.15), channel_id=1, replica_groups=mesh['rows'=16,'vecs'=2] {'rows'}, dimensions={0} | all-to-all | bytes 1048576 | tf_op jit(solution)/shard_map/all_to_all | solution.py:186
  98.3 2.9 %shard_map.76 = bf16[16,128,128]{2,1,0:T(8,128)(2,1)} custom-call(s32[4,32]{1,0:T(4,128)S(1)} %copy-done.3, s32[16]{0:T(128)S(1)} %get-tuple-element.27.pick_ref, f32[4,32]{1,0:T(4,128)S(1)} %copy-done.4, f32[1]{0:T(128)S(6)} %copy.12.c_ref, f32[1]{0:T(128)S(6)} %copy.13.w_ref, bf16[16,128,128]{2,1,0:T(8,128)(2,1)S(1)} %all_to_all.39.recv_ref, ...), custom_call_target="tpu_custom_call" | custom-call | flops 536870912 | bytes 5636096 | tf_op jit(solution)/shard_map/pallas_call | solution.py:108
  101.2 3.8 %all-to-all-start.5 = ((bf16[16,128,128]{2,1,0:T(8,128)(2,1)}), bf16[16,128,128]{2,1,0:T(8,128)(2,1)S(1)}, u32[]{:S(2)}, u32[]{:S(2)}) async-start(bf16[16,128,128]{2,1,0:T(8,128)(2,1)} %shard_map.76), calls=%async_computation.5 | async-start | bytes 1048576 | tf_op jit(solution)/shard_map/all_to_all | solution.py:186
  105.1 13.7 %all-to-all-done.5 = bf16[16,128,128]{2,1,0:T(8,128)(2,1)S(1)} async-done(((bf16[16,128,128]{2,1,0:T(8,128)(2,1)}), bf16[16,128,128]{2,1,0:T(8,128)(2,1)S(1)}, u32[]{:S(2)}, u32[]{:S(2)}) %all-to-all-start.5) | async-done | bytes 524320 | tf_op jit(solution)/shard_map/all_to_all | solution.py:186
  118.8 1.2 %gather_fusion = bf16[4,128,128]{2,1,0:T(8,128)(2,1)} fusion(bf16[16,128,128]{2,1,0:T(8,128)(2,1)S(1)} %all-to-all-done.5, s32[1024]{0:T(1024)S(1)} %pad_clamp_fusion), kind=kCustom, calls=%fused_computation | custom fusion | bytes 262160 | tf_op jit(solution)/shard_map/jit(_take)/gather | solution.py:204
  (4 shorter events, 0.0 us)
Async XLA Ops:
  0.0 59.3 %copy-start.3 = (s32[4,32]{1,0:T(4,128)S(1)}, s32[4,32]{1,0:T(4,128)}, u32[]{:S(2)}) copy-start(s32[4,32]{1,0:T(4,128)} %cols_ref.5) | copy-start | bytes 1540
  0.0 59.3 %copy-start.2 = (bf16[512,128]{1,0:T(8,128)(2,1)S(1)}, bf16[512,128]{1,0:T(8,128)(2,1)}, u32[]{:S(2)}) copy-start(bf16[512,128]{1,0:T(8,128)(2,1)} %param.7) | copy-start | bytes 393220
  0.0 59.3 %copy-start.4 = (f32[4,32]{1,0:T(4,128)S(1)}, f32[4,32]{1,0:T(4,128)}, u32[]{:S(2)}) copy-start(f32[4,32]{1,0:T(4,128)} %scl_ref.5) | copy-start | bytes 1540
  2.3 15.5 %all-to-all-start = ((s32[16,1,2]{2,1,0:T(1,128)}), s32[16,1,2]{2,1,0:T(1,128)S(1)}, u32[]{:S(2)}, u32[]{:S(2)}) async-start(s32[16,1,2]{2,1,0:T(1,128)} %copy.10), calls=%async_computation | async-start | bytes 16384 | tf_op jit(solution)/shard_map/all_to_all | solution.py:181
  18.9 17.6 %all-to-all-start.1 = ((bf16[16,128,128]{2,1,0:T(8,128)(2,1)}), bf16[16,128,128]{2,1,0:T(8,128)(2,1)S(1)}, u32[]{:S(2)}, u32[]{:S(2)}) async-start(bf16[16,128,128]{2,1,0:T(8,128)(2,1)} %select_select_fusion), calls=%async_computation.1 | async-start | bytes 1048576 | tf_op jit(solution)/shard_map/all_to_all | solution.py:186
  36.4 2.2 %copy-start = (bf16[4,32,128,128]{3,2,1,0:T(8,128)(2,1)S(1)}, bf16[4,32,128,128]{3,2,1,0:T(8,128)(2,1)}, u32[]{:S(2)}) copy-start(bf16[4,32,128,128]{3,2,1,0:T(8,128)(2,1)} %blk_ref.7) | copy-start | bytes 12582916
  38.6 20.6 %copy-start.1 = (bf16[4,32,128,128]{3,2,1,0:T(8,128)(2,1)S(1)}, bf16[4,32,128,128]{3,2,1,0:T(8,128)(2,1)}, u32[]{:S(2)}) copy-start(bf16[4,32,128,128]{3,2,1,0:T(8,128)(2,1)} %blk_ref.7) | copy-start | bytes 12582916
  101.2 17.5 %all-to-all-start.5 = ((bf16[16,128,128]{2,1,0:T(8,128)(2,1)}), bf16[16,128,128]{2,1,0:T(8,128)(2,1)S(1)}, u32[]{:S(2)}, u32[]{:S(2)}) async-start(bf16[16,128,128]{2,1,0:T(8,128)(2,1)} %shard_map.76), calls=%async_computation.5 | async-start | bytes 1048576 | tf_op jit(solution)/shard_map/all_to_all | solution.py:186

commit v15 on v11

--- a/solution.py
+++ b/solution.py
@@ -48,27 +48,20 @@
     lax.fori_loop(0, go_ref.shape[0], put, 0)
 
 
-def first_step_kernel(first, cols_hbm, pick_ref, scl_hbm, c_ref, w_ref, recv_ref, blk_ref, cur_hbm, *rest):
+def first_step_kernel(first, slot_ref, pick_ref, scl_ref, c_ref, w_ref, recv_ref, blk_ref, cur_hbm, *rest):
     if first:
-        out_ref, go_ref, cols_ref, scl_ref, cur_ref, sems = rest
+        out_ref, go_ref, cur_ref, sems = rest
     else:
-        prev_ref, out_ref, go_ref, cols_ref, scl_ref, cur_ref, sems = rest
-    copies = [
-        pltpu.make_async_copy(cols_hbm, cols_ref, sems.at[0]),
-        pltpu.make_async_copy(scl_hbm, scl_ref, sems.at[1]),
-        pltpu.make_async_copy(cur_hbm, cur_ref, sems.at[2]),
-    ]
-    for copy in copies:
-        copy.start()
-    copies[0].wait()
-    copies[1].wait()
-    local_rows, per_row = cols_ref.shape
+        prev_ref, out_ref, go_ref, cur_ref, sems = rest
+    copy = pltpu.make_async_copy(cur_hbm, cur_ref, sems.at[0])
+    copy.start()
+    local_rows, per_row = slot_ref.shape
     shift = c_ref[0]
     width = w_ref[0]
     for r in range(local_rows):
 
         def body(k, acc):
-            s = cols_ref[r, k] // local_rows
+            s = slot_ref[r, k]
             prod = jnp.dot(blk_ref[r, k], recv_ref[s], preferred_element_type=jnp.float32)
             return acc + scl_ref[r, k] * prod
 
@@ -76,7 +69,7 @@
             0, per_row, body, jnp.zeros(out_ref.shape[1:], jnp.float32), unroll=True
         )
         if r == 0:
-            copies[2].wait()
+            copy.wait()
         cur = cur_ref[r].astype(jnp.float32)
         if first:
             new = (acc - shift * cur) / width
@@ -128,10 +121,9 @@
     if first:
         cur = pltpu.with_memory_space_constraint(cur, hbm)
     args = [
-        pltpu.with_memory_space_constraint(columns, hbm), pick,
-        pltpu.with_memory_space_constraint(scales, hbm), center, half_width, received, blocks, cur,
+        columns // blocks.shape[0], pick, scales + 0.0, center, half_width, received, blocks, cur,
     ]
-    in_specs = [anywhere, smem, anywhere, smem, smem, vmem, vmem, anywhere]
+    in_specs = [smem, smem, smem, smem, smem, vmem, vmem, anywhere]
     if not first:
         args.append(prev)
         in_specs.append(vmem)
@@ -146,10 +138,8 @@
         in_specs=in_specs,
         out_specs=(vmem, vmem),
         scratch_shapes=[
-            pltpu.SMEM(columns.shape, columns.dtype),
-            pltpu.SMEM(scales.shape, scales.dtype),
             pltpu.VMEM(cur.shape, cur.dtype),
-            pltpu.SemaphoreType.DMA((3,)),
+            pltpu.SemaphoreType.DMA((1,)),
         ],
         compiler_params=pltpu.CompilerParams(vmem_limit_bytes=8 * 1024 * 1024),
         cost_estimate=pl.CostEstimate(flops=flops, bytes_accessed=nbytes, transcendentals=0),

time: 121 us -> 122 us (level)
    unnamed x10 -> x12, local copies, waits for them, and re-layouts: 2.2 us -> 2.88 us
where the time goes in v15:
time: 122 us; the launch traced here: 121 us
  blocking collectives  52.4 us (43%)
  waiting for transfers between devices  32.7 us (27%)
  starting transfers between devices  15.7 us (13%)
  Pallas kernels  10.4 us (9%)
  local copies, waits for them, and re-layouts  5.69 us (5%)
  other arithmetic  2.59 us (2%)
  between operations  1.39 us (1%)
    all_to_all x3, blocking collectives, exchange(): lax.all_to_all(outgoing, 'rows', split_axis=0, concat_axis=0, tiled=True)  52.4 us
    all_to_all x2, waiting for transfers between devices, exchange(): lax.all_to_all(outgoing, 'rows', split_axis=0, concat_axis=0, tiled=True)  26.3 us
    all_to_all x1, starting transfers between devices, on_device(): lax.all_to_all(asked, 'rows', split_axis=0, concat_axis=0, tiled=True)  8.32 us
    all_to_all x2, starting transfers between devices, exchange(): lax.all_to_all(outgoing, 'rows', split_axis=0, concat_axis=0, tiled=True)  7.42 us
    pallas_call x3, Pallas kernels, chebyshev_step(): pl.pallas_call(functools.partial(step_kernel, first), out_shape=(jax.Shap...  7.06 us
    all_to_all x1, waiting for transfers between devices, on_device(): lax.all_to_all(asked, 'rows', split_axis=0, concat_axis=0, tiled=True)  6.37 us
    pallas_call x1, Pallas kernels, first_chebyshev_step(): pl.pallas_call(functools.partial(first_step_kernel, first), out_shape=(ja...  3.35 us
    unnamed x12, local copies, waits for them, and re-layouts  2.88 us
  transfers between devices with their start and end apart: 3, of which 3 were waited for; matrix products, arithmetic and copies ran while one was open for 1% of the time, Pallas kernels for 0%

profile of v15, /device:TPU:0, one launch (start us, length us, event | category | flops | bytes accessed | tf_op | source)
XLA Modules:
  0.0 121.0 jit_solution(18191529318659476687)
XLA Ops:
  0.0 0.0 copy-start.5
  0.0 0.0 copy-start.2
  0.0 0.0 copy-start.4
  0.0 0.7 and_select_fusion.1
  0.7 0.7 add_select_fusion.1
  1.4 0.1 select_reduce_fusion.1
  1.5 0.1 select_reduce_fusion
  1.6 0.7 copy.10
  2.3 8.3 %all-to-all-start = ((s32[16,1,2]{2,1,0:T(1,128)}), s32[16,1,2]{2,1,0:T(1,128)S(1)}, u32[]{:S(2)}, u32[]{:S(2)}) async-start(s32[16,1,2]{2,1,0:T(1,128)} %copy.10), calls=%async_computation | async-start | bytes 16384 | tf_op jit(solution)/shard_map/all_to_all | solution.py:164
  10.6 0.8 fusion.1
  11.5 6.4 %all-to-all-done = s32[16,1,2]{2,1,0:T(1,128)S(1)} async-done(((s32[16,1,2]{2,1,0:T(1,128)}), s32[16,1,2]{2,1,0:T(1,128)S(1)}, u32[]{:S(2)}, u32[]{:S(2)}) %all-to-all-start) | async-done | bytes 160 | tf_op jit(solution)/shard_map/all_to_all | solution.py:164
  17.8 0.1 copy.11
  17.9 1.0 select_select_fusion
  18.9 3.6 %all-to-all-start.1 = ((bf16[16,128,128]{2,1,0:T(8,128)(2,1)}), bf16[16,128,128]{2,1,0:T(8,128)(2,1)S(1)}, u32[]{:S(2)}, u32[]{:S(2)}) async-start(bf16[16,128,128]{2,1,0:T(8,128)(2,1)} %select_select_fusion), calls=%async_computation.1 | async-start | bytes 1048576 | tf_op jit(solution)/shard_map/all_to_all | solution.py:169
  23.8 12.7 %all-to-all-done.1.recv_ref = bf16[16,128,128]{2,1,0:T(8,128)(2,1)S(1)} async-done(((bf16[16,128,128]{2,1,0:T(8,128)(2,1)}), bf16[16,128,128]{2,1,0:T(8,128)(2,1)S(1)}, u32[]{:S(2)}, u32[]{:S(2)}) %all-to-all-start.1) | async-done | bytes 524320 | tf_op jit(solution)/shard_map/all_to_all | solution.py:169
  36.4 0.0 copy-start
  36.4 2.2 %copy-done = bf16[4,32,128,128]{3,2,1,0:T(8,128)(2,1)S(1)} copy-done((bf16[4,32,128,128]{3,2,1,0:T(8,128)(2,1)S(1)}, bf16[4,32,128,128]{3,2,1,0:T(8,128)(2,1)}, u32[]{:S(2)}) %copy-start) | copy-done | bytes 4194328
  38.6 0.7 copy-done.3
  39.3 3.3 %shard_map.73 = (bf16[4,128,128]{2,1,0:T(8,128)(2,1)S(1)}, bf16[16,128,128]{2,1,0:T(8,128)(2,1)S(1)}) custom-call(s32[4,32]{1,0:T(4,128)S(1)} %get-tuple-element.23.slot_ref, s32[16]{0:T(128)S(1)} %get-tuple-element.28.pick_ref, f32[4,32]{1,0:T(4,128)S(1)} %copy-done.3, f32[1]{0:T(128)S(6)} %copy.12.c_ref, f32[1]{0:T(128)S(6)} %copy.13.w_ref, ...), custom_call_target="tpu_custom_call" | custom-call | flops 536870912 | bytes 5636096 | tf_op jit(solution)/shard_map/pallas_call | solution.py:132
  42.7 17.5 %all_to_all.37.recv_ref = bf16[16,128,128]{2,1,0:T(8,128)(2,1)S(1)} all-to-all(bf16[16,128,128]{2,1,0:T(8,128)(2,1)S(1)} %get-tuple-element.12), channel_id=1, replica_groups=mesh['rows'=16,'vecs'=2] {'rows'}, dimensions={0} | all-to-all | bytes 1048576 | tf_op jit(solution)/shard_map/all_to_all | solution.py:169
  60.2 0.0 copy-done.5
  60.2 0.0 copy-done.2
  60.2 0.0 copy-done.4
  60.2 0.0 copy-done.1
  60.2 2.1 %shard_map.74 = (bf16[4,128,128]{2,1,0:T(8,128)(2,1)S(1)}, bf16[16,128,128]{2,1,0:T(8,128)(2,1)S(1)}) custom-call(s32[4,32]{1,0:T(4,128)S(1)} %copy-done.5, s32[16]{0:T(128)S(1)} %get-tuple-element.28.pick_ref, f32[4,32]{1,0:T(4,128)S(1)} %copy-done.4, f32[1]{0:T(128)S(6)} %copy.12.c_ref, f32[1]{0:T(128)S(6)} %copy.13.w_ref, ...), custom_call_target="tpu_custom_call" | custom-call | flops 536870912 | bytes 5636096 | tf_op jit(solution)/shard_map/pallas_call | solution.py:99
  62.3 17.5 %all_to_all.38.recv_ref = bf16[16,128,128]{2,1,0:T(8,128)(2,1)S(1)} all-to-all(bf16[16,128,128]{2,1,0:T(8,128)(2,1)S(1)} %get-tuple-element.14), channel_id=1, replica_groups=mesh['rows'=16,'vecs'=2] {'rows'}, dimensions={0} | all-to-all | bytes 1048576 | tf_op jit(solution)/shard_map/all_to_all | solution.py:169
  79.8 2.1 %shard_map.75 = (bf16[4,128,128]{2,1,0:T(8,128)(2,1)S(1)}, bf16[16,128,128]{2,1,0:T(8,128)(2,1)S(1)}) custom-call(s32[4,32]{1,0:T(4,128)S(1)} %copy-done.5, s32[16]{0:T(128)S(1)} %get-tuple-element.28.pick_ref, f32[4,32]{1,0:T(4,128)S(1)} %copy-done.4, f32[1]{0:T(128)S(6)} %copy.12.c_ref, f32[1]{0:T(128)S(6)} %copy.13.w_ref, ...), custom_call_target="tpu_custom_call" | custom-call | flops 536870912 | bytes 5636096 | tf_op jit(solution)/shard_map/pallas_call | solution.py:99
  81.9 17.4 %all_to_all.39.recv_ref = bf16[16,128,128]{2,1,0:T(8,128)(2,1)S(1)} all-to-all(bf16[16,128,128]{2,1,0:T(8,128)(2,1)S(1)} %get-tuple-element.16), channel_id=1, replica_groups=mesh['rows'=16,'vecs'=2] {'rows'}, dimensions={0} | all-to-all | bytes 1048576 | tf_op jit(solution)/shard_map/all_to_all | solution.py:169
  99.3 2.9 %shard_map.76 = (bf16[4,128,128]{2,1,0:T(8,128)(2,1)}, bf16[16,128,128]{2,1,0:T(8,128)(2,1)}) custom-call(s32[4,32]{1,0:T(4,128)S(1)} %copy-done.5, s32[16]{0:T(128)S(1)} %get-tuple-element.29.pick_ref, f32[4,32]{1,0:T(4,128)S(1)} %copy-done.4, f32[1]{0:T(128)S(6)} %copy.12.c_ref, f32[1]{0:T(128)S(6)} %copy.13.w_ref, ...), custom_call_target="tpu_custom_call" | custom-call | flops 536870912 | bytes 5636096 | tf_op jit(solution)/shard_map/pallas_call | solution.py:99
  102.2 3.8 %all-to-all-start.5 = ((bf16[16,128,128]{2,1,0:T(8,128)(2,1)}), bf16[16,128,128]{2,1,0:T(8,128)(2,1)S(1)}, u32[]{:S(2)}, u32[]{:S(2)}) async-start(bf16[16,128,128]{2,1,0:T(8,128)(2,1)} %get-tuple-element.18), calls=%async_computation.5 | async-start | bytes 1048576 | tf_op jit(solution)/shard_map/all_to_all | solution.py:169
  106.1 13.7 %all-to-all-done.5 = bf16[16,128,128]{2,1,0:T(8,128)(2,1)S(1)} async-done(((bf16[16,128,128]{2,1,0:T(8,128)(2,1)}), bf16[16,128,128]{2,1,0:T(8,128)(2,1)S(1)}, u32[]{:S(2)}, u32[]{:S(2)}) %all-to-all-start.5) | async-done | bytes 524320 | tf_op jit(solution)/shard_map/all_to_all | solution.py:169
  119.7 1.2 %gather_fusion = bf16[4,128,128]{2,1,0:T(8,128)(2,1)} fusion(bf16[16,128,128]{2,1,0:T(8,128)(2,1)S(1)} %all-to-all-done.5, s32[1024]{0:T(1024)S(1)} %pad_clamp_fusion), kind=kCustom, calls=%fused_computation | custom fusion | bytes 262160 | tf_op jit(solution)/shard_map/jit(_take)/gather | solution.py:184
  (6 shorter events, 0.0 us)
Async XLA Ops:
  0.0 60.2 %copy-start.5 = (s32[4,32]{1,0:T(4,128)S(1)}, s32[4,32]{1,0:T(4,128)}, u32[]{:S(2)}) copy-start(s32[4,32]{1,0:T(4,128)} %cols_ref.5) | copy-start | bytes 1540
  0.0 60.2 %copy-start.2 = (bf16[512,128]{1,0:T(8,128)(2,1)S(1)}, bf16[512,128]{1,0:T(8,128)(2,1)}, u32[]{:S(2)}) copy-start(bf16[512,128]{1,0:T(8,128)(2,1)} %param.7) | copy-start | bytes 393220
  0.0 60.2 %copy-start.4 = (f32[4,32]{1,0:T(4,128)S(1)}, f32[4,32]{1,0:T(4,128)}, u32[]{:S(2)}) copy-start(f32[4,32]{1,0:T(4,128)} %scl_ref.7) | copy-start | bytes 1540
  2.3 15.5 %all-to-all-start = ((s32[16,1,2]{2,1,0:T(1,128)}), s32[16,1,2]{2,1,0:T(1,128)S(1)}, u32[]{:S(2)}, u32[]{:S(2)}) async-start(s32[16,1,2]{2,1,0:T(1,128)} %copy.10), calls=%async_computation | async-start | bytes 16384 | tf_op jit(solution)/shard_map/all_to_all | solution.py:164
  18.9 17.6 %all-to-all-start.1 = ((bf16[16,128,128]{2,1,0:T(8,128)(2,1)}), bf16[16,128,128]{2,1,0:T(8,128)(2,1)S(1)}, u32[]{:S(2)}, u32[]{:S(2)}) async-start(bf16[16,128,128]{2,1,0:T(8,128)(2,1)} %select_select_fusion), calls=%async_computation.1 | async-start | bytes 1048576 | tf_op jit(solution)/shard_map/all_to_all | solution.py:169
  36.4 2.2 %copy-start = (bf16[4,32,128,128]{3,2,1,0:T(8,128)(2,1)S(1)}, bf16[4,32,128,128]{3,2,1,0:T(8,128)(2,1)}, u32[]{:S(2)}) copy-start(bf16[4,32,128,128]{3,2,1,0:T(8,128)(2,1)} %blk_ref.7) | copy-start | bytes 12582916
  38.6 0.7 copy-start.3
  39.3 20.9 %copy-start.1 = (bf16[4,32,128,128]{3,2,1,0:T(8,128)(2,1)S(1)}, bf16[4,32,128,128]{3,2,1,0:T(8,128)(2,1)}, u32[]{:S(2)}) copy-start(bf16[4,32,128,128]{3,2,1,0:T(8,128)(2,1)} %blk_ref.7) | copy-start | bytes 12582916
  102.2 17.5 %all-to-all-start.5 = ((bf16[16,128,128]{2,1,0:T(8,128)(2,1)}), bf16[16,128,128]{2,1,0:T(8,128)(2,1)S(1)}, u32[]{:S(2)}, u32[]{:S(2)}) async-start(bf16[16,128,128]{2,1,0:T(8,128)(2,1)} %get-tuple-element.18), calls=%async_computation.5 | async-start | bytes 1048576 | tf_op jit(solution)/shard_map/all_to_all | solution.py:169

commit v16 on v15

--- a/solution.py
+++ b/solution.py
@@ -121,7 +121,7 @@
     if first:
         cur = pltpu.with_memory_space_constraint(cur, hbm)
     args = [
-        columns // blocks.shape[0], pick, scales + 0.0, center, half_width, received, blocks, cur,
+        columns // blocks.shape[0], pick, jnp.abs(scales), center, half_width, received, blocks, cur,
     ]
     in_specs = [smem, smem, smem, smem, smem, vmem, vmem, anywhere]
     if not first:

time: 122 us -> 121 us (level)
    unnamed x12 -> x10, local copies, waits for them, and re-layouts: 2.88 us -> 2.2 us
where the time goes in v16:
time: 121 us; the launch traced here: 120 us
  blocking collectives  52.4 us (43%)
  waiting for transfers between devices  32 us (26%)
  starting transfers between devices  15.7 us (13%)
  Pallas kernels  10.4 us (9%)
  local copies, waits for them, and re-layouts  5.01 us (4%)
  other arithmetic  3.28 us (3%)
  between operations  1.38 us (1%)
    all_to_all x3, blocking collectives, exchange(): lax.all_to_all(outgoing, 'rows', split_axis=0, concat_axis=0, tiled=True)  52.4 us
    all_to_all x2, waiting for transfers between devices, exchange(): lax.all_to_all(outgoing, 'rows', split_axis=0, concat_axis=0, tiled=True)  25.7 us
    all_to_all x1, starting transfers between devices, on_device(): lax.all_to_all(asked, 'rows', split_axis=0, concat_axis=0, tiled=True)  8.32 us
    all_to_all x2, starting transfers between devices, exchange(): lax.all_to_all(outgoing, 'rows', split_axis=0, concat_axis=0, tiled=True)  7.41 us
    pallas_call x3, Pallas kernels, chebyshev_step(): pl.pallas_call(functools.partial(step_kernel, first), out_shape=(jax.Shap...  7.06 us
    all_to_all x1, waiting for transfers between devices, on_device(): lax.all_to_all(asked, 'rows', split_axis=0, concat_axis=0, tiled=True)  6.37 us
    pallas_call x1, Pallas kernels, first_chebyshev_step(): pl.pallas_call(functools.partial(first_step_kernel, first), out_shape=(ja...  3.35 us
  transfers between devices with their start and end apart: 3, of which 3 were waited for; matrix products, arithmetic and copies ran while one was open for 1% of the time, Pallas kernels for 0%

profile of v16, /device:TPU:0, one launch (start us, length us, event | category | flops | bytes accessed | tf_op | source)
XLA Modules:
  0.0 120.3 jit_solution(3897053458241388778)
XLA Ops:
  0.0 0.0 copy-start.3
  0.0 0.0 copy-start.2
  0.0 0.0 copy-start.4
  0.0 0.7 and_select_fusion.1
  0.7 0.7 add_select_fusion.1
  1.4 0.1 select_reduce_fusion.1
  1.5 0.1 select_reduce_fusion
  1.6 0.7 copy.10
  2.3 8.3 %all-to-all-start = ((s32[16,1,2]{2,1,0:T(1,128)}), s32[16,1,2]{2,1,0:T(1,128)S(1)}, u32[]{:S(2)}, u32[]{:S(2)}) async-start(s32[16,1,2]{2,1,0:T(1,128)} %copy.10), calls=%async_computation | async-start | bytes 16384 | tf_op jit(solution)/shard_map/all_to_all | solution.py:164
  10.6 0.8 fusion.1
  11.5 6.4 %all-to-all-done = s32[16,1,2]{2,1,0:T(1,128)S(1)} async-done(((s32[16,1,2]{2,1,0:T(1,128)}), s32[16,1,2]{2,1,0:T(1,128)S(1)}, u32[]{:S(2)}, u32[]{:S(2)}) %all-to-all-start) | async-done | bytes 160 | tf_op jit(solution)/shard_map/all_to_all | solution.py:164
  17.8 0.1 copy.11
  17.9 1.0 select_select_fusion
  18.9 3.6 %all-to-all-start.1 = ((bf16[16,128,128]{2,1,0:T(8,128)(2,1)}), bf16[16,128,128]{2,1,0:T(8,128)(2,1)S(1)}, u32[]{:S(2)}, u32[]{:S(2)}) async-start(bf16[16,128,128]{2,1,0:T(8,128)(2,1)} %select_select_fusion), calls=%async_computation.1 | async-start | bytes 1048576 | tf_op jit(solution)/shard_map/all_to_all | solution.py:169
  23.8 0.7 abs.3.scl_ref
  24.4 12.0 %all-to-all-done.1.recv_ref = bf16[16,128,128]{2,1,0:T(8,128)(2,1)S(1)} async-done(((bf16[16,128,128]{2,1,0:T(8,128)(2,1)}), bf16[16,128,128]{2,1,0:T(8,128)(2,1)S(1)}, u32[]{:S(2)}, u32[]{:S(2)}) %all-to-all-start.1) | async-done | bytes 524320 | tf_op jit(solution)/shard_map/all_to_all | solution.py:169
  36.4 0.0 copy-start
  36.4 2.2 %copy-done = bf16[4,32,128,128]{3,2,1,0:T(8,128)(2,1)S(1)} copy-done((bf16[4,32,128,128]{3,2,1,0:T(8,128)(2,1)S(1)}, bf16[4,32,128,128]{3,2,1,0:T(8,128)(2,1)}, u32[]{:S(2)}) %copy-start) | copy-done | bytes 4194328
  38.6 3.4 %shard_map.73 = (bf16[4,128,128]{2,1,0:T(8,128)(2,1)S(1)}, bf16[16,128,128]{2,1,0:T(8,128)(2,1)S(1)}) custom-call(s32[4,32]{1,0:T(4,128)S(1)} %get-tuple-element.23.slot_ref, s32[16]{0:T(128)S(1)} %get-tuple-element.28.pick_ref, f32[4,32]{1,0:T(4,128)S(1)} %abs.3.scl_ref, f32[1]{0:T(128)S(6)} %copy.12.c_ref, f32[1]{0:T(128)S(6)} %copy.13.w_ref, ...), custom_call_target="tpu_custom_call" | custom-call | flops 536870912 | bytes 5636096 | tf_op jit(solution)/shard_map/pallas_call | solution.py:132
  42.0 17.5 %all_to_all.37.recv_ref = bf16[16,128,128]{2,1,0:T(8,128)(2,1)S(1)} all-to-all(bf16[16,128,128]{2,1,0:T(8,128)(2,1)S(1)} %get-tuple-element.12), channel_id=1, replica_groups=mesh['rows'=16,'vecs'=2] {'rows'}, dimensions={0} | all-to-all | bytes 1048576 | tf_op jit(solution)/shard_map/all_to_all | solution.py:169
  59.5 0.0 copy-done.3
  59.5 0.0 copy-done.2
  59.5 0.0 copy-done.4
  59.5 0.0 copy-done.1
  59.6 2.1 %shard_map.74 = (bf16[4,128,128]{2,1,0:T(8,128)(2,1)S(1)}, bf16[16,128,128]{2,1,0:T(8,128)(2,1)S(1)}) custom-call(s32[4,32]{1,0:T(4,128)S(1)} %copy-done.3, s32[16]{0:T(128)S(1)} %get-tuple-element.28.pick_ref, f32[4,32]{1,0:T(4,128)S(1)} %copy-done.4, f32[1]{0:T(128)S(6)} %copy.12.c_ref, f32[1]{0:T(128)S(6)} %copy.13.w_ref, ...), custom_call_target="tpu_custom_call" | custom-call | flops 536870912 | bytes 5636096 | tf_op jit(solution)/shard_map/pallas_call | solution.py:99
  61.6 17.5 %all_to_all.38.recv_ref = bf16[16,128,128]{2,1,0:T(8,128)(2,1)S(1)} all-to-all(bf16[16,128,128]{2,1,0:T(8,128)(2,1)S(1)} %get-tuple-element.14), channel_id=1, replica_groups=mesh['rows'=16,'vecs'=2] {'rows'}, dimensions={0} | all-to-all | bytes 1048576 | tf_op jit(solution)/shard_map/all_to_all | solution.py:169
  79.1 2.1 %shard_map.75 = (bf16[4,128,128]{2,1,0:T(8,128)(2,1)S(1)}, bf16[16,128,128]{2,1,0:T(8,128)(2,1)S(1)}) custom-call(s32[4,32]{1,0:T(4,128)S(1)} %copy-done.3, s32[16]{0:T(128)S(1)} %get-tuple-element.28.pick_ref, f32[4,32]{1,0:T(4,128)S(1)} %copy-done.4, f32[1]{0:T(128)S(6)} %copy.12.c_ref, f32[1]{0:T(128)S(6)} %copy.13.w_ref, ...), custom_call_target="tpu_custom_call" | custom-call | flops 536870912 | bytes 5636096 | tf_op jit(solution)/shard_map/pallas_call | solution.py:99
  81.2 17.4 %all_to_all.39.recv_ref = bf16[16,128,128]{2,1,0:T(8,128)(2,1)S(1)} all-to-all(bf16[16,128,128]{2,1,0:T(8,128)(2,1)S(1)} %get-tuple-element.16), channel_id=1, replica_groups=mesh['rows'=16,'vecs'=2] {'rows'}, dimensions={0} | all-to-all | bytes 1048576 | tf_op jit(solution)/shard_map/all_to_all | solution.py:169
  98.6 2.9 %shard_map.76 = (bf16[4,128,128]{2,1,0:T(8,128)(2,1)}, bf16[16,128,128]{2,1,0:T(8,128)(2,1)}) custom-call(s32[4,32]{1,0:T(4,128)S(1)} %copy-done.3, s32[16]{0:T(128)S(1)} %get-tuple-element.29.pick_ref, f32[4,32]{1,0:T(4,128)S(1)} %copy-done.4, f32[1]{0:T(128)S(6)} %copy.12.c_ref, f32[1]{0:T(128)S(6)} %copy.13.w_ref, ...), custom_call_target="tpu_custom_call" | custom-call | flops 536870912 | bytes 5636096 | tf_op jit(solution)/shard_map/pallas_call | solution.py:99
  101.5 3.8 %all-to-all-start.5 = ((bf16[16,128,128]{2,1,0:T(8,128)(2,1)}), bf16[16,128,128]{2,1,0:T(8,128)(2,1)S(1)}, u32[]{:S(2)}, u32[]{:S(2)}) async-start(bf16[16,128,128]{2,1,0:T(8,128)(2,1)} %get-tuple-element.18), calls=%async_computation.5 | async-start | bytes 1048576 | tf_op jit(solution)/shard_map/all_to_all | solution.py:169
  105.4 13.7 %all-to-all-done.5 = bf16[16,128,128]{2,1,0:T(8,128)(2,1)S(1)} async-done(((bf16[16,128,128]{2,1,0:T(8,128)(2,1)}), bf16[16,128,128]{2,1,0:T(8,128)(2,1)S(1)}, u32[]{:S(2)}, u32[]{:S(2)}) %all-to-all-start.5) | async-done | bytes 524320 | tf_op jit(solution)/shard_map/all_to_all | solution.py:169
  119.1 1.2 %gather_fusion = bf16[4,128,128]{2,1,0:T(8,128)(2,1)} fusion(bf16[16,128,128]{2,1,0:T(8,128)(2,1)S(1)} %all-to-all-done.5, s32[1024]{0:T(1024)S(1)} %pad_clamp_fusion), kind=kCustom, calls=%fused_computation | custom fusion | bytes 262160 | tf_op jit(solution)/shard_map/jit(_take)/gather | solution.py:184
  (5 shorter events, 0.0 us)
Async XLA Ops:
  0.0 59.5 %copy-start.3 = (s32[4,32]{1,0:T(4,128)S(1)}, s32[4,32]{1,0:T(4,128)}, u32[]{:S(2)}) copy-start(s32[4,32]{1,0:T(4,128)} %cols_ref.5) | copy-start | bytes 1540
  0.0 59.5 %copy-start.2 = (bf16[512,128]{1,0:T(8,128)(2,1)S(1)}, bf16[512,128]{1,0:T(8,128)(2,1)}, u32[]{:S(2)}) copy-start(bf16[512,128]{1,0:T(8,128)(2,1)} %param.7) | copy-start | bytes 393220
  0.0 59.5 %copy-start.4 = (f32[4,32]{1,0:T(4,128)S(1)}, f32[4,32]{1,0:T(4,128)}, u32[]{:S(2)}) copy-start(f32[4,32]{1,0:T(4,128)} %scl_ref.5) | copy-start | bytes 1540
  2.3 15.5 %all-to-all-start = ((s32[16,1,2]{2,1,0:T(1,128)}), s32[16,1,2]{2,1,0:T(1,128)S(1)}, u32[]{:S(2)}, u32[]{:S(2)}) async-start(s32[16,1,2]{2,1,0:T(1,128)} %copy.10), calls=%async_computation | async-start | bytes 16384 | tf_op jit(solution)/shard_map/all_to_all | solution.py:164
  18.9 17.6 %all-to-all-start.1 = ((bf16[16,128,128]{2,1,0:T(8,128)(2,1)}), bf16[16,128,128]{2,1,0:T(8,128)(2,1)S(1)}, u32[]{:S(2)}, u32[]{:S(2)}) async-start(bf16[16,128,128]{2,1,0:T(8,128)(2,1)} %select_select_fusion), calls=%async_computation.1 | async-start | bytes 1048576 | tf_op jit(solution)/shard_map/all_to_all | solution.py:169
  36.4 2.2 %copy-start = (bf16[4,32,128,128]{3,2,1,0:T(8,128)(2,1)S(1)}, bf16[4,32,128,128]{3,2,1,0:T(8,128)(2,1)}, u32[]{:S(2)}) copy-start(bf16[4,32,128,128]{3,2,1,0:T(8,128)(2,1)} %blk_ref.7) | copy-start | bytes 12582916
  38.6 20.9 %copy-start.1 = (bf16[4,32,128,128]{3,2,1,0:T(8,128)(2,1)S(1)}, bf16[4,32,128,128]{3,2,1,0:T(8,128)(2,1)}, u32[]{:S(2)}) copy-start(bf16[4,32,128,128]{3,2,1,0:T(8,128)(2,1)} %blk_ref.7) | copy-start | bytes 12582916
  101.5 17.5 %all-to-all-start.5 = ((bf16[16,128,128]{2,1,0:T(8,128)(2,1)}), bf16[16,128,128]{2,1,0:T(8,128)(2,1)S(1)}, u32[]{:S(2)}, u32[]{:S(2)}) async-start(bf16[16,128,128]{2,1,0:T(8,128)(2,1)} %get-tuple-element.18), calls=%async_computation.5 | async-start | bytes 1048576 | tf_op jit(solution)/shard_map/all_to_all | solution.py:169
